TPU v7x, 256 devices: a whole 4x4x8 slice. The times are simulated.
256 devices in a mesh: tok: 64 (over z, y, core), pool: 4 (over x).
Axes of the slice: x: 4, y: 4, z: 8, core: 2. Of those that a mesh axis runs over, the one named last changes fastest.
Arguments:
- stream: bfloat16 [16384, 1024], P(('tok', 'pool')), may hold values from -6 to 6
- queries: bfloat16 [16384, 1024], P(('tok', 'pool')), may hold values from -2000 to 2000
- fresh_kv: bfloat16 [16384, 1024], P(('tok', 'pool')), may hold values from -16 to 16
- cache_block_pool: bfloat16 [2048, 64, 1024], P(('tok', 'pool')), may hold values from -9 to 9
- block_table: int32 [64, 16], P('tok'), may hold values from 0 to 31, as said below
- cached_len: int32 [64, 3], P('tok'), may hold values from 1 to 1024, as said below
- request_ids: int32 [64, 256], P('tok'), may hold values from 0 to 2, never falling along the last dimension, each value on 1 to 128 neighbouring positions
- output_weight: bfloat16 [1024, 1024], replicated, may hold values from -0.1875 to 0.1875
- norm_gain: float32 [1024], replicated, may hold values from 0.5 to 1.5
- expert_gate_up: bfloat16 [64, 1024, 512], P('tok'), may hold values from -0.1875 to 0.1875
- expert_down: bfloat16 [64, 256, 1024], P('tok'), may hold values from -0.25 to 0.25
- routes: int32 [16384, 8], P(('tok', 'pool')), may hold values from 0 to 31, all different within a row; in each aligned block of 64 rows (0 to 63, 64 to 127, ...) at most 32 rows name the same one
- route_weight: float32 [16384, 8], P(('tok', 'pool')), may hold values from 0.05 to 0.4
Outputs:
- attended: bfloat16 [16384, 1024], P(('tok', 'pool'))
- layer_out: bfloat16 [16384, 1024], P(('tok', 'pool'))
Inputs may be any that keep to these rules, and one draw needn't show every extreme that they name: `block_table`: a group's 16 entries are distinct slots of its pool, slot s lying on pool device s // 8 of the group; in every group some pool device has all its 8 slots listed. `cached_len`: in every group some request sees all 1024 cached tokens. `request_ids`: never falling along a group's tokens; each request has 1 to 128 tokens, some request exactly 128. `routes`: each token names 8 different experts; among the 64 rows of one device no expert is named more than 32 times, a bound that some block reaches.
All inputs are finite; a program needn't handle non-finite values.
Results may differ from a plain program's by a relative error of at most 0.017.
Values may be sent and summed in bfloat16 or wider, within the bound.
No kernel may reach another device: no remote copies, remote signals or barrier semaphores. Data moves between devices by JAX's collectives and lax.ppermute only.
A program may use at most 64 MiB of HBM per device.

v0:
```python
import jax
import jax.numpy as jnp
from jax import lax
from jax.sharding import PartitionSpec as P

QUERY_HEADS = 16
KEY_VALUE_HEADS = 8
HEAD_SIZE = 64
EXPERTS = 32
FF = 512
TOPK = 8
CAP = 32


score_scale = 0.015625
masked_filler = -1e30


def block_group():
    for candidate in (8, 4, 2, 1):
        return candidate
    return 1


def masked_scores(query_row_block, key_value_pairs, visible):
    kv_heads = query_row_block.shape[1]
    head_dim = query_row_block.shape[3]
    key_count = key_value_pairs.shape[0]
    middle = key_value_pairs.shape[1] // 2
    key_row_block = key_value_pairs[:, :middle].reshape(key_count, kv_heads, head_dim)
    value_row_block = key_value_pairs[:, middle:].reshape(key_count, kv_heads, head_dim)
    scores = (
        jnp.einsum(
            "qhgd,khd->qhgk", query_row_block, key_row_block, preferred_element_type=jnp.float32
        )
        * score_scale
    )
    scores = jnp.where(visible[:, None, None, :], scores, masked_filler)
    return (scores, value_row_block)


def attend_update(partial_value, query_row_block, key_value_pairs, visible):
    running, denominator, summed = partial_value
    scores, value_row_block = masked_scores(query_row_block, key_value_pairs, visible)
    shown_keys = visible[:, None, None, :]
    highest = jnp.maximum(running, jnp.max(scores, axis=-1))
    rescale = jnp.exp(running - highest)
    weights = jnp.where(shown_keys, jnp.exp(scores - highest[..., None]), 0.0)
    denominator = denominator * rescale + jnp.sum(weights, axis=-1)
    product = jnp.einsum(
        "qhgk,khd->qhgd",
        weights.astype(jnp.bfloat16),
        value_row_block,
        preferred_element_type=jnp.float32,
    )
    summed = summed * rescale[..., None] + product
    return (highest, denominator, summed)


def scan_blocks(step_fn, carried, blocks, logical, limit_len):
    number = blocks.shape[0]
    block_len = blocks.shape[1]
    per_step = block_group()
    offsets = jnp.arange(block_len, dtype=jnp.int32)

    def visit(state, pieces):
        group_blocks, group_logical = pieces
        positions = (group_logical[:, None] * block_len + offsets[None, :]).reshape(-1)
        listed = jnp.repeat(group_logical >= 0, block_len)
        visible = listed[None, :] & (positions[None, :] < limit_len[:, None])
        return (step_fn(state, group_blocks.reshape(per_step * block_len, -1), visible), None)

    carried, leftover = lax.scan(
        visit,
        carried,
        (
            blocks.reshape(number // per_step, per_step, block_len, -1),
            logical.reshape(number // per_step, per_step),
        ),
    )
    return carried


def unit_ffn(rows_in, gate_up_weight, down_weight):
    per_device = gate_up_weight.shape[0]
    width = rows_in.shape[2]
    slots_here = rows_in.shape[1]
    sources = rows_in.shape[0] // per_device
    shaped = rows_in.reshape(sources, per_device, slots_here, width)
    gate_up = jnp.einsum(
        "sucd,udf->sucf", shaped, gate_up_weight, preferred_element_type=jnp.float32
    )
    hidden_units = gate_up_weight.shape[2] // 2
    inner = (jax.nn.silu(gate_up[..., :hidden_units]) * gate_up[..., hidden_units:]).astype(
        jnp.bfloat16
    )
    produced = jnp.einsum(
        "sucf,ufd->sucd", inner, down_weight, preferred_element_type=jnp.float32
    ).astype(jnp.bfloat16)
    return produced.reshape(sources * per_device, slots_here, width)


def direct_dispatch(send_rows, split, expert_gate_up, expert_down):
    width = send_rows.shape[1]
    unit_rows = jnp.repeat(send_rows.reshape(EXPERTS, CAP, width), split, axis=0)
    produced = unit_ffn(
        lax.all_to_all(unit_rows, "tok", split_axis=0, concat_axis=0, tiled=True),
        expert_gate_up,
        expert_down,
    )
    returned = lax.all_to_all(produced, "tok", split_axis=0, concat_axis=0, tiled=True)
    summed = jnp.sum(returned.reshape(EXPERTS, split, CAP, width).astype(jnp.float32), axis=1)
    return summed.astype(jnp.bfloat16).reshape(EXPERTS * CAP, width)


def body(
    stream,
    queries,
    fresh_kv,
    cache_block_pool,
    block_table,
    cached_len,
    request_ids,
    output_weight,
    norm_gain,
    expert_gate_up,
    expert_down,
    routes,
    route_weight,
):
    tokens_per_device = stream.shape[0]
    width = stream.shape[1]
    heads_per_group = QUERY_HEADS // KEY_VALUE_HEADS
    pool_size = lax.axis_size("pool")
    pool_idx = lax.axis_index("pool")
    segments = request_ids[0]
    lengths = cached_len[0]
    table = block_table[0]
    list_len = table.shape[0]
    pool_blocks = cache_block_pool.shape[0]
    slots_all = pool_size * pool_blocks
    row_start = pool_idx * tokens_per_device
    query_index = row_start + jnp.arange(tokens_per_device, dtype=jnp.int32)
    query_seg = lax.dynamic_slice_in_dim(segments, row_start, tokens_per_device)
    request_range = jnp.arange(lengths.shape[0], dtype=jnp.int32)
    row_len = jnp.sum(
        jnp.where(segments[:, None] == request_range[None, :], lengths[None, :], 0), axis=1
    )
    query_len = lax.dynamic_slice_in_dim(row_len, row_start, tokens_per_device)
    slot_block = (
        jnp.sum(
            jnp.where(
                table[None, :] == jnp.arange(slots_all, dtype=jnp.int32)[:, None],
                jnp.arange(list_len, dtype=jnp.int32)[None, :] + 1,
                0,
            ),
            axis=1,
        )
        - 1
    )
    query_row_block = queries.reshape(
        tokens_per_device, KEY_VALUE_HEADS, heads_per_group, HEAD_SIZE
    )
    start_state = (
        jnp.full((tokens_per_device, KEY_VALUE_HEADS, heads_per_group), masked_filler, jnp.float32),
        jnp.zeros((tokens_per_device, KEY_VALUE_HEADS, heads_per_group), jnp.float32),
        jnp.zeros((tokens_per_device, KEY_VALUE_HEADS, heads_per_group, HEAD_SIZE), jnp.float32),
    )
    piece = lax.all_gather(fresh_kv, "pool", axis=0, tiled=True)
    key_count = piece.shape[0]
    key_index = jnp.arange(key_count, dtype=jnp.int32)
    visible = (segments[None, :] == query_seg[:, None]) & (
        key_index[None, :] <= query_index[:, None]
    )
    fresh_state = attend_update(start_state, query_row_block, piece, visible)

    def fetch_step(partial_value, piece):

        def update_step(state, key_value_pairs, visible):
            return attend_update(state, query_row_block, key_value_pairs, visible)

        return scan_blocks(update_step, partial_value, piece, slot_block, query_len)

    running, denominator, summed = fetch_step(
        fresh_state, lax.all_gather(cache_block_pool, "pool", axis=0, tiled=True)
    )
    context = summed / denominator[..., None]
    attended = context.reshape(tokens_per_device, QUERY_HEADS * HEAD_SIZE).astype(jnp.bfloat16)
    residual = stream.astype(jnp.float32) + jnp.dot(
        attended, output_weight, preferred_element_type=jnp.float32
    )
    meansq = jnp.mean(residual * residual, axis=-1, keepdims=True)
    normed = (residual * lax.rsqrt(meansq + 1e-06) * norm_gain).astype(jnp.bfloat16)
    flat_routes = routes.reshape(-1)
    onehot = (flat_routes[:, None] == jnp.arange(EXPERTS, dtype=jnp.int32)[None, :]).astype(
        jnp.int32
    )
    earlier = jnp.cumsum(onehot, axis=0) - onehot
    slot_of = jnp.sum(earlier * onehot, axis=1)
    destination = flat_routes * CAP + slot_of
    send_rows = (
        jnp.zeros((EXPERTS * CAP, width), jnp.bfloat16)
        .at[destination]
        .set(jnp.repeat(normed, TOPK, axis=0))
    )
    split = FF // (expert_gate_up.shape[2] // 2)
    expert_rows = direct_dispatch(send_rows, split, expert_gate_up, expert_down)
    picked = expert_rows[destination].reshape(tokens_per_device, TOPK, width)
    experts_sum = jnp.einsum("tkd,tk->td", picked.astype(jnp.float32), route_weight)
    layer_out = (residual + experts_sum).astype(jnp.bfloat16)
    return (attended, layer_out)


def solution(mesh):
    placed = (
        P(("tok", "pool"), None),
        P(("tok", "pool"), None),
        P(("tok", "pool"), None),
        P(("tok", "pool"), None, None),
        P("tok", None),
        P("tok", None),
        P("tok", None),
        P(),
        P(),
        P("tok", None, None),
        P("tok", None, None),
        P(("tok", "pool"), None),
        P(("tok", "pool"), None),
    )
    return jax.shard_map(
        body,
        mesh=mesh,
        in_specs=placed,
        out_specs=(P(("tok", "pool"), None), P(("tok", "pool"), None)),
        check_vma=False,
    )
```

profile of v0, /device:TPU:8, one launch (start us, length us, event | category | flops | bytes accessed | tf_op | source)
XLA Modules:
  0.0 344.3 jit_solution(4494204630573688395)
XLA Ops:
  8.9 13.3 %all_gather.6 = bf16[256,1024]{1,0:T(8,128)(2,1)S(1)} all-gather(bf16[64,1024]{1,0:T(8,128)(2,1)} %param.17), channel_id=1, replica_groups=mesh['tok'=64,'pool'=4] {'pool'}, dimensions={0}, use_global_device_ids=true | all-gather | bytes 655360 | tf_op jit(solution)/shard_map/all_gather | solution.py:169
  24.6 1.0 copy.48
  26.1 1.2 reduce-window.6
  27.7 35.8 %all-gather.2.cloned.1.call-done = bf16[32,64,1024]{2,1,0:T(8,128)(2,1)} async-done(((bf16[8,64,1024]{2,1,0:T(8,128)(2,1)}), bf16[32,64,1024]{2,1,0:T(8,128)(2,1)}) %all-gather.2.cloned.1.call-update) | async-done | bytes 4194320 | tf_op jit(solution)/shard_map/all_gather | solution.py:185
  63.4 39.7 %while.15 = (s32[]{:T(128)}, f32[64,8,2]{0,2,1:T(2,128)S(1)}, f32[64,8,2]{0,2,1:T(2,128)S(1)}, f32[64,8,2,64]{0,3,2,1:T(8,128)}, s32[4,8]{1,0:T(4,128)S(1)}, /*i...) while((s32[]{:T(128)}, f32[64,8,2]{0,2,1:T(2,128)S(1)}, ...), condition=%wide.region_7.8_spmd.clone, body=%wide.region_4.7_spmd.clone.sunk | while | flops 141232656 | bytes 22882844 | solution.py:73
  63.9 1.3 constant_dynamic-slice_fusion.3
  66.3 1.5 fusion.69
  67.9 1.3 copy-done.1
  70.1 3.2 fusion.71
  73.8 1.3 constant_dynamic-slice_fusion.3
  76.2 1.5 fusion.69
  77.8 1.3 copy-done.1
  80.0 3.2 fusion.71
  83.7 1.3 constant_dynamic-slice_fusion.3
  86.2 1.5 fusion.69
  87.7 1.3 copy-done.1
  90.0 3.2 fusion.71
  93.6 1.3 constant_dynamic-slice_fusion.3
  96.1 1.5 fusion.69
  97.6 1.3 copy-done.1
  99.9 3.2 fusion.71
  103.1 1.1 divide_convert_fusion
  104.3 1.5 multiply_reduce_fusion
  105.9 4.2 %scatter_custom_fusion = bf16[1024,1024]{1,0:T(8,128)(2,1)} fusion(s32[512]{0:T(512)S(1)} %bitcast.177, bf16[]{:T(256)} %constant.42.clone.1, bf16[64,1024]{1,0:T(8,128)(2,1)S(1)} %multiply_convert_fusion), kind=kCustom, calls=%fused_computation.40 | custom fusion | bytes 2228226 | tf_op jit(solution)/shard_map/scatter | solution.py:204
  110.1 2.1 broadcast_in_dim.116
  112.2 106.7 %all_to_all.10 = bf16[64,32,1024]{2,1,0:T(8,128)(2,1)S(1)} all-to-all(bf16[64,32,1024]{2,1,0:T(8,128)(2,1)S(1)} %bitcast.163), channel_id=1, replica_groups=mesh['tok'=64,'pool'=4] {'tok'}, dimensions={0} | all-to-all | bytes 8388608 | tf_op jit(solution)/shard_map/all_to_all | solution.py:107
  218.9 2.3 convolution_bitcast_fusion.1
  221.2 3.3 convolution_convert_fusion
  224.5 5.8 %all-to-all-start.1 = ((bf16[64,32,1024]{2,1,0:T(8,128)(2,1)}), bf16[64,32,1024]{2,1,0:T(8,128)(2,1)}, u32[]{:S(2)}, u32[]{:S(2)}) async-start(bf16[64,32,1024]{2,1,0:T(8,128)(2,1)} %convolution_convert_fusion), calls=%async_computation.1 | async-start | bytes 8388608 | tf_op jit(solution)/shard_map/all_to_all | solution.py:111
  231.2 95.2 %all-to-all-done.1 = bf16[64,32,1024]{2,1,0:T(8,128)(2,1)} async-done(((bf16[64,32,1024]{2,1,0:T(8,128)(2,1)}), bf16[64,32,1024]{2,1,0:T(8,128)(2,1)}, u32[]{:S(2)}, u32[]{:S(2)}) %all-to-all-start.1) | async-done | bytes 4194336 | tf_op jit(solution)/shard_map/all_to_all | solution.py:111
  326.4 5.3 %bitcast_reduce_fusion = bf16[32,32,1024]{2,1,0:T(8,128)(2,1)} fusion(bf16[64,32,1024]{2,1,0:T(8,128)(2,1)} %all-to-all-done.1), kind=kLoop, calls=%fused_computation.25 | loop fusion | flops 1048576 | bytes 6291456 | tf_op jit(solution)/shard_map/reduce_sum | solution.py:112
  331.7 4.6 %gather_fusion = bf16[512,1024]{1,0:T(8,128)(2,1)S(1)} fusion(bf16[1024,1024]{1,0:T(8,128)(2,1)} %bitcast.161, s32[1024]{0:T(1024)S(1)} %pad_clamp_fusion), kind=kCustom, calls=%fused_computation | custom fusion | bytes 2099200 | tf_op jit(solution)/shard_map/gather | solution.py:208
  (120 shorter events, 16.6 us)
Async XLA Ops:
  7.2 97.1 %copy-start = (bf16[1024,1024]{1,0:T(8,128)(2,1)S(1)}, bf16[1024,1024]{1,0:T(8,128)(2,1)}, u32[]{:S(2)}) copy-start(bf16[1024,1024]{1,0:T(8,128)(2,1)} %param.22) | copy-start | bytes 6291460
  7.2 15.2 %copy-start.2 = (bf16[64,1024]{1,0:T(8,128)(2,1)S(1)}, bf16[64,1024]{1,0:T(8,128)(2,1)}, u32[]{:S(2)}) copy-start(bf16[64,1024]{1,0:T(8,128)(2,1)} %param.16) | copy-start | bytes 393220
  7.2 56.3 %all-gather.2.cloned.1.call-start = ((), (), s32[]{:S(2)}) async-start(), calls=%async_computation.2 | async-start | bytes 5242880 | tf_op jit(solution)/shard_map/all_gather | solution.py:185
  7.9 14.9 %copy-start.6 = (s32[1,256]{1,0:T(1,128)S(1)}, s32[1,256]{1,0:T(1,128)}, u32[]{:S(2)}) copy-start(s32[1,256]{1,0:T(1,128)} %param.21) | copy-start | bytes 3076
  23.4 2.2 copy-start.10
  23.4 2.3 copy-start.7
  23.4 2.5 copy-start.3
  67.9 1.3 copy-start.1
  77.8 1.3 copy-start.1
  87.7 1.3 copy-start.1
  97.6 1.3 copy-start.1
  103.1 2.7 copy-start.4
  112.2 106.7 %copy-start.8 = (bf16[1,1024,512]{2,1,0:T(8,128)(2,1)S(1)}, bf16[1,1024,512]{2,1,0:T(8,128)(2,1)}, u32[]{:S(2)}) copy-start(bf16[1,1024,512]{2,1,0:T(8,128)(2,1)} %param.24) | copy-start | bytes 3145732
  218.9 2.4 copy-start.9
  224.5 5.8 %copy-start.5 = (f32[64,8]{0,1:T(8,128)S(1)}, f32[64,8]{0,1:T(8,128)}, u32[]{:S(2)}) copy-start(f32[64,8]{0,1:T(8,128)} %param.27) | copy-start | bytes 6148
  224.5 101.9 %all-to-all-start.1 = ((bf16[64,32,1024]{2,1,0:T(8,128)(2,1)}), bf16[64,32,1024]{2,1,0:T(8,128)(2,1)}, u32[]{:S(2)}, u32[]{:S(2)}) async-start(bf16[64,32,1024]{2,1,0:T(8,128)(2,1)} %convolution_convert_fusion), calls=%async_computation.1 | async-start | bytes 8388608 | tf_op jit(solution)/shard_map/all_to_all | solution.py:111
Sparse Core Ops, SparseCore 0:
  9.8 53.5 all-gather.1
where the time goes:
time: 345 us; the launch traced here: 344 us
  waiting for transfers between devices  132 us (38%)
  blocking collectives  120 us (35%)
  local copies, waits for them, and re-layouts  31.7 us (9%)
  matrix products  27.7 us (8%)
  between operations  14.3 us (4%)
  other arithmetic  12.8 us (4%)
  starting transfers between devices  5.79 us (2%)
    all_to_all x1, blocking collectives, direct_dispatch(): lax.all_to_all(unit_rows, 'tok', split_axis=0, concat_axis=0, tiled=True)  107 us
    all_to_all x1, waiting for transfers between devices, direct_dispatch(): lax.all_to_all(produced, 'tok', split_axis=0, concat_axis=0, tiled=True)  95.2 us
    all_gather x1, waiting for transfers between devices, body(): lax.all_gather(cache_block_pool, 'pool', axis=0, tiled=True)  35.8 us
    dot_general x5, matrix products, attend_update(): jnp.einsum('qhgk,khd->qhgd', weights.astype(jnp.bfloat16), value_row_bloc...  13.6 us
    all_gather x1, blocking collectives, body(): piece = lax.all_gather(fresh_kv, 'pool', axis=0, tiled=True)  13.3 us
  transfers between devices with their start and end apart: 2, of which 2 were waited for; matrix products, arithmetic and copies ran while one was open for 2% of the time, Pallas kernels for 0%

commit v1 on v0

--- a/solution.py
+++ b/solution.py
@@ -70,7 +70,7 @@
         visible = listed[None, :] & (positions[None, :] < limit_len[:, None])
         return (step_fn(state, group_blocks.reshape(per_step * block_len, -1), visible), None)
 
-    carried, leftover = lax.scan(
+    carried, _ = lax.scan(
         visit,
         carried,
         (
@@ -81,36 +81,35 @@
     return carried
 
 
-def unit_ffn(rows_in, gate_up_weight, down_weight):
-    per_device = gate_up_weight.shape[0]
-    width = rows_in.shape[2]
-    slots_here = rows_in.shape[1]
-    sources = rows_in.shape[0] // per_device
-    shaped = rows_in.reshape(sources, per_device, slots_here, width)
-    gate_up = jnp.einsum(
-        "sucd,udf->sucf", shaped, gate_up_weight, preferred_element_type=jnp.float32
-    )
-    hidden_units = gate_up_weight.shape[2] // 2
-    inner = (jax.nn.silu(gate_up[..., :hidden_units]) * gate_up[..., hidden_units:]).astype(
-        jnp.bfloat16
-    )
-    produced = jnp.einsum(
-        "sucf,ufd->sucd", inner, down_weight, preferred_element_type=jnp.float32
-    ).astype(jnp.bfloat16)
-    return produced.reshape(sources * per_device, slots_here, width)
+def pair_ffn(rows_in, gate_up_pair, down_pair):
+    hidden_units = gate_up_pair.shape[2] // 2
+    total = None
+    for part in range(gate_up_pair.shape[0]):
+        gate_up = jnp.dot(rows_in, gate_up_pair[part], preferred_element_type=jnp.float32)
+        inner = (jax.nn.silu(gate_up[:, :hidden_units]) * gate_up[:, hidden_units:]).astype(
+            jnp.bfloat16
+        )
+        produced = jnp.dot(inner, down_pair[part], preferred_element_type=jnp.float32).astype(
+            jnp.bfloat16
+        ).astype(jnp.float32)
+        total = produced if total is None else total + produced
+    return total.astype(jnp.bfloat16)
 
 
 def direct_dispatch(send_rows, split, expert_gate_up, expert_down):
     width = send_rows.shape[1]
-    unit_rows = jnp.repeat(send_rows.reshape(EXPERTS, CAP, width), split, axis=0)
-    produced = unit_ffn(
-        lax.all_to_all(unit_rows, "tok", split_axis=0, concat_axis=0, tiled=True),
-        expert_gate_up,
-        expert_down,
-    )
-    returned = lax.all_to_all(produced, "tok", split_axis=0, concat_axis=0, tiled=True)
-    summed = jnp.sum(returned.reshape(EXPERTS, split, CAP, width).astype(jnp.float32), axis=1)
-    return summed.astype(jnp.bfloat16).reshape(EXPERTS * CAP, width)
+    gate_up_pair, down_pair = expert_gate_up, expert_down
+    unit_rows = send_rows.reshape(EXPERTS * split, CAP // split, width)
+    arrived = lax.all_to_all(unit_rows, "tok", split_axis=0, concat_axis=0, tiled=True)
+    produced = pair_ffn(arrived.reshape(-1, width), gate_up_pair, down_pair)
+    returned = lax.all_to_all(
+        produced.reshape(EXPERTS * split, CAP // split, width),
+        "tok",
+        split_axis=0,
+        concat_axis=0,
+        tiled=True,
+    )
+    return returned.reshape(EXPERTS * CAP, width)
 
 
 def body(
@@ -130,6 +129,10 @@
 ):
     tokens_per_device = stream.shape[0]
     width = stream.shape[1]
+    tok_size = lax.axis_size("tok")
+    sibling = [(t, t ^ 1) for t in range(tok_size)]
+    sibling_gate_up = lax.ppermute(expert_gate_up, "tok", sibling)
+    sibling_down = lax.ppermute(expert_down, "tok", sibling)
     heads_per_group = QUERY_HEADS // KEY_VALUE_HEADS
     pool_size = lax.axis_size("pool")
     pool_idx = lax.axis_index("pool")
@@ -181,9 +184,8 @@
 
         return scan_blocks(update_step, partial_value, piece, slot_block, query_len)
 
-    running, denominator, summed = fetch_step(
-        fresh_state, lax.all_gather(cache_block_pool, "pool", axis=0, tiled=True)
-    )
+    gathered_pool = lax.all_gather(cache_block_pool, "pool", axis=0, tiled=True)
+    _, denominator, summed = fetch_step(fresh_state, gathered_pool)
     context = summed / denominator[..., None]
     attended = context.reshape(tokens_per_device, QUERY_HEADS * HEAD_SIZE).astype(jnp.bfloat16)
     residual = stream.astype(jnp.float32) + jnp.dot(
@@ -204,7 +206,12 @@
         .set(jnp.repeat(normed, TOPK, axis=0))
     )
     split = FF // (expert_gate_up.shape[2] // 2)
-    expert_rows = direct_dispatch(send_rows, split, expert_gate_up, expert_down)
+    expert_rows = direct_dispatch(
+        send_rows,
+        split,
+        jnp.concatenate([expert_gate_up, sibling_gate_up], axis=0),
+        jnp.concatenate([expert_down, sibling_down], axis=0),
+    )
     picked = expert_rows[destination].reshape(tokens_per_device, TOPK, width)
     experts_sum = jnp.einsum("tkd,tk->td", picked.astype(jnp.float32), route_weight)
     layer_out = (residual + experts_sum).astype(jnp.bfloat16)

time: 345 us -> 253 us (0.73)
  blocking collectives: 120 us -> 13.3 us
  starting transfers between devices: 5.79 us -> 17.3 us
  other arithmetic: 12.8 us -> 7.52 us
  waiting for transfers between devices: 132 us -> 137 us
  matrix products: 27.7 us -> 32.3 us
    all_to_all x1 -> x0, blocking collectives: 107 us -> none  [direct_dispatch(): lax.all_to_all(unit_rows, 'tok', split_axis=0, concat_axis=0, tiled=True)]
    all_to_all x1 -> x2, starting transfers between devices: 5.75 us -> 16.6 us  [the longest x1 10.9 us: direct_dispatch(): lax.all_to_all(unit_rows, 'tok', split_axis=0, concat_axis=0, tiled=True)]
    all_to_all x1 -> x2, waiting for transfers between devices: 95.2 us -> 101 us  [the longest x1 50.6 us: direct_dispatch(): lax.all_to_all(unit_rows, 'tok', split_axis=0, concat_axis=0, tiled=True)]
    reduce_sum x1 -> x0, other arithmetic: 5.27 us -> none  [direct_dispatch(): jnp.sum(returned.reshape(EXPERTS, split, CAP, width).astype(jnp.float32),...]
    dot_general x2 -> x4, matrix products: 5.63 us -> 10.2 us  [the longest x2 6.19 us: pair_ffn(): jnp.dot(rows_in, gate_up_pair[part], preferred_element_type=jnp.float32)]
  transfers between devices with their start and end apart: 2 -> 5, of which waited for: 2 -> 3; matrix products, arithmetic and copies ran while one was open for 2% -> 6% of each run, Pallas kernels for 0% -> 0%
where the time goes in v1:
time: 253 us; the launch traced here: 252 us
  waiting for transfers between devices  137 us (54%)
  matrix products  32.3 us (13%)
  local copies, waits for them, and re-layouts  29.5 us (12%)
  starting transfers between devices  17.3 us (7%)
  between operations  14.3 us (6%)
  blocking collectives  13.3 us (5%)
  other arithmetic  7.52 us (3%)
    all_to_all x1, waiting for transfers between devices, direct_dispatch(): lax.all_to_all(unit_rows, 'tok', split_axis=0, concat_axis=0, tiled=True)  50.6 us
    all_to_all x1, waiting for transfers between devices, direct_dispatch(): lax.all_to_all(produced.reshape(EXPERTS * split, CAP // split, width), 't...  50.2 us
    all_gather x1, waiting for transfers between devices, body(): gathered_pool = lax.all_gather(cache_block_pool, 'pool', axis=0, tiled=True)  35.8 us
    dot_general x5, matrix products, attend_update(): jnp.einsum('qhgk,khd->qhgd', weights.astype(jnp.bfloat16), value_row_bloc...  13.6 us
    all_gather x1, blocking collectives, body(): piece = lax.all_gather(fresh_kv, 'pool', axis=0, tiled=True)  13.3 us
    all_to_all x1, starting transfers between devices, direct_dispatch(): lax.all_to_all(unit_rows, 'tok', split_axis=0, concat_axis=0, tiled=True)  10.9 us
    dot_general x5, matrix products, masked_scores(): jnp.einsum('qhgd,khd->qhgk', query_row_block, key_row_block, preferred_el...  6.54 us
    dot_general x2, matrix products, pair_ffn(): jnp.dot(rows_in, gate_up_pair[part], preferred_element_type=jnp.float32)  6.19 us
  transfers between devices with their start and end apart: 5, of which 3 were waited for; matrix products, arithmetic and copies ran while one was open for 6% of the time, Pallas kernels for 0%

profile of v1, /device:TPU:8, one launch (start us, length us, event | category | flops | bytes accessed | tf_op | source)
XLA Modules:
  0.0 251.7 jit_solution(11565498838492972777)
XLA Ops:
  8.9 13.3 %all_gather.6 = bf16[256,1024]{1,0:T(8,128)(2,1)S(1)} all-gather(bf16[64,1024]{1,0:T(8,128)(2,1)} %param.17), channel_id=1, replica_groups=mesh['tok'=64,'pool'=4] {'pool'}, dimensions={0}, use_global_device_ids=true | all-gather | bytes 655360 | tf_op jit(solution)/shard_map/all_gather | solution.py:172
  24.6 1.0 copy.48
  25.9 1.2 reduce-window.6
  27.7 35.8 %all-gather.2.cloned.1.call-done = bf16[32,64,1024]{2,1,0:T(8,128)(2,1)} async-done(((bf16[8,64,1024]{2,1,0:T(8,128)(2,1)}), bf16[32,64,1024]{2,1,0:T(8,128)(2,1)}) %all-gather.2.cloned.1.call-update) | async-done | bytes 4194320 | tf_op jit(solution)/shard_map/all_gather | solution.py:187
  63.4 39.6 %while.15 = (s32[]{:T(128)}, f32[64,8,2]{0,2,1:T(2,128)S(1)}, f32[64,8,2]{0,2,1:T(2,128)S(1)}, f32[64,8,2,64]{0,3,2,1:T(8,128)}, s32[4,8]{1,0:T(4,128)S(1)}, /*i...) while((s32[]{:T(128)}, f32[64,8,2]{0,2,1:T(2,128)S(1)}, ...), condition=%wide.region_7.8_spmd.clone, body=%wide.region_4.7_spmd.clone.sunk | while | flops 141232656 | bytes 22882836 | solution.py:73
  63.9 1.3 constant_dynamic-slice_fusion.3
  66.3 1.5 fusion.79
  67.9 1.3 copy-done.1
  70.1 3.2 %fusion.81 = f32[64,8,2,64]{0,3,2,1:T(8,128)} fusion(bf16[512,8,64,1]{0,2,3,1:T(8,128)(2,1)S(1)} %bitcast.157, f32[8,512,64,2]{1,2,3,0:T(8,128)} %copy-done.1, f32[64,8,2]{0,2,1:T(2,128)S(1)} %max.5, pred[64,512]{1,0:T(8,128)(4,1)S(1)} %compare_and_fusion.2, f32[64,8,2,64]{0,3,2,1:T(8,128)} %get-tuple-element.209, f32[64,8,2]{0,2,1:T(2,128)S(1)} %bitcast.170), kind=kOutput, calls=%fused_computation.9.clone.1 | convolution fusion | flops 69861376 | bytes 3186688 | tf_op jit(solution)/shard_map/while/body/eval_jaxpr/qhgk,khd->qhgd/dot_general | solution.py:50
  73.8 1.3 constant_dynamic-slice_fusion.3
  76.2 1.5 fusion.79
  77.8 1.3 copy-done.1
  80.0 3.2 %fusion.81 = f32[64,8,2,64]{0,3,2,1:T(8,128)} fusion(bf16[512,8,64,1]{0,2,3,1:T(8,128)(2,1)S(1)} %bitcast.157, f32[8,512,64,2]{1,2,3,0:T(8,128)} %copy-done.1, f32[64,8,2]{0,2,1:T(2,128)S(1)} %max.5, pred[64,512]{1,0:T(8,128)(4,1)S(1)} %compare_and_fusion.2, f32[64,8,2,64]{0,3,2,1:T(8,128)} %get-tuple-element.209, f32[64,8,2]{0,2,1:T(2,128)S(1)} %bitcast.170), kind=kOutput, calls=%fused_computation.9.clone.1 | convolution fusion | flops 69861376 | bytes 3186688 | tf_op jit(solution)/shard_map/while/body/eval_jaxpr/qhgk,khd->qhgd/dot_general | solution.py:50
  83.7 1.3 constant_dynamic-slice_fusion.3
  86.1 1.5 fusion.79
  87.7 1.3 copy-done.1
  89.9 3.2 %fusion.81 = f32[64,8,2,64]{0,3,2,1:T(8,128)} fusion(bf16[512,8,64,1]{0,2,3,1:T(8,128)(2,1)S(1)} %bitcast.157, f32[8,512,64,2]{1,2,3,0:T(8,128)} %copy-done.1, f32[64,8,2]{0,2,1:T(2,128)S(1)} %max.5, pred[64,512]{1,0:T(8,128)(4,1)S(1)} %compare_and_fusion.2, f32[64,8,2,64]{0,3,2,1:T(8,128)} %get-tuple-element.209, f32[64,8,2]{0,2,1:T(2,128)S(1)} %bitcast.170), kind=kOutput, calls=%fused_computation.9.clone.1 | convolution fusion | flops 69861376 | bytes 3186688 | tf_op jit(solution)/shard_map/while/body/eval_jaxpr/qhgk,khd->qhgd/dot_general | solution.py:50
  93.6 1.3 constant_dynamic-slice_fusion.3
  96.0 1.5 fusion.79
  97.6 1.3 copy-done.1
  99.8 3.2 %fusion.81 = f32[64,8,2,64]{0,3,2,1:T(8,128)} fusion(bf16[512,8,64,1]{0,2,3,1:T(8,128)(2,1)S(1)} %bitcast.157, f32[8,512,64,2]{1,2,3,0:T(8,128)} %copy-done.1, f32[64,8,2]{0,2,1:T(2,128)S(1)} %max.5, pred[64,512]{1,0:T(8,128)(4,1)S(1)} %compare_and_fusion.2, f32[64,8,2,64]{0,3,2,1:T(8,128)} %get-tuple-element.209, f32[64,8,2]{0,2,1:T(2,128)S(1)} %bitcast.170), kind=kOutput, calls=%fused_computation.9.clone.1 | convolution fusion | flops 69861376 | bytes 3186688 | tf_op jit(solution)/shard_map/while/body/eval_jaxpr/qhgk,khd->qhgd/dot_general | solution.py:50
  103.1 1.1 divide_convert_fusion
  104.2 1.5 multiply_reduce_fusion
  105.9 4.1 %scatter_custom_fusion = bf16[1024,1024]{1,0:T(8,128)(2,1)} fusion(s32[512]{0:T(512)S(1)} %bitcast.171, bf16[]{:T(256)} %constant.42.clone.1, bf16[64,1024]{1,0:T(8,128)(2,1)S(1)} %multiply_convert_fusion), kind=kCustom, calls=%fused_computation.42 | custom fusion | bytes 2228226 | tf_op jit(solution)/shard_map/scatter | solution.py:206
  110.0 10.9 %all-to-all-start = ((bf16[64,16,1024]{2,1,0:T(8,128)(2,1)}), bf16[64,16,1024]{2,1,0:T(8,128)(2,1)}, u32[]{:S(2)}, u32[]{:S(2)}) async-start(bf16[64,16,1024]{2,1,0:T(8,128)(2,1)} %bitcast.158), calls=%async_computation | async-start | bytes 4194304 | tf_op jit(solution)/shard_map/all_to_all | solution.py:103
  121.4 50.6 %all-to-all-done = bf16[64,16,1024]{2,1,0:T(8,128)(2,1)} async-done(((bf16[64,16,1024]{2,1,0:T(8,128)(2,1)}), bf16[64,16,1024]{2,1,0:T(8,128)(2,1)}, u32[]{:S(2)}, u32[]{:S(2)}) %all-to-all-start) | async-done | bytes 2097184 | tf_op jit(solution)/shard_map/all_to_all | solution.py:103
  172.0 3.1 %fusion.23 = f32[1024,512]{1,0:T(8,128)S(1)} fusion(bf16[1024,1024]{1,0:T(8,128)(2,1)} %bitcast.19, bf16[1,1024,512]{2,1,0:T(8,128)(2,1)} %param.24), kind=kOutput, calls=%fused_computation.40 | convolution fusion | flops 1073741824 | bytes 5242880 | tf_op jit(solution)/shard_map/dot_general | solution.py:88
  175.9 3.1 %fusion.21 = f32[1024,512]{1,0:T(8,128)S(1)} fusion(bf16[1024,1024]{1,0:T(8,128)(2,1)} %bitcast.19, bf16[1,1024,512]{2,1,0:T(8,128)(2,1)} %collective-permute-done), kind=kOutput, calls=%fused_computation.38 | convolution fusion | flops 1073741824 | bytes 5242880 | tf_op jit(solution)/shard_map/dot_general | solution.py:88
  179.0 3.2 %add_convert_fusion = bf16[1024,1024]{1,0:T(8,128)(2,1)} fusion(bf16[1024,1024]{1,0:T(8,128)(2,1)S(1)} %fusion.31, f32[1024,512]{1,0:T(8,128)S(1)} %fusion.21, bf16[1,256,1024]{2,1,0:T(8,128)(2,1)} %collective-permute-done.1), kind=kOutput, calls=%fused_computation.25 | convolution fusion | flops 543686656 | bytes 6815744 | tf_op jit(solution)/shard_map/dot_general | solution.py:92
  182.2 5.7 %all-to-all-start.1 = ((bf16[64,16,1024]{2,1,0:T(8,128)(2,1)}), bf16[64,16,1024]{2,1,0:T(8,128)(2,1)}, u32[]{:S(2)}, u32[]{:S(2)}) async-start(bf16[64,16,1024]{2,1,0:T(8,128)(2,1)} %bitcast.163), calls=%async_computation.1 | async-start | bytes 4194304 | tf_op jit(solution)/shard_map/all_to_all | solution.py:105
  188.9 50.2 %all-to-all-done.1 = bf16[64,16,1024]{2,1,0:T(8,128)(2,1)} async-done(((bf16[64,16,1024]{2,1,0:T(8,128)(2,1)}), bf16[64,16,1024]{2,1,0:T(8,128)(2,1)}, u32[]{:S(2)}, u32[]{:S(2)}) %all-to-all-start.1) | async-done | bytes 2097184 | tf_op jit(solution)/shard_map/all_to_all | solution.py:105
  239.1 4.6 %gather_fusion = bf16[512,1024]{1,0:T(8,128)(2,1)S(1)} fusion(bf16[1024,1024]{1,0:T(8,128)(2,1)} %bitcast.25, s32[1024]{0:T(1024)S(1)} %pad_clamp_fusion), kind=kCustom, calls=%fused_computation | custom fusion | bytes 2099200 | tf_op jit(solution)/shard_map/gather | solution.py:215
  (123 shorter events, 18.0 us)
Async XLA Ops:
  7.2 97.0 %copy-start = (bf16[1024,1024]{1,0:T(8,128)(2,1)S(1)}, bf16[1024,1024]{1,0:T(8,128)(2,1)}, u32[]{:S(2)}) copy-start(bf16[1024,1024]{1,0:T(8,128)(2,1)} %param.22) | copy-start | bytes 6291460
  7.2 15.2 %copy-start.2 = (bf16[64,1024]{1,0:T(8,128)(2,1)S(1)}, bf16[64,1024]{1,0:T(8,128)(2,1)}, u32[]{:S(2)}) copy-start(bf16[64,1024]{1,0:T(8,128)(2,1)} %param.16) | copy-start | bytes 393220
  7.2 56.3 %all-gather.2.cloned.1.call-start = ((), (), s32[]{:S(2)}) async-start(), calls=%async_computation.2 | async-start | bytes 5242880 | tf_op jit(solution)/shard_map/all_gather | solution.py:187
  7.9 14.9 %copy-start.6 = (s32[1,256]{1,0:T(1,128)S(1)}, s32[1,256]{1,0:T(1,128)}, u32[]{:S(2)}) copy-start(s32[1,256]{1,0:T(1,128)} %param.21) | copy-start | bytes 3076
  23.4 2.2 copy-start.7
  23.4 2.3 copy-start.9
  23.5 3.9 %copy-start.3 = (s32[64,8]{0,1:T(8,128)S(1)}, s32[64,8]{0,1:T(8,128)}, u32[]{:S(2)}) copy-start(s32[64,8]{0,1:T(8,128)} %param.26) | copy-start | bytes 6148
  67.9 1.3 copy-start.1
  77.8 1.3 copy-start.1
  87.7 1.3 copy-start.1
  97.6 1.3 copy-start.1
  103.1 2.7 %copy-start.4 = (f32[1024]{0:T(1024)S(1)}, f32[1024]{0:T(1024)}, u32[]{:S(2)}) copy-start(f32[1024]{0:T(1024)} %param.23) | copy-start | bytes 12292
  110.0 11.1 %copy-start.8 = (bf16[1,256,1024]{2,1,0:T(8,128)(2,1)S(1)}, bf16[1,256,1024]{2,1,0:T(8,128)(2,1)}, u32[]{:S(2)}) copy-start(bf16[1,256,1024]{2,1,0:T(8,128)(2,1)} %param.25) | copy-start | bytes 1572868
  110.0 62.0 %all-to-all-start = ((bf16[64,16,1024]{2,1,0:T(8,128)(2,1)}), bf16[64,16,1024]{2,1,0:T(8,128)(2,1)}, u32[]{:S(2)}, u32[]{:S(2)}) async-start(bf16[64,16,1024]{2,1,0:T(8,128)(2,1)} %bitcast.158), calls=%async_computation | async-start | bytes 4194304 | tf_op jit(solution)/shard_map/all_to_all | solution.py:103
  120.8 55.0 %collective-permute-start = (bf16[1,1024,512]{2,1,0:T(8,128)(2,1)}, bf16[1,1024,512]{2,1,0:T(8,128)(2,1)}, u32[]{:S(2)}, u32[]{:S(2)}) collective-permute-start(bf16[1,1024,512]{2,1,0:T(8,128)(2,1)} %param.24), channel_id=1, source_target_pairs={{0,4},{4,0},{8,12},{12,8},{16,20},{20,16},{24,28},{28,24},{32,36},... | collective-permute-start | bytes 3145736 | tf_op jit(solution)/shard_map/ppermute | solution.py:134
  121.0 57.9 %collective-permute-start.1 = (bf16[1,256,1024]{2,1,0:T(8,128)(2,1)S(1)}, bf16[1,256,1024]{2,1,0:T(8,128)(2,1)}, u32[]{:S(2)}, u32[]{:S(2)}) collective-permute-start(bf16[1,256,1024]{2,1,0:T(8,128)(2,1)S(1)} %copy-done.8), channel_id=1, source_target_pairs={{0,4},{4,0},{8,12},{12,8},{16,20},{20,16},{24,28},{28,24},{32,36},... | collective-permute-start | bytes 1572872 | tf_op jit(solution)/shard_map/ppermute | solution.py:135
  182.2 5.8 %copy-start.5 = (f32[64,8]{0,1:T(8,128)S(1)}, f32[64,8]{0,1:T(8,128)}, u32[]{:S(2)}) copy-start(f32[64,8]{0,1:T(8,128)} %param.27) | copy-start | bytes 6148
  182.2 56.9 %all-to-all-start.1 = ((bf16[64,16,1024]{2,1,0:T(8,128)(2,1)}), bf16[64,16,1024]{2,1,0:T(8,128)(2,1)}, u32[]{:S(2)}, u32[]{:S(2)}) async-start(bf16[64,16,1024]{2,1,0:T(8,128)(2,1)} %bitcast.163), calls=%async_computation.1 | async-start | bytes 4194304 | tf_op jit(solution)/shard_map/all_to_all | solution.py:105
Sparse Core Ops, SparseCore 0:
  9.8 53.5 all-gather.1

commit v2 on v1

v2 whole, which is shorter than its diff:
```python
import jax
import jax.numpy as jnp
from jax import lax
from jax.sharding import PartitionSpec as P

QUERY_HEADS = 16
KEY_VALUE_HEADS = 8
HEAD_SIZE = 64
EXPERTS = 32
FF = 512
TOPK = 8
CAP = 32


score_scale = 0.015625
masked_filler = -1e30


def pair_ffn(rows_in, gate_up_pair, down_pair):
    hidden_units = gate_up_pair.shape[2] // 2
    total = None
    for part in range(gate_up_pair.shape[0]):
        gate_up = jnp.dot(rows_in, gate_up_pair[part], preferred_element_type=jnp.float32)
        inner = (jax.nn.silu(gate_up[:, :hidden_units]) * gate_up[:, hidden_units:]).astype(
            jnp.bfloat16
        )
        produced = jnp.dot(inner, down_pair[part], preferred_element_type=jnp.float32).astype(
            jnp.bfloat16
        ).astype(jnp.float32)
        total = produced if total is None else total + produced
    return total.astype(jnp.bfloat16)


def direct_dispatch(send_rows, split, expert_gate_up, expert_down):
    width = send_rows.shape[1]
    gate_up_pair, down_pair = expert_gate_up, expert_down
    unit_rows = send_rows.reshape(EXPERTS * split, CAP // split, width)
    arrived = lax.all_to_all(unit_rows, "tok", split_axis=0, concat_axis=0, tiled=True)
    produced = pair_ffn(arrived.reshape(-1, width), gate_up_pair, down_pair)
    returned = lax.all_to_all(
        produced.reshape(EXPERTS * split, CAP // split, width),
        "tok",
        split_axis=0,
        concat_axis=0,
        tiled=True,
    )
    return returned.reshape(EXPERTS * CAP, width)


def body(
    stream,
    queries,
    fresh_kv,
    cache_block_pool,
    block_table,
    cached_len,
    request_ids,
    output_weight,
    norm_gain,
    expert_gate_up,
    expert_down,
    routes,
    route_weight,
):
    tokens_per_device = stream.shape[0]
    width = stream.shape[1]
    tok_size = lax.axis_size("tok")
    sibling = [(t, t ^ 1) for t in range(tok_size)]
    sibling_gate_up = lax.ppermute(expert_gate_up, "tok", sibling)
    sibling_down = lax.ppermute(expert_down, "tok", sibling)
    heads_per_group = QUERY_HEADS // KEY_VALUE_HEADS
    kv_width = KEY_VALUE_HEADS * HEAD_SIZE
    pool_size = lax.axis_size("pool")
    pool_idx = lax.axis_index("pool")
    segments = request_ids[0]
    lengths = cached_len[0]
    table = block_table[0]
    list_len = table.shape[0]
    pool_blocks = cache_block_pool.shape[0]
    block_len = cache_block_pool.shape[1]
    group_tokens = segments.shape[0]
    request_range = jnp.arange(lengths.shape[0], dtype=jnp.int32)
    row_len = jnp.sum(
        jnp.where(segments[:, None] == request_range[None, :], lengths[None, :], 0), axis=1
    )
    local_slots = pool_idx * pool_blocks + jnp.arange(pool_blocks, dtype=jnp.int32)
    slot_block = (
        jnp.sum(
            jnp.where(
                table[None, :] == local_slots[:, None],
                jnp.arange(list_len, dtype=jnp.int32)[None, :] + 1,
                0,
            ),
            axis=1,
        )
        - 1
    )
    offsets = jnp.arange(block_len, dtype=jnp.int32)
    cache_pos = (slot_block[:, None] * block_len + offsets[None, :]).reshape(-1)
    cache_listed = jnp.repeat(slot_block >= 0, block_len)
    cache_visible = cache_listed[None, :] & (cache_pos[None, :] < row_len[:, None])
    query_order = jnp.arange(group_tokens, dtype=jnp.int32)
    fresh_order = pool_idx * tokens_per_device + jnp.arange(tokens_per_device, dtype=jnp.int32)
    fresh_seg = lax.dynamic_slice_in_dim(segments, pool_idx * tokens_per_device, tokens_per_device)
    fresh_visible = (fresh_seg[None, :] == segments[:, None]) & (
        fresh_order[None, :] <= query_order[:, None]
    )
    visible = jnp.concatenate([cache_visible, fresh_visible], axis=1)
    group_queries = lax.all_gather(queries, "pool", axis=0, tiled=True)
    key_value_pairs = jnp.concatenate(
        [cache_block_pool.reshape(pool_blocks * block_len, 2 * kv_width), fresh_kv], axis=0
    )
    key_count = key_value_pairs.shape[0]
    query_row_block = group_queries.reshape(
        group_tokens, KEY_VALUE_HEADS, heads_per_group, HEAD_SIZE
    )
    key_row_block = key_value_pairs[:, :kv_width].reshape(key_count, KEY_VALUE_HEADS, HEAD_SIZE)
    value_row_block = key_value_pairs[:, kv_width:].reshape(key_count, KEY_VALUE_HEADS, HEAD_SIZE)
    scores = (
        jnp.einsum(
            "qhgd,khd->qhgk",
            query_row_block,
            key_row_block,
            preferred_element_type=jnp.float32,
        )
        * score_scale
    )
    shown_keys = visible[:, None, None, :]
    scores = jnp.where(shown_keys, scores, masked_filler)
    highest = jnp.max(scores, axis=-1)
    weights = jnp.where(shown_keys, jnp.exp(scores - highest[..., None]), 0.0)
    denominator = jnp.sum(weights, axis=-1)
    summed = jnp.einsum(
        "qhgk,khd->qhgd",
        weights.astype(jnp.bfloat16),
        value_row_block,
        preferred_element_type=jnp.float32,
    )
    partial = jnp.concatenate(
        [summed, highest[..., None], denominator[..., None]], axis=-1
    ).reshape(pool_size, tokens_per_device, -1)
    gathered = lax.all_to_all(partial, "pool", split_axis=0, concat_axis=0, tiled=True).reshape(
        pool_size, tokens_per_device, KEY_VALUE_HEADS, heads_per_group, HEAD_SIZE + 2
    )
    part_max = gathered[..., HEAD_SIZE]
    running = jnp.max(part_max, axis=0)
    rescale = jnp.exp(part_max - running[None])
    denominator = jnp.sum(gathered[..., HEAD_SIZE + 1] * rescale, axis=0)
    summed = jnp.sum(gathered[..., :HEAD_SIZE] * rescale[..., None], axis=0)
    context = summed / denominator[..., None]
    attended = context.reshape(tokens_per_device, QUERY_HEADS * HEAD_SIZE).astype(jnp.bfloat16)
    residual = stream.astype(jnp.float32) + jnp.dot(
        attended, output_weight, preferred_element_type=jnp.float32
    )
    meansq = jnp.mean(residual * residual, axis=-1, keepdims=True)
    normed = (residual * lax.rsqrt(meansq + 1e-06) * norm_gain).astype(jnp.bfloat16)
    flat_routes = routes.reshape(-1)
    onehot = (flat_routes[:, None] == jnp.arange(EXPERTS, dtype=jnp.int32)[None, :]).astype(
        jnp.int32
    )
    earlier = jnp.cumsum(onehot, axis=0) - onehot
    slot_of = jnp.sum(earlier * onehot, axis=1)
    destination = flat_routes * CAP + slot_of
    send_rows = (
        jnp.zeros((EXPERTS * CAP, width), jnp.bfloat16)
        .at[destination]
        .set(jnp.repeat(normed, TOPK, axis=0))
    )
    split = FF // (expert_gate_up.shape[2] // 2)
    expert_rows = direct_dispatch(
        send_rows,
        split,
        jnp.concatenate([expert_gate_up, sibling_gate_up], axis=0),
        jnp.concatenate([expert_down, sibling_down], axis=0),
    )
    picked = expert_rows[destination].reshape(tokens_per_device, TOPK, width)
    experts_sum = jnp.einsum("tkd,tk->td", picked.astype(jnp.float32), route_weight)
    layer_out = (residual + experts_sum).astype(jnp.bfloat16)
    return (attended, layer_out)


def solution(mesh):
    placed = (
        P(("tok", "pool"), None),
        P(("tok", "pool"), None),
        P(("tok", "pool"), None),
        P(("tok", "pool"), None, None),
        P("tok", None),
        P("tok", None),
        P("tok", None),
        P(),
        P(),
        P("tok", None, None),
        P("tok", None, None),
        P(("tok", "pool"), None),
        P(("tok", "pool"), None),
    )
    return jax.shard_map(
        body,
        mesh=mesh,
        in_specs=placed,
        out_specs=(P(("tok", "pool"), None), P(("tok", "pool"), None)),
        check_vma=False,
    )
```

time: 253 us -> 221 us (0.87)
  waiting for transfers between devices: 137 us -> 113 us
  matrix products: 32.3 us -> 15.9 us
  between operations: 14.3 us -> 1.03 us
  other arithmetic: 7.52 us -> 20.4 us
  starting transfers between devices: 17.3 us -> 22.5 us
    all_gather x1 -> x0, waiting for transfers between devices: 35.8 us -> none  [body(): gathered_pool = lax.all_gather(cache_block_pool, 'pool', axis=0, tiled=True)]
    dot_general x10 -> x2, matrix products: 20.2 us -> 3.95 us  [the longest x1 2.43 us: body(): jnp.einsum('qhgk,khd->qhgd', weights.astype(jnp.bfloat16), value_row_bloc...]
    reshape x2 -> x4, local copies, waits for them, and re-layouts: 0.25 us -> 13.1 us  [the longest x2 6.07 us: body(): partial = jnp.concatenate([summed, highest[..., None], denominator[..., N...]
    all_to_all x0 -> x1, waiting for transfers between devices: none -> 11.9 us  [body(): lax.all_to_all(partial, 'pool', split_axis=0, concat_axis=0, tiled=True)]
    slice x0 -> x1, other arithmetic: none -> 8.08 us  [body(): denominator = jnp.sum(gathered[..., HEAD_SIZE + 1] * rescale, axis=0)]
    slice x16 -> x1, local copies, waits for them, and re-layouts: 5.71 us -> 0.22 us  [the longest x5 4.15 us: masked_scores(): key_value_pairs[:, :middle].reshape(key_count, kv_heads, head_dim)]
    dynamic_slice x5 -> x0, local copies, waits for them, and re-layouts: 5.41 us -> none  [the longest x4 5.33 us: scan_blocks(): lax.scan(visit, carried, (blocks.reshape(number // per_step, per_step, bl...]
    while x12 -> x0, local copies, waits for them, and re-layouts: 5.25 us -> none
  transfers between devices with their start and end apart: 5 -> 5, of which waited for: 3 -> 3; matrix products, arithmetic and copies ran while one was open for 6% -> 4% of each run, Pallas kernels for 0% -> 0%
where the time goes in v2:
time: 221 us; the launch traced here: 220 us
  waiting for transfers between devices  113 us (51%)
  local copies, waits for them, and re-layouts  31.8 us (14%)
  starting transfers between devices  22.5 us (10%)
  other arithmetic  20.4 us (9%)
  matrix products  15.9 us (7%)
  blocking collectives  14.8 us (7%)
    all_to_all x1, waiting for transfers between devices, direct_dispatch(): lax.all_to_all(produced.reshape(EXPERTS * split, CAP // split, width), 't...  51 us
    all_to_all x1, waiting for transfers between devices, direct_dispatch(): lax.all_to_all(unit_rows, 'tok', split_axis=0, concat_axis=0, tiled=True)  50.5 us
    all_gather x1, blocking collectives, body(): group_queries = lax.all_gather(queries, 'pool', axis=0, tiled=True)  14.8 us
    all_to_all x1, starting transfers between devices, direct_dispatch(): lax.all_to_all(unit_rows, 'tok', split_axis=0, concat_axis=0, tiled=True)  12.4 us
    all_to_all x1, waiting for transfers between devices, body(): lax.all_to_all(partial, 'pool', split_axis=0, concat_axis=0, tiled=True)  11.9 us
    slice x1, other arithmetic, body(): denominator = jnp.sum(gathered[..., HEAD_SIZE + 1] * rescale, axis=0)  8.08 us
    unnamed x28, local copies, waits for them, and re-layouts  6.27 us
    reshape x2, local copies, waits for them, and re-layouts, body(): partial = jnp.concatenate([summed, highest[..., None], denominator[..., N...  6.07 us
  transfers between devices with their start and end apart: 5, of which 3 were waited for; matrix products, arithmetic and copies ran while one was open for 4% of the time, Pallas kernels for 0%

profile of v2, /device:TPU:8, one launch (start us, length us, event | category | flops | bytes accessed | tf_op | source)
XLA Modules:
  0.0 219.9 jit_solution(3458734009087718512)
XLA Ops:
  0.7 1.0 select_reduce_fusion.1
  1.7 0.5 iota_add_fusion.1
  2.5 1.5 copy.51
  4.3 14.8 %all_gather.3 = bf16[256,1024]{1,0:T(8,128)(2,1)} all-gather(bf16[64,1024]{1,0:T(8,128)(2,1)} %param.14), channel_id=1, replica_groups=mesh['tok'=64,'pool'=4] {'pool'}, dimensions={0}, use_global_device_ids=true | all-gather | bytes 655360 | tf_op jit(solution)/shard_map/all_gather | solution.py:109
  19.1 2.1 copy.53
  21.3 0.7 fusion.34
  22.4 1.5 fusion
  23.9 2.2 %fusion.1 = f32[256,8,2]{0,2,1:T(2,128)S(1)} fusion(f32[8,576,256,2]{2,1,3,0:T(8,128)S(1)} %get-tuple-element.8, f32[256,8,2]{0,2,1:T(2,128)S(1)} %get-tuple-element.7, pred[256,576]{0,1:T(8,128)(4,1)S(1)} %pad_add_fusion), kind=kLoop, calls=%fused_computation.5 | loop fusion | flops 11792384 | bytes 9617408 | tf_op jit(solution)/shard_map/reduce_sum | solution.py:132
  26.2 2.4 %fusion.7 = f32[256,8,2,64]{0,3,2,1:T(8,128)S(1)} fusion(bf16[576,8,64,1]{0,2,3,1:T(8,128)(2,1)S(1)} %bitcast.111, f32[8,576,256,2]{2,1,3,0:T(8,128)S(1)} %get-tuple-element.8, f32[256,8,2]{0,2,1:T(2,128)S(1)} %get-tuple-element.7, pred[256,576]{0,1:T(8,128)(4,1)S(1)} %pad_add_fusion), kind=kOutput, calls=%fused_computation.12 | convolution fusion | flops 313786368 | bytes 11239424 | tf_op jit(solution)/shard_map/qhgk,khd->qhgd/dot_general | solution.py:133
  28.8 2.3 %reshape.174 = f32[4,64,1056]{1,0,2:T(4,128)} reshape(f32[256,8,2,66]{0,3,2,1:T(8,128)S(1)} %pad_maximum_fusion) | data formatting | bytes 2162688 | tf_op jit(solution)/shard_map/reshape | solution.py:141
  31.1 3.8 %copy.67 = f32[4,64,1056]{2,1,0:T(8,128)} copy(f32[4,64,1056]{1,0,2:T(4,128)} %reshape.174) | data formatting | bytes 2162688 | tf_op jit(solution)/shard_map/reshape | solution.py:141
  34.8 3.7 %all-to-all-start = ((f32[4,64,1056]{2,1,0:T(8,128)}), f32[4,64,1056]{2,1,0:T(8,128)S(1)}, u32[]{:S(2)}, u32[]{:S(2)}) async-start(f32[4,64,1056]{2,1,0:T(8,128)} %copy.67), calls=%async_computation | async-start | bytes 2359296 | tf_op jit(solution)/shard_map/all_to_all | solution.py:142
  38.8 1.2 reduce-window.6
  40.6 11.9 %all-to-all-done = f32[4,64,1056]{2,1,0:T(8,128)S(1)} async-done(((f32[4,64,1056]{2,1,0:T(8,128)}), f32[4,64,1056]{2,1,0:T(8,128)S(1)}, u32[]{:S(2)}, u32[]{:S(2)}) %all-to-all-start) | async-done | bytes 1081376 | tf_op jit(solution)/shard_map/all_to_all | solution.py:142
  52.5 5.5 %reshape.146 = f32[4,64,8,2,66]{4,3,2,1,0:T(2,128)} reshape(f32[4,64,1056]{2,1,0:T(8,128)S(1)} %all-to-all-done) | data formatting | bytes 2162688 | tf_op jit(solution)/shard_map/reshape | solution.py:142
  58.0 8.1 %fusion.44 = (f32[4,64,8,2,1]{4,3,2,1,0:T(2,128)}, f32[64,8,2]{2,1,0:T(8,128)S(1)}, f32[4,64,8,2,1]{4,3,2,1,0:T(2,128)}) fusion(f32[4,64,8,2,66]{4,3,2,1,0:T(2,128)} %reshape.146), kind=kLoop, calls=%fused_computation.81 | loop fusion | flops 3072 | bytes 69632 | tf_op jit(solution)/shard_map/slice | solution.py:148
  66.1 2.9 %copy.68 = f32[4,64,8,2,1]{1,2,3,0,4:T(8,128)S(1)} copy(f32[4,64,8,2,1]{4,3,2,1,0:T(2,128)} %get-tuple-element.4) | data formatting | bytes 32768
  68.9 2.9 %copy.69 = f32[4,64,8,2,1]{1,2,4,3,0:T(8,128)S(1)} copy(f32[4,64,8,2,1]{4,3,2,1,0:T(2,128)} %get-tuple-element.2) | data formatting | bytes 32768
  72.6 4.3 %fusion.6 = f32[64,8,2,64]{3,2,1,0:T(2,128)S(1)} fusion(f32[4,64,8,2,66]{4,3,2,1,0:T(2,128)} %reshape.146, f32[4,64,8,2]{3,2,1,0:T(8,128)S(1)} %copy.56), kind=kLoop, calls=%fused_computation.11 | loop fusion | flops 458752 | bytes 1327104 | tf_op jit(solution)/shard_map/reduce_sum | solution.py:149
  76.9 0.7 divide_convert_fusion
  77.9 1.5 multiply_reduce_fusion
  79.6 4.1 %scatter_custom_fusion = bf16[1024,1024]{1,0:T(8,128)(2,1)} fusion(s32[512]{0:T(512)S(1)} %bitcast.112, bf16[]{:T(256)} %constant.15.clone.1, bf16[64,1024]{1,0:T(8,128)(2,1)S(1)} %multiply_convert_fusion), kind=kCustom, calls=%fused_computation.27 | custom fusion | bytes 2228226 | tf_op jit(solution)/shard_map/scatter | solution.py:167
  83.7 12.4 %all-to-all-start.1 = ((bf16[64,16,1024]{2,1,0:T(8,128)(2,1)}), bf16[64,16,1024]{2,1,0:T(8,128)(2,1)}, u32[]{:S(2)}, u32[]{:S(2)}) async-start(bf16[64,16,1024]{2,1,0:T(8,128)(2,1)} %bitcast.106), calls=%async_computation.1 | async-start | bytes 4194304 | tf_op jit(solution)/shard_map/all_to_all | solution.py:38
  96.7 50.5 %all-to-all-done.1 = bf16[64,16,1024]{2,1,0:T(8,128)(2,1)} async-done(((bf16[64,16,1024]{2,1,0:T(8,128)(2,1)}), bf16[64,16,1024]{2,1,0:T(8,128)(2,1)}, u32[]{:S(2)}, u32[]{:S(2)}) %all-to-all-start.1) | async-done | bytes 2097184 | tf_op jit(solution)/shard_map/all_to_all | solution.py:38
  147.3 2.9 %fusion.16 = f32[1024,512]{1,0:T(8,128)S(1)} fusion(bf16[1024,1024]{1,0:T(8,128)(2,1)} %bitcast.22, bf16[1,1024,512]{2,1,0:T(8,128)(2,1)S(1)} %copy-done.9), kind=kOutput, calls=%fused_computation.25 | convolution fusion | flops 1073741824 | bytes 5242880 | tf_op jit(solution)/shard_map/dot_general | solution.py:23
  150.2 0.7 fusion.22
  150.9 3.1 %fusion.14 = f32[1024,512]{1,0:T(8,128)S(1)} fusion(bf16[1024,1024]{1,0:T(8,128)(2,1)} %bitcast.22, bf16[1,1024,512]{2,1,0:T(8,128)(2,1)} %collective-permute-done), kind=kOutput, calls=%fused_computation.23 | convolution fusion | flops 1073741824 | bytes 5242880 | tf_op jit(solution)/shard_map/dot_general | solution.py:23
  154.0 3.2 %add_convert_fusion = bf16[1024,1024]{1,0:T(8,128)(2,1)} fusion(bf16[1024,1024]{1,0:T(8,128)(2,1)S(1)} %fusion.22, f32[1024,512]{1,0:T(8,128)S(1)} %fusion.14, bf16[1,256,1024]{2,1,0:T(8,128)(2,1)} %collective-permute-done.1), kind=kOutput, calls=%fused_computation.9 | convolution fusion | flops 543686656 | bytes 6815744 | tf_op jit(solution)/shard_map/dot_general | solution.py:27
  157.3 5.8 %all-to-all-start.2 = ((bf16[64,16,1024]{2,1,0:T(8,128)(2,1)}), bf16[64,16,1024]{2,1,0:T(8,128)(2,1)}, u32[]{:S(2)}, u32[]{:S(2)}) async-start(bf16[64,16,1024]{2,1,0:T(8,128)(2,1)} %bitcast.108), calls=%async_computation.2 | async-start | bytes 4194304 | tf_op jit(solution)/shard_map/all_to_all | solution.py:40
  163.2 51.0 %all-to-all-done.2 = bf16[64,16,1024]{2,1,0:T(8,128)(2,1)} async-done(((bf16[64,16,1024]{2,1,0:T(8,128)(2,1)}), bf16[64,16,1024]{2,1,0:T(8,128)(2,1)}, u32[]{:S(2)}, u32[]{:S(2)}) %all-to-all-start.2) | async-done | bytes 2097184 | tf_op jit(solution)/shard_map/all_to_all | solution.py:40
  214.2 4.6 %gather_fusion = bf16[512,1024]{1,0:T(8,128)(2,1)S(1)} fusion(bf16[1024,1024]{1,0:T(8,128)(2,1)} %bitcast.28, s32[1024]{0:T(1024)S(1)} %pad_clamp_fusion), kind=kCustom, calls=%fused_computation | custom fusion | bytes 2099200 | tf_op jit(solution)/shard_map/gather | solution.py:176
  219.2 0.7 fusion.30
  (66 shorter events, 4.2 us)
Async XLA Ops:
  0.6 77.3 %copy-start = (bf16[1024,1024]{1,0:T(8,128)(2,1)S(1)}, bf16[1024,1024]{1,0:T(8,128)(2,1)}, u32[]{:S(2)}) copy-start(bf16[1024,1024]{1,0:T(8,128)(2,1)} %param.20) | copy-start | bytes 6291460
  0.6 3.4 %copy-start.3 = (bf16[64,1024]{1,0:T(8,128)(2,1)S(1)}, bf16[64,1024]{1,0:T(8,128)(2,1)}, u32[]{:S(2)}) copy-start(bf16[64,1024]{1,0:T(8,128)(2,1)} %param.15) | copy-start | bytes 393220
  2.5 18.6 %copy-start.7 = (s32[1,256]{1,0:T(1,128)S(1)}, s32[1,256]{1,0:T(1,128)}, u32[]{:S(2)}) copy-start(s32[1,256]{1,0:T(1,128)} %param.19) | copy-start | bytes 3076
  2.5 18.7 %copy-start.8 = (s32[1,3]{1,0:T(1,128)S(1)}, s32[1,3]{1,0:T(1,128)}, u32[]{:S(2)}) copy-start(s32[1,3]{1,0:T(1,128)} %param.18) | copy-start | bytes 40
  21.1 1.3 copy-start.1
  31.1 7.5 %copy-start.4 = (s32[64,8]{0,1:T(8,128)S(1)}, s32[64,8]{0,1:T(8,128)}, u32[]{:S(2)}) copy-start(s32[64,8]{0,1:T(8,128)} %param.24) | copy-start | bytes 6148
  34.8 17.7 %all-to-all-start = ((f32[4,64,1056]{2,1,0:T(8,128)}), f32[4,64,1056]{2,1,0:T(8,128)S(1)}, u32[]{:S(2)}, u32[]{:S(2)}) async-start(f32[4,64,1056]{2,1,0:T(8,128)} %copy.67), calls=%async_computation | async-start | bytes 2359296 | tf_op jit(solution)/shard_map/all_to_all | solution.py:142
  76.9 2.5 %copy-start.5 = (f32[1024]{0:T(1024)S(1)}, f32[1024]{0:T(1024)}, u32[]{:S(2)}) copy-start(f32[1024]{0:T(1024)} %param.21) | copy-start | bytes 12292
  77.9 5.8 %copy-start.2 = (bf16[64,1024]{1,0:T(8,128)(2,1)}, bf16[64,1024]{1,0:T(8,128)(2,1)S(1)}, u32[]{:S(2)}) copy-start(bf16[64,1024]{1,0:T(8,128)(2,1)S(1)} %convert_element_type.49) | copy-start | bytes 393220
  83.7 12.4 %copy-start.9 = (bf16[1,1024,512]{2,1,0:T(8,128)(2,1)S(1)}, bf16[1,1024,512]{2,1,0:T(8,128)(2,1)}, u32[]{:S(2)}) copy-start(bf16[1,1024,512]{2,1,0:T(8,128)(2,1)} %param.22) | copy-start | bytes 3145732
  83.7 63.6 %all-to-all-start.1 = ((bf16[64,16,1024]{2,1,0:T(8,128)(2,1)}), bf16[64,16,1024]{2,1,0:T(8,128)(2,1)}, u32[]{:S(2)}, u32[]{:S(2)}) async-start(bf16[64,16,1024]{2,1,0:T(8,128)(2,1)} %bitcast.106), calls=%async_computation.1 | async-start | bytes 4194304 | tf_op jit(solution)/shard_map/all_to_all | solution.py:38
  96.1 54.8 %collective-permute-start = (bf16[1,1024,512]{2,1,0:T(8,128)(2,1)S(1)}, bf16[1,1024,512]{2,1,0:T(8,128)(2,1)}, u32[]{:S(2)}, u32[]{:S(2)}) collective-permute-start(bf16[1,1024,512]{2,1,0:T(8,128)(2,1)S(1)} %copy-done.9), channel_id=1, source_target_pairs={{0,4},{4,0},{8,12},{12,8},{16,20},{20,16},{24,28},{28,24},{32,36},... | collective-permute-start | bytes 3145736 | tf_op jit(solution)/shard_map/ppermute | solution.py:69
  96.3 57.7 %collective-permute-start.1 = (bf16[1,256,1024]{2,1,0:T(8,128)(2,1)}, bf16[1,256,1024]{2,1,0:T(8,128)(2,1)}, u32[]{:S(2)}, u32[]{:S(2)}) collective-permute-start(bf16[1,256,1024]{2,1,0:T(8,128)(2,1)} %param.23), channel_id=1, source_target_pairs={{0,4},{4,0},{8,12},{12,8},{16,20},{20,16},{24,28},{28,24},{32,36},... | collective-permute-start | bytes 1572872 | tf_op jit(solution)/shard_map/ppermute | solution.py:70
  147.3 2.9 %copy-start.10 = (bf16[1,256,1024]{2,1,0:T(8,128)(2,1)S(1)}, bf16[1,256,1024]{2,1,0:T(8,128)(2,1)}, u32[]{:S(2)}) copy-start(bf16[1,256,1024]{2,1,0:T(8,128)(2,1)} %param.23) | copy-start | bytes 1572868
  157.3 5.8 %copy-start.6 = (f32[64,8]{0,1:T(8,128)S(1)}, f32[64,8]{0,1:T(8,128)}, u32[]{:S(2)}) copy-start(f32[64,8]{0,1:T(8,128)} %param.25) | copy-start | bytes 6148
  157.3 56.9 %all-to-all-start.2 = ((bf16[64,16,1024]{2,1,0:T(8,128)(2,1)}), bf16[64,16,1024]{2,1,0:T(8,128)(2,1)}, u32[]{:S(2)}, u32[]{:S(2)}) async-start(bf16[64,16,1024]{2,1,0:T(8,128)(2,1)} %bitcast.108), calls=%async_computation.2 | async-start | bytes 4194304 | tf_op jit(solution)/shard_map/all_to_all | solution.py:40

commit v3 on v2

--- a/solution.py
+++ b/solution.py
@@ -98,15 +98,28 @@
     offsets = jnp.arange(block_len, dtype=jnp.int32)
     cache_pos = (slot_block[:, None] * block_len + offsets[None, :]).reshape(-1)
     cache_listed = jnp.repeat(slot_block >= 0, block_len)
-    cache_visible = cache_listed[None, :] & (cache_pos[None, :] < row_len[:, None])
-    query_order = jnp.arange(group_tokens, dtype=jnp.int32)
+    shifts = range(pool_size)
+    block_source = [(pool_idx - shift) % pool_size for shift in shifts]
+    query_order = (
+        jnp.stack(block_source)[:, None] * tokens_per_device
+        + jnp.arange(tokens_per_device, dtype=jnp.int32)[None, :]
+    ).reshape(-1)
+    query_seg = segments[query_order]
+    query_len = row_len[query_order]
+    cache_visible = cache_listed[None, :] & (cache_pos[None, :] < query_len[:, None])
     fresh_order = pool_idx * tokens_per_device + jnp.arange(tokens_per_device, dtype=jnp.int32)
     fresh_seg = lax.dynamic_slice_in_dim(segments, pool_idx * tokens_per_device, tokens_per_device)
-    fresh_visible = (fresh_seg[None, :] == segments[:, None]) & (
+    fresh_visible = (fresh_seg[None, :] == query_seg[:, None]) & (
         fresh_order[None, :] <= query_order[:, None]
     )
     visible = jnp.concatenate([cache_visible, fresh_visible], axis=1)
-    group_queries = lax.all_gather(queries, "pool", axis=0, tiled=True)
+    query_blocks = [queries] + [
+        lax.ppermute(
+            queries, "pool", [(i, (i + shift) % pool_size) for i in range(pool_size)]
+        )
+        for shift in shifts[1:]
+    ]
+    group_queries = jnp.concatenate(query_blocks, axis=0)
     key_value_pairs = jnp.concatenate(
         [cache_block_pool.reshape(pool_blocks * block_len, 2 * kv_width), fresh_kv], axis=0
     )
@@ -136,18 +149,34 @@
         value_row_block,
         preferred_element_type=jnp.float32,
     )
+    stat_pad = 128 - 2 * QUERY_HEADS
     partial = jnp.concatenate(
-        [summed, highest[..., None], denominator[..., None]], axis=-1
+        [
+            summed.reshape(group_tokens, QUERY_HEADS * HEAD_SIZE),
+            highest.reshape(group_tokens, QUERY_HEADS),
+            denominator.reshape(group_tokens, QUERY_HEADS),
+            jnp.zeros((group_tokens, stat_pad), jnp.float32),
+        ],
+        axis=1,
     ).reshape(pool_size, tokens_per_device, -1)
-    gathered = lax.all_to_all(partial, "pool", split_axis=0, concat_axis=0, tiled=True).reshape(
-        pool_size, tokens_per_device, KEY_VALUE_HEADS, heads_per_group, HEAD_SIZE + 2
-    )
-    part_max = gathered[..., HEAD_SIZE]
+    partials = [partial[0]] + [
+        lax.ppermute(
+            partial[shift], "pool", [(i, (i - shift) % pool_size) for i in range(pool_size)]
+        )
+        for shift in shifts[1:]
+    ]
+    gathered = jnp.stack(partials)
+    acc_width = QUERY_HEADS * HEAD_SIZE
+    part_max = gathered[:, :, acc_width : acc_width + QUERY_HEADS]
+    part_sum = gathered[:, :, acc_width + QUERY_HEADS : acc_width + 2 * QUERY_HEADS]
     running = jnp.max(part_max, axis=0)
     rescale = jnp.exp(part_max - running[None])
-    denominator = jnp.sum(gathered[..., HEAD_SIZE + 1] * rescale, axis=0)
-    summed = jnp.sum(gathered[..., :HEAD_SIZE] * rescale[..., None], axis=0)
-    context = summed / denominator[..., None]
+    denominator = jnp.sum(part_sum * rescale, axis=0)
+    summed = jnp.sum(
+        gathered[:, :, :acc_width] * jnp.repeat(rescale, HEAD_SIZE, axis=2), axis=0
+    )
+    denominator = jnp.repeat(denominator, HEAD_SIZE, axis=1)
+    context = summed / denominator
     attended = context.reshape(tokens_per_device, QUERY_HEADS * HEAD_SIZE).astype(jnp.bfloat16)
     residual = stream.astype(jnp.float32) + jnp.dot(
         attended, output_weight, preferred_element_type=jnp.float32

time: 221 us -> 213 us (0.964)
  blocking collectives: 14.8 us -> 0 us
  matrix products: 15.9 us -> 23.5 us
  starting transfers between devices: 22.5 us -> 27.2 us
  other arithmetic: 20.4 us -> 16.5 us
    all_gather x1 -> x0, blocking collectives: 14.8 us -> none  [body(): group_queries = lax.all_gather(queries, 'pool', axis=0, tiled=True)]
    ppermute x0 -> x6, waiting for transfers between devices: none -> 13.1 us  [the longest x3 13.1 us: body(): lax.ppermute(partial[shift], 'pool', [(i, (i - shift) % pool_size) for i...]
    all_to_all x1 -> x0, waiting for transfers between devices: 11.9 us -> none  [body(): lax.all_to_all(partial, 'pool', split_axis=0, concat_axis=0, tiled=True)]
    ppermute x0 -> x6, starting transfers between devices: none -> 8.47 us  [the longest x3 5.73 us: body(): lax.ppermute(queries, 'pool', [(i, (i + shift) % pool_size) for i in rang...]
    slice x1 -> x0, other arithmetic: 8.08 us -> none  [body(): denominator = jnp.sum(gathered[..., HEAD_SIZE + 1] * rescale, axis=0)]
    reshape x3 -> x6, local copies, waits for them, and re-layouts: 11.6 us -> 5.63 us  [the longest x1 2.76 us: body(): jnp.repeat(rescale, HEAD_SIZE, axis=2)]
    dot_general x1, matrix products: 1.52 us -> 6.17 us  [body(): jnp.einsum('qhgd,khd->qhgk', query_row_block, key_row_block, preferred_el...]
    gather x0 -> x2, local copies, waits for them, and re-layouts: none -> 3.96 us  [the longest x1 2.02 us: body(): query_seg = segments[query_order]]
  transfers between devices with their start and end apart: 5 -> 10, of which waited for: 3 -> 5; matrix products, arithmetic and copies ran while one was open for 4% -> 11% of each run, Pallas kernels for 0% -> 0%
where the time goes in v3:
time: 213 us; the launch traced here: 212 us
  waiting for transfers between devices  114 us (54%)
  local copies, waits for them, and re-layouts  30.1 us (14%)
  starting transfers between devices  27.2 us (13%)
  matrix products  23.5 us (11%)
  other arithmetic  16.5 us (8%)
    all_to_all x1, waiting for transfers between devices, direct_dispatch(): lax.all_to_all(unit_rows, 'tok', split_axis=0, concat_axis=0, tiled=True)  50.6 us
    all_to_all x1, waiting for transfers between devices, direct_dispatch(): lax.all_to_all(produced.reshape(EXPERTS * split, CAP // split, width), 't...  50.2 us
    ppermute x3, waiting for transfers between devices, body(): lax.ppermute(partial[shift], 'pool', [(i, (i - shift) % pool_size) for i...  13.1 us
    all_to_all x1, starting transfers between devices, direct_dispatch(): lax.all_to_all(unit_rows, 'tok', split_axis=0, concat_axis=0, tiled=True)  12.4 us
    dot_general x2, matrix products, pair_ffn(): jnp.dot(rows_in, gate_up_pair[part], preferred_element_type=jnp.float32)  6.21 us
    dot_general x1, matrix products, body(): jnp.einsum('qhgd,khd->qhgk', query_row_block, key_row_block, preferred_el...  6.17 us
    reduce_sum x1, other arithmetic, body(): denominator = jnp.sum(weights, axis=-1)  5.89 us
    all_to_all x1, starting transfers between devices, direct_dispatch(): lax.all_to_all(produced.reshape(EXPERTS * split, CAP // split, width), 't...  5.74 us
  transfers between devices with their start and end apart: 10, of which 5 were waited for; matrix products, arithmetic and copies ran while one was open for 11% of the time, Pallas kernels for 0%

profile of v3, /device:TPU:8, one launch (start us, length us, event | category | flops | bytes accessed | tf_op | source)
XLA Modules:
  0.0 212.1 jit_solution(5576416400010934564)
XLA Ops:
  0.6 1.6 collective-permute-start
  2.2 2.7 %collective-permute-start.1 = (bf16[64,1024]{1,0:T(8,128)(2,1)}, bf16[64,1024]{1,0:T(8,128)(2,1)}, u32[]{:S(2)}, u32[]{:S(2)}) collective-permute-start(bf16[64,1024]{1,0:T(8,128)(2,1)} %param.14), channel_id=1, source_target_pairs={{0,2},{1,3},{2,0},{3,1},{4,6},{5,7},{6,4},{7,5},{8,10},{9,11},{10,... | collective-permute-start | bytes 393224 | tf_op jit(solution)/shard_map/ppermute | solution.py:117
  4.9 1.4 collective-permute-start.2
  10.0 2.0 gather_fusion.1
  12.8 1.9 gather_fusion
  15.0 1.5 copy.50
  17.4 1.2 reduce-window.6
  19.3 2.1 %pad_maximum_fusion.1 = (bf16[576,512]{0,1:T(8,128)(2,1)}, bf16[576,512]{0,1:T(8,128)(2,1)}) fusion(bf16[64,1024]{0,1:T(8,128)(2,1)} %copy.51, bf16[512,1024]{0,1:T(8,128)(2,1)S(1)} %copy.50), kind=kLoop, calls=%fused_computation.32 | loop fusion | flops 2359296 | bytes 2359296 | tf_op jit(solution)/shard_map/concatenate | solution.py:123
  21.5 1.2 pad_maximum_fusion.2
  22.7 1.0 copy.52
  23.7 6.2 %fusion = (f32[256,8,2]{0,2,1:T(2,128)S(1)}, f32[8,576,256,2]{2,1,3,0:T(8,128)}) fusion(pred[256,576]{0,1:T(8,128)(4,1)S(1)} %pad_add_fusion, bf16[576,8,64,1]{0,2,3,1:T(8,128)(2,1)S(1)} %bitcast.119, bf16[256,8,2,64]{0,3,2,1:T(8,128)(2,1)} %bitcast.121), kind=kOutput, calls=%fused_computation.6 | convolution fusion | flops 309063680 | bytes 10715136 | tf_op jit(solution)/shard_map/qhgd,khd->qhgk/dot_general | solution.py:133
  29.9 5.9 %fusion.1 = f32[256,8,2]{0,2,1:T(2,128)S(1)} fusion(f32[8,576,256,2]{2,1,3,0:T(8,128)} %get-tuple-element.19, f32[256,8,2]{0,2,1:T(2,128)S(1)} %get-tuple-element.18, pred[256,576]{0,1:T(8,128)(4,1)S(1)} %pad_add_fusion), kind=kLoop, calls=%fused_computation.7 | loop fusion | flops 11792384 | bytes 9617408 | tf_op jit(solution)/shard_map/reduce_sum | solution.py:145
  36.5 5.2 %fusion.3 = f32[8,64,256,2]{2,1,3,0:T(8,128)S(1)} fusion(bf16[576,8,64,1]{0,2,3,1:T(8,128)(2,1)} %bitcast.124, f32[8,576,256,2]{2,1,3,0:T(8,128)} %get-tuple-element.19, f32[256,8,2]{0,2,1:T(2,128)S(1)} %get-tuple-element.18, pred[256,576]{0,1:T(8,128)(4,1)S(1)} %pad_add_fusion), kind=kOutput, calls=%fused_computation.9 | convolution fusion | flops 313786368 | bytes 11239424 | tf_op jit(solution)/shard_map/qhgk,khd->qhgd/dot_general | solution.py:146
  41.7 1.3 copy.53
  44.4 1.4 concatenate.19
  46.0 2.6 %collective-permute-start.4 = (f32[64,1152]{1,0:T(8,128)S(1)}, f32[64,1152]{1,0:T(8,128)S(1)}, u32[]{:S(2)}, u32[]{:S(2)}) collective-permute-start(f32[64,1152]{1,0:T(8,128)S(1)} %get-tuple-element.14), channel_id=1, source_target_pairs={{0,2},{1,3},{2,0},{3,1},{4,6},{5,7},{6,4},{7,5},{8,10},{9,11},{10,... | collective-permute-start | bytes 884744 | tf_op jit(solution)/shard_map/ppermute | solution.py:163
  48.8 7.1 %collective-permute-done.3 = f32[64,1152]{1,0:T(8,128)S(1)} collective-permute-done((f32[64,1152]{1,0:T(8,128)S(1)}, f32[64,1152]{1,0:T(8,128)S(1)}, u32[]{:S(2)}, u32[]{:S(2)}) %collective-permute-start.3) | collective-permute-done | bytes 294944 | tf_op jit(solution)/shard_map/ppermute | solution.py:163
  55.9 1.6 collective-permute-done.4
  57.5 4.3 %collective-permute-done.5 = f32[64,1152]{1,0:T(8,128)S(1)} collective-permute-done((f32[64,1152]{1,0:T(8,128)S(1)}, f32[64,1152]{1,0:T(8,128)S(1)}, u32[]{:S(2)}, u32[]{:S(2)}) %collective-permute-start.5) | collective-permute-done | bytes 294944 | tf_op jit(solution)/shard_map/ppermute | solution.py:163
  62.7 2.0 broadcast_in_dim.93
  64.6 2.8 %reshape.235 = f32[4,64,1024]{2,1,0:T(8,128)} reshape(f32[4,64,16,64]{3,2,1,0:T(8,128)} %broadcast_in_dim.93) | data formatting | bytes 2097152 | tf_op jit(solution)/shard_map/reshape | solution.py:176
  67.4 1.4 fusion.8
  69.9 1.5 multiply_reduce_fusion
  71.5 4.1 %scatter_custom_fusion = bf16[1024,1024]{1,0:T(8,128)(2,1)} fusion(s32[512]{0:T(512)S(1)} %bitcast.125, bf16[]{:T(256)} %constant.78.clone.1, bf16[64,1024]{1,0:T(8,128)(2,1)S(1)} %multiply_convert_fusion), kind=kCustom, calls=%fused_computation.28 | custom fusion | bytes 2228226 | tf_op jit(solution)/shard_map/scatter | solution.py:196
  75.6 12.4 %all-to-all-start = ((bf16[64,16,1024]{2,1,0:T(8,128)(2,1)}), bf16[64,16,1024]{2,1,0:T(8,128)(2,1)}, u32[]{:S(2)}, u32[]{:S(2)}) async-start(bf16[64,16,1024]{2,1,0:T(8,128)(2,1)} %bitcast.109), calls=%async_computation | async-start | bytes 4194304 | tf_op jit(solution)/shard_map/all_to_all | solution.py:38
  88.6 50.6 %all-to-all-done = bf16[64,16,1024]{2,1,0:T(8,128)(2,1)} async-done(((bf16[64,16,1024]{2,1,0:T(8,128)(2,1)}), bf16[64,16,1024]{2,1,0:T(8,128)(2,1)}, u32[]{:S(2)}, u32[]{:S(2)}) %all-to-all-start) | async-done | bytes 2097184 | tf_op jit(solution)/shard_map/all_to_all | solution.py:38
  139.2 3.1 %fusion.13 = f32[1024,512]{1,0:T(8,128)S(1)} fusion(bf16[1024,1024]{1,0:T(8,128)(2,1)} %bitcast.30, bf16[1,1024,512]{2,1,0:T(8,128)(2,1)} %param.22), kind=kOutput, calls=%fused_computation.26 | convolution fusion | flops 1073741824 | bytes 5242880 | tf_op jit(solution)/shard_map/dot_general | solution.py:23
  143.1 3.1 %fusion.11 = f32[1024,512]{1,0:T(8,128)S(1)} fusion(bf16[1024,1024]{1,0:T(8,128)(2,1)} %bitcast.30, bf16[1,1024,512]{2,1,0:T(8,128)(2,1)} %collective-permute-done.6), kind=kOutput, calls=%fused_computation.24 | convolution fusion | flops 1073741824 | bytes 5242880 | tf_op jit(solution)/shard_map/dot_general | solution.py:23
  146.2 3.2 %add_convert_fusion = bf16[1024,1024]{1,0:T(8,128)(2,1)} fusion(bf16[1024,1024]{1,0:T(8,128)(2,1)S(1)} %fusion.19, f32[1024,512]{1,0:T(8,128)S(1)} %fusion.11, bf16[1,256,1024]{2,1,0:T(8,128)(2,1)} %collective-permute-done.7), kind=kOutput, calls=%fused_computation.11 | convolution fusion | flops 543686656 | bytes 6815744 | tf_op jit(solution)/shard_map/dot_general | solution.py:27
  149.5 5.7 %all-to-all-start.1 = ((bf16[64,16,1024]{2,1,0:T(8,128)(2,1)}), bf16[64,16,1024]{2,1,0:T(8,128)(2,1)}, u32[]{:S(2)}, u32[]{:S(2)}) async-start(bf16[64,16,1024]{2,1,0:T(8,128)(2,1)} %bitcast.120), calls=%async_computation.1 | async-start | bytes 4194304 | tf_op jit(solution)/shard_map/all_to_all | solution.py:40
  156.1 50.2 %all-to-all-done.1 = bf16[64,16,1024]{2,1,0:T(8,128)(2,1)} async-done(((bf16[64,16,1024]{2,1,0:T(8,128)(2,1)}), bf16[64,16,1024]{2,1,0:T(8,128)(2,1)}, u32[]{:S(2)}, u32[]{:S(2)}) %all-to-all-start.1) | async-done | bytes 2097184 | tf_op jit(solution)/shard_map/all_to_all | solution.py:40
  206.4 4.6 %gather_fusion.2 = bf16[512,1024]{1,0:T(8,128)(2,1)S(1)} fusion(bf16[1024,1024]{1,0:T(8,128)(2,1)} %bitcast.36, s32[1024]{0:T(1024)S(1)} %pad_clamp_fusion), kind=kCustom, calls=%fused_computation.2 | custom fusion | bytes 2099200 | tf_op jit(solution)/shard_map/gather | solution.py:205
  (80 shorter events, 14.2 us)
Async XLA Ops:
  0.6 69.2 %copy-start = (bf16[1024,1024]{1,0:T(8,128)(2,1)S(1)}, bf16[1024,1024]{1,0:T(8,128)(2,1)}, u32[]{:S(2)}) copy-start(bf16[1024,1024]{1,0:T(8,128)(2,1)} %param.20) | copy-start | bytes 6291460
  0.6 20.8 %collective-permute-start = (bf16[64,1024]{1,0:T(8,128)(2,1)}, bf16[64,1024]{1,0:T(8,128)(2,1)}, u32[]{:S(2)}, u32[]{:S(2)}) collective-permute-start(bf16[64,1024]{1,0:T(8,128)(2,1)} %param.14), channel_id=1, source_target_pairs={{0,1},{1,2},{2,3},{3,0},{4,5},{5,6},{6,7},{7,4},{8,9},{9,10},{10,1... | collective-permute-start | bytes 393224 | tf_op jit(solution)/shard_map/ppermute | solution.py:117
  2.2 19.2 %collective-permute-start.1 = (bf16[64,1024]{1,0:T(8,128)(2,1)}, bf16[64,1024]{1,0:T(8,128)(2,1)}, u32[]{:S(2)}, u32[]{:S(2)}) collective-permute-start(bf16[64,1024]{1,0:T(8,128)(2,1)} %param.14), channel_id=1, source_target_pairs={{0,2},{1,3},{2,0},{3,1},{4,6},{5,7},{6,4},{7,5},{8,10},{9,11},{10,... | collective-permute-start | bytes 393224 | tf_op jit(solution)/shard_map/ppermute | solution.py:117
  4.9 16.5 %collective-permute-start.2 = (bf16[64,1024]{1,0:T(8,128)(2,1)}, bf16[64,1024]{1,0:T(8,128)(2,1)}, u32[]{:S(2)}, u32[]{:S(2)}) collective-permute-start(bf16[64,1024]{1,0:T(8,128)(2,1)} %param.14), channel_id=1, source_target_pairs={{0,3},{1,0},{2,1},{3,2},{4,7},{5,4},{6,5},{7,6},{8,11},{9,8},{10,9... | collective-permute-start | bytes 393224 | tf_op jit(solution)/shard_map/ppermute | solution.py:117
  10.0 6.6 %copy-start.3 = (bf16[64,1024]{1,0:T(8,128)(2,1)S(1)}, bf16[64,1024]{1,0:T(8,128)(2,1)}, u32[]{:S(2)}) copy-start(bf16[64,1024]{1,0:T(8,128)(2,1)} %param.15) | copy-start | bytes 393220
  18.8 3.9 %copy-start.4 = (s32[32,5]{0,1:T(8,128)}, s32[32,5]{0,1:T(8,128)S(1)}, u32[]{:S(2)}) copy-start(s32[32,5]{0,1:T(8,128)S(1)} %reduce-window.9) | copy-start | bytes 1924
  21.4 2.2 %copy-start.1 = (bf16[576,512]{0,1:T(8,128)(2,1)S(1)}, bf16[576,512]{0,1:T(8,128)(2,1)}, u32[]{:S(2)}) copy-start(bf16[576,512]{0,1:T(8,128)(2,1)} %get-tuple-element.10) | copy-start | bytes 1769476
  41.7 2.8 %copy-start.2 = (f32[256,16]{1,0:T(8,128)S(1)}, f32[256,16]{1,0:T(8,128)}, u32[]{:S(2)}) copy-start(f32[256,16]{1,0:T(8,128)} %copy.55) | copy-start | bytes 49156
  44.4 4.2 %slice-start = ((s32[32,5]{0,1:T(8,128)}), s32[32,4]{0,1:T(4,128)S(1)}, s32[]{:S(2)}) async-start(s32[32,5]{0,1:T(8,128)} %copy-done.4), calls=%async_computation.2 | async-start | bytes 4096 | tf_op jit(solution)/shard_map/slice.1
  45.9 10.0 %collective-permute-start.3 = (f32[64,1152]{1,0:T(8,128)S(1)}, f32[64,1152]{1,0:T(8,128)S(1)}, u32[]{:S(2)}, u32[]{:S(2)}) collective-permute-start(f32[64,1152]{1,0:T(8,128)S(1)} %get-tuple-element.15), channel_id=1, source_target_pairs={{0,3},{1,0},{2,1},{3,2},{4,7},{5,4},{6,5},{7,6},{8,11},{9,8},{10,9... | collective-permute-start | bytes 884744 | tf_op jit(solution)/shard_map/ppermute | solution.py:163
  46.0 11.5 %collective-permute-start.4 = (f32[64,1152]{1,0:T(8,128)S(1)}, f32[64,1152]{1,0:T(8,128)S(1)}, u32[]{:S(2)}, u32[]{:S(2)}) collective-permute-start(f32[64,1152]{1,0:T(8,128)S(1)} %get-tuple-element.14), channel_id=1, source_target_pairs={{0,2},{1,3},{2,0},{3,1},{4,6},{5,7},{6,4},{7,5},{8,10},{9,11},{10,... | collective-permute-start | bytes 884744 | tf_op jit(solution)/shard_map/ppermute | solution.py:163
  48.7 13.2 %collective-permute-start.5 = (f32[64,1152]{1,0:T(8,128)S(1)}, f32[64,1152]{1,0:T(8,128)S(1)}, u32[]{:S(2)}, u32[]{:S(2)}) collective-permute-start(f32[64,1152]{1,0:T(8,128)S(1)} %get-tuple-element.13), channel_id=1, source_target_pairs={{0,1},{1,2},{2,3},{3,0},{4,5},{5,6},{6,7},{7,4},{8,9},{9,10},{10,1... | collective-permute-start | bytes 884744 | tf_op jit(solution)/shard_map/ppermute | solution.py:163
  68.8 2.6 %copy-start.5 = (f32[1024]{0:T(1024)S(1)}, f32[1024]{0:T(1024)}, u32[]{:S(2)}) copy-start(f32[1024]{0:T(1024)} %param.21) | copy-start | bytes 12292
  75.6 12.6 %copy-start.7 = (bf16[1,256,1024]{2,1,0:T(8,128)(2,1)S(1)}, bf16[1,256,1024]{2,1,0:T(8,128)(2,1)}, u32[]{:S(2)}) copy-start(bf16[1,256,1024]{2,1,0:T(8,128)(2,1)} %param.23) | copy-start | bytes 1572868
  75.6 63.6 %all-to-all-start = ((bf16[64,16,1024]{2,1,0:T(8,128)(2,1)}), bf16[64,16,1024]{2,1,0:T(8,128)(2,1)}, u32[]{:S(2)}, u32[]{:S(2)}) async-start(bf16[64,16,1024]{2,1,0:T(8,128)(2,1)} %bitcast.109), calls=%async_computation | async-start | bytes 4194304 | tf_op jit(solution)/shard_map/all_to_all | solution.py:38
  88.0 55.1 %collective-permute-start.6 = (bf16[1,1024,512]{2,1,0:T(8,128)(2,1)}, bf16[1,1024,512]{2,1,0:T(8,128)(2,1)}, u32[]{:S(2)}, u32[]{:S(2)}) collective-permute-start(bf16[1,1024,512]{2,1,0:T(8,128)(2,1)} %param.22), channel_id=1, source_target_pairs={{0,4},{4,0},{8,12},{12,8},{16,20},{20,16},{24,28},{28,24},{32,36},... | collective-permute-start | bytes 3145736 | tf_op jit(solution)/shard_map/ppermute | solution.py:69
  88.2 58.0 %collective-permute-start.7 = (bf16[1,256,1024]{2,1,0:T(8,128)(2,1)S(1)}, bf16[1,256,1024]{2,1,0:T(8,128)(2,1)}, u32[]{:S(2)}, u32[]{:S(2)}) collective-permute-start(bf16[1,256,1024]{2,1,0:T(8,128)(2,1)S(1)} %copy-done.7), channel_id=1, source_target_pairs={{0,4},{4,0},{8,12},{12,8},{16,20},{20,16},{24,28},{28,24},{32,36},... | collective-permute-start | bytes 1572872 | tf_op jit(solution)/shard_map/ppermute | solution.py:70
  149.5 5.8 %copy-start.6 = (f32[64,8]{0,1:T(8,128)S(1)}, f32[64,8]{0,1:T(8,128)}, u32[]{:S(2)}) copy-start(f32[64,8]{0,1:T(8,128)} %param.25) | copy-start | bytes 6148
  149.5 56.9 %all-to-all-start.1 = ((bf16[64,16,1024]{2,1,0:T(8,128)(2,1)}), bf16[64,16,1024]{2,1,0:T(8,128)(2,1)}, u32[]{:S(2)}, u32[]{:S(2)}) async-start(bf16[64,16,1024]{2,1,0:T(8,128)(2,1)} %bitcast.120), calls=%async_computation.1 | async-start | bytes 4194304 | tf_op jit(solution)/shard_map/all_to_all | solution.py:40

commit v4 on v2

--- a/solution.py
+++ b/solution.py
@@ -63,7 +63,6 @@
     route_weight,
 ):
     tokens_per_device = stream.shape[0]
-    width = stream.shape[1]
     tok_size = lax.axis_size("tok")
     sibling = [(t, t ^ 1) for t in range(tok_size)]
     sibling_gate_up = lax.ppermute(expert_gate_up, "tok", sibling)
@@ -78,7 +77,6 @@
     list_len = table.shape[0]
     pool_blocks = cache_block_pool.shape[0]
     block_len = cache_block_pool.shape[1]
-    group_tokens = segments.shape[0]
     request_range = jnp.arange(lengths.shape[0], dtype=jnp.int32)
     row_len = jnp.sum(
         jnp.where(segments[:, None] == request_range[None, :], lengths[None, :], 0), axis=1
@@ -98,56 +96,86 @@
     offsets = jnp.arange(block_len, dtype=jnp.int32)
     cache_pos = (slot_block[:, None] * block_len + offsets[None, :]).reshape(-1)
     cache_listed = jnp.repeat(slot_block >= 0, block_len)
-    cache_visible = cache_listed[None, :] & (cache_pos[None, :] < row_len[:, None])
-    query_order = jnp.arange(group_tokens, dtype=jnp.int32)
+    shifts = range(pool_size)
     fresh_order = pool_idx * tokens_per_device + jnp.arange(tokens_per_device, dtype=jnp.int32)
     fresh_seg = lax.dynamic_slice_in_dim(segments, pool_idx * tokens_per_device, tokens_per_device)
-    fresh_visible = (fresh_seg[None, :] == segments[:, None]) & (
-        fresh_order[None, :] <= query_order[:, None]
-    )
-    visible = jnp.concatenate([cache_visible, fresh_visible], axis=1)
-    group_queries = lax.all_gather(queries, "pool", axis=0, tiled=True)
     key_value_pairs = jnp.concatenate(
         [cache_block_pool.reshape(pool_blocks * block_len, 2 * kv_width), fresh_kv], axis=0
     )
     key_count = key_value_pairs.shape[0]
-    query_row_block = group_queries.reshape(
-        group_tokens, KEY_VALUE_HEADS, heads_per_group, HEAD_SIZE
-    )
     key_row_block = key_value_pairs[:, :kv_width].reshape(key_count, KEY_VALUE_HEADS, HEAD_SIZE)
     value_row_block = key_value_pairs[:, kv_width:].reshape(key_count, KEY_VALUE_HEADS, HEAD_SIZE)
-    scores = (
-        jnp.einsum(
-            "qhgd,khd->qhgk",
-            query_row_block,
-            key_row_block,
+    stat_pad = 128 - 2 * QUERY_HEADS
+
+    def attend_block(query_block, source):
+        first = source * tokens_per_device
+        query_order = first + jnp.arange(tokens_per_device, dtype=jnp.int32)
+        query_seg = lax.dynamic_slice_in_dim(segments, first, tokens_per_device)
+        query_len = lax.dynamic_slice_in_dim(row_len, first, tokens_per_device)
+        cache_visible = cache_listed[None, :] & (cache_pos[None, :] < query_len[:, None])
+        fresh_visible = (fresh_seg[None, :] == query_seg[:, None]) & (
+            fresh_order[None, :] <= query_order[:, None]
+        )
+        visible = jnp.concatenate([cache_visible, fresh_visible], axis=1)
+        query_row_block = query_block.reshape(
+            tokens_per_device, KEY_VALUE_HEADS, heads_per_group, HEAD_SIZE
+        )
+        scores = (
+            jnp.einsum(
+                "qhgd,khd->qhgk",
+                query_row_block,
+                key_row_block,
+                preferred_element_type=jnp.float32,
+            )
+            * score_scale
+        )
+        shown_keys = visible[:, None, None, :]
+        scores = jnp.where(shown_keys, scores, masked_filler)
+        highest = jnp.max(scores, axis=-1)
+        weights = jnp.where(shown_keys, jnp.exp(scores - highest[..., None]), 0.0)
+        denominator = jnp.sum(weights, axis=-1)
+        summed = jnp.einsum(
+            "qhgk,khd->qhgd",
+            weights.astype(jnp.bfloat16),
+            value_row_block,
             preferred_element_type=jnp.float32,
         )
-        * score_scale
-    )
-    shown_keys = visible[:, None, None, :]
-    scores = jnp.where(shown_keys, scores, masked_filler)
-    highest = jnp.max(scores, axis=-1)
-    weights = jnp.where(shown_keys, jnp.exp(scores - highest[..., None]), 0.0)
-    denominator = jnp.sum(weights, axis=-1)
-    summed = jnp.einsum(
-        "qhgk,khd->qhgd",
-        weights.astype(jnp.bfloat16),
-        value_row_block,
-        preferred_element_type=jnp.float32,
-    )
-    partial = jnp.concatenate(
-        [summed, highest[..., None], denominator[..., None]], axis=-1
-    ).reshape(pool_size, tokens_per_device, -1)
-    gathered = lax.all_to_all(partial, "pool", split_axis=0, concat_axis=0, tiled=True).reshape(
-        pool_size, tokens_per_device, KEY_VALUE_HEADS, heads_per_group, HEAD_SIZE + 2
-    )
-    part_max = gathered[..., HEAD_SIZE]
+        return jnp.concatenate(
+            [
+                summed.reshape(tokens_per_device, QUERY_HEADS * HEAD_SIZE),
+                highest.reshape(tokens_per_device, QUERY_HEADS),
+                denominator.reshape(tokens_per_device, QUERY_HEADS),
+                jnp.zeros((tokens_per_device, stat_pad), jnp.float32),
+            ],
+            axis=1,
+        )
+
+    query_blocks = [queries] + [
+        lax.ppermute(
+            queries, "pool", [(i, (i + shift) % pool_size) for i in range(pool_size)]
+        )
+        for shift in shifts[1:]
+    ]
+    partials = [None] * pool_size
+    for shift in list(shifts[1:]) + [0]:
+        partial = attend_block(query_blocks[shift], (pool_idx - shift) % pool_size)
+        if shift:
+            partial = lax.ppermute(
+                partial, "pool", [(i, (i - shift) % pool_size) for i in range(pool_size)]
+            )
+        partials[shift] = partial
+    gathered = jnp.stack(partials)
+    acc_width = QUERY_HEADS * HEAD_SIZE
+    part_max = gathered[:, :, acc_width : acc_width + QUERY_HEADS]
+    part_sum = gathered[:, :, acc_width + QUERY_HEADS : acc_width + 2 * QUERY_HEADS]
     running = jnp.max(part_max, axis=0)
     rescale = jnp.exp(part_max - running[None])
-    denominator = jnp.sum(gathered[..., HEAD_SIZE + 1] * rescale, axis=0)
-    summed = jnp.sum(gathered[..., :HEAD_SIZE] * rescale[..., None], axis=0)
-    context = summed / denominator[..., None]
+    denominator = jnp.sum(part_sum * rescale, axis=0)
+    summed = jnp.sum(
+        gathered[:, :, :acc_width] * jnp.repeat(rescale, HEAD_SIZE, axis=2), axis=0
+    )
+    denominator = jnp.repeat(denominator, HEAD_SIZE, axis=1)
+    context = summed / denominator
     attended = context.reshape(tokens_per_device, QUERY_HEADS * HEAD_SIZE).astype(jnp.bfloat16)
     residual = stream.astype(jnp.float32) + jnp.dot(
         attended, output_weight, preferred_element_type=jnp.float32
@@ -161,11 +189,11 @@
     earlier = jnp.cumsum(onehot, axis=0) - onehot
     slot_of = jnp.sum(earlier * onehot, axis=1)
     destination = flat_routes * CAP + slot_of
-    send_rows = (
-        jnp.zeros((EXPERTS * CAP, width), jnp.bfloat16)
-        .at[destination]
-        .set(jnp.repeat(normed, TOPK, axis=0))
-    )
+    slot_range = jnp.arange(EXPERTS * CAP, dtype=jnp.int32)
+    placed = destination.reshape(tokens_per_device, TOPK)[None, :, :] == slot_range[:, None, None]
+    send_rows = jnp.dot(
+        jnp.any(placed, axis=2).astype(jnp.bfloat16), normed, preferred_element_type=jnp.float32
+    ).astype(jnp.bfloat16)
     split = FF // (expert_gate_up.shape[2] // 2)
     expert_rows = direct_dispatch(
         send_rows,
@@ -173,8 +201,13 @@
         jnp.concatenate([expert_gate_up, sibling_gate_up], axis=0),
         jnp.concatenate([expert_down, sibling_down], axis=0),
     )
-    picked = expert_rows[destination].reshape(tokens_per_device, TOPK, width)
-    experts_sum = jnp.einsum("tkd,tk->td", picked.astype(jnp.float32), route_weight)
+    mixing = jnp.sum(jnp.where(placed, route_weight[None, :, :], 0.0), axis=2).T
+    experts_sum = jnp.dot(
+        mixing,
+        expert_rows.astype(jnp.float32),
+        precision=lax.Precision.HIGHEST,
+        preferred_element_type=jnp.float32,
+    )
     layer_out = (residual + experts_sum).astype(jnp.bfloat16)
     return (attended, layer_out)
 

time: 221 us -> 204 us (0.923)
  blocking collectives: 14.8 us -> 0 us
  matrix products: 15.9 us -> 28.1 us
  waiting for transfers between devices: 113 us -> 101 us
  starting transfers between devices: 22.5 us -> 28.3 us
  local copies, waits for them, and re-layouts: 31.8 us -> 27.6 us
  other arithmetic: 20.4 us -> 17.3 us
    all_gather x1 -> x0, blocking collectives: 14.8 us -> none  [body(): group_queries = lax.all_gather(queries, 'pool', axis=0, tiled=True)]
    dot_general x3 -> x10, matrix products: 4.37 us -> 16.3 us  [the longest x4 7.37 us: attend_block(): jnp.einsum('qhgk,khd->qhgd', weights.astype(jnp.bfloat16), value_row_bloc...]
    all_to_all x1 -> x0, waiting for transfers between devices: 11.9 us -> none  [body(): lax.all_to_all(partial, 'pool', split_axis=0, concat_axis=0, tiled=True)]
    ppermute x0 -> x6, starting transfers between devices: none -> 9.49 us  [the longest x3 5.13 us: body(): lax.ppermute(queries, 'pool', [(i, (i + shift) % pool_size) for i in rang...]
    slice x1 -> x0, other arithmetic: 8.08 us -> none  [body(): denominator = jnp.sum(gathered[..., HEAD_SIZE + 1] * rescale, axis=0)]
    gather x1 -> x0, local copies, waits for them, and re-layouts: 4.59 us -> none  [body(): picked = expert_rows[destination].reshape(tokens_per_device, TOPK, width)]
    scatter x1 -> x0, local copies, waits for them, and re-layouts: 4.1 us -> none  [body(): send_rows = jnp.zeros((EXPERTS * CAP, width), jnp.bfloat16).at[destinatio...]
    all_to_all x1 -> x0, starting transfers between devices: 3.71 us -> none  [body(): lax.all_to_all(partial, 'pool', split_axis=0, concat_axis=0, tiled=True)]
  transfers between devices with their start and end apart: 5 -> 10, of which waited for: 3 -> 3; matrix products, arithmetic and copies ran while one was open for 4% -> 23% of each run, Pallas kernels for 0% -> 0%
where the time goes in v4:
time: 204 us; the launch traced here: 203 us
  waiting for transfers between devices  101 us (50%)
  starting transfers between devices  28.3 us (14%)
  matrix products  28.1 us (14%)
  local copies, waits for them, and re-layouts  27.6 us (14%)
  other arithmetic  17.3 us (8%)
    all_to_all x1, waiting for transfers between devices, direct_dispatch(): lax.all_to_all(unit_rows, 'tok', split_axis=0, concat_axis=0, tiled=True)  50.6 us
    all_to_all x1, waiting for transfers between devices, direct_dispatch(): lax.all_to_all(produced.reshape(EXPERTS * split, CAP // split, width), 't...  49.5 us
    all_to_all x1, starting transfers between devices, direct_dispatch(): lax.all_to_all(unit_rows, 'tok', split_axis=0, concat_axis=0, tiled=True)  12.4 us
    dot_general x4, matrix products, attend_block(): jnp.einsum('qhgk,khd->qhgd', weights.astype(jnp.bfloat16), value_row_bloc...  7.37 us
    dot_general x2, matrix products, pair_ffn(): jnp.dot(rows_in, gate_up_pair[part], preferred_element_type=jnp.float32)  6.2 us
    reduce_sum x4, other arithmetic, attend_block(): denominator = jnp.sum(weights, axis=-1)  5.89 us
    all_to_all x1, starting transfers between devices, direct_dispatch(): lax.all_to_all(produced.reshape(EXPERTS * split, CAP // split, width), 't...  5.73 us
    ppermute x3, starting transfers between devices, body(): lax.ppermute(queries, 'pool', [(i, (i + shift) % pool_size) for i in rang...  5.13 us
  transfers between devices with their start and end apart: 10, of which 3 were waited for; matrix products, arithmetic and copies ran while one was open for 23% of the time, Pallas kernels for 0%

profile of v4, /device:TPU:8, one launch (start us, length us, event | category | flops | bytes accessed | tf_op | source)
XLA Modules:
  0.0 203.0 jit_solution(17534218117299052972)
XLA Ops:
  0.6 1.6 collective-permute-start
  2.2 1.7 collective-permute-start.4
  4.0 1.8 collective-permute-start.2
  13.3 2.3 %copy.109 = bf16[512,1024]{0,1:T(8,128)(2,1)} copy(bf16[512,1024]{1,0:T(8,128)(2,1)} %bitcast.166) | data formatting | bytes 2097152 | tf_op jit(solution)/shard_map/reshape | solution.py:103
  15.9 1.3 pad_maximum_fusion.1
  17.9 1.5 fusion.5
  19.4 1.8 fusion.19
  24.9 1.8 fusion.13
  26.8 1.5 fusion.11
  29.5 1.9 fusion.15
  31.4 1.5 fusion.9
  34.1 1.5 fusion.1
  35.6 1.5 fusion.7
  37.1 1.8 fusion.17
  41.8 2.0 collective-permute-start.3
  43.9 1.2 copy.116
  47.4 1.7 collective-permute-start.1
  52.5 1.4 copy.114
  54.8 2.1 %fusion.4 = pred[1024,64]{0,1:T(8,128)(4,1)} fusion(s32[64,8]{1,0:T(8,128)} %copy.133), kind=kLoop, calls=%fused_computation.15 | loop fusion | flops 983040 | bytes 67584 | tf_op jit(solution)/shard_map/reduce_or | solution.py:195
  58.8 2.0 broadcast_in_dim.146
  60.7 2.8 %reshape.209 = f32[4,64,1024]{2,1,0:T(8,128)} reshape(f32[4,64,16,64]{3,2,1,0:T(8,128)} %broadcast_in_dim.146) | data formatting | bytes 2097152 | tf_op jit(solution)/shard_map/reshape | solution.py:175
  63.5 1.4 fusion.28
  65.2 1.5 multiply_reduce_fusion
  66.7 2.1 %convolution_convert_fusion = bf16[1024,1024]{1,0:T(8,128)(2,1)} fusion(pred[1024,64]{0,1:T(8,128)(4,1)S(1)} %copy-done.12, f32[64,1024]{1,0:T(8,128)S(1)} %get-tuple-element.42, f32[1024]{0:T(1024)S(1)} %copy-done.19, f32[64]{0:T(128)S(1)} %add_rsqrt_fusion), kind=kOutput, calls=%fused_computation.16 | convolution fusion | flops 135462912 | bytes 2429184 | tf_op jit(solution)/shard_map/dot_general | solution.py:194
  68.8 12.4 %all-to-all-start = ((bf16[64,16,1024]{2,1,0:T(8,128)(2,1)}), bf16[64,16,1024]{2,1,0:T(8,128)(2,1)}, u32[]{:S(2)}, u32[]{:S(2)}) async-start(bf16[64,16,1024]{2,1,0:T(8,128)(2,1)} %bitcast.152), calls=%async_computation | async-start | bytes 4194304 | tf_op jit(solution)/shard_map/all_to_all | solution.py:38
  81.8 50.6 %all-to-all-done = bf16[64,16,1024]{2,1,0:T(8,128)(2,1)} async-done(((bf16[64,16,1024]{2,1,0:T(8,128)(2,1)}), bf16[64,16,1024]{2,1,0:T(8,128)(2,1)}, u32[]{:S(2)}, u32[]{:S(2)}) %all-to-all-start) | async-done | bytes 2097184 | tf_op jit(solution)/shard_map/all_to_all | solution.py:38
  132.4 3.1 %fusion.31 = f32[1024,512]{1,0:T(8,128)S(1)} fusion(bf16[1024,1024]{1,0:T(8,128)(2,1)} %bitcast.46, bf16[1,1024,512]{2,1,0:T(8,128)(2,1)} %param.22), kind=kOutput, calls=%fused_computation.47 | convolution fusion | flops 1073741824 | bytes 5242880 | tf_op jit(solution)/shard_map/dot_general | solution.py:23
  136.3 3.1 %fusion.29 = f32[1024,512]{1,0:T(8,128)S(1)} fusion(bf16[1024,1024]{1,0:T(8,128)(2,1)} %bitcast.46, bf16[1,1024,512]{2,1,0:T(8,128)(2,1)} %collective-permute-done.6), kind=kOutput, calls=%fused_computation.45 | convolution fusion | flops 1073741824 | bytes 5242880 | tf_op jit(solution)/shard_map/dot_general | solution.py:23
  139.4 3.2 %add_convert_fusion = bf16[1024,1024]{1,0:T(8,128)(2,1)} fusion(bf16[1024,1024]{1,0:T(8,128)(2,1)S(1)} %fusion.34, f32[1024,512]{1,0:T(8,128)S(1)} %fusion.29, bf16[1,256,1024]{2,1,0:T(8,128)(2,1)} %collective-permute-done.7), kind=kOutput, calls=%fused_computation | convolution fusion | flops 543686656 | bytes 6815744 | tf_op jit(solution)/shard_map/dot_general | solution.py:27
  142.7 5.7 %all-to-all-start.1 = ((bf16[64,16,1024]{2,1,0:T(8,128)(2,1)}), bf16[64,16,1024]{2,1,0:T(8,128)(2,1)}, u32[]{:S(2)}, u32[]{:S(2)}) async-start(bf16[64,16,1024]{2,1,0:T(8,128)(2,1)} %bitcast.165), calls=%async_computation.1 | async-start | bytes 4194304 | tf_op jit(solution)/shard_map/all_to_all | solution.py:40
  150.0 49.5 %all-to-all-done.1 = bf16[64,16,1024]{2,1,0:T(8,128)(2,1)} async-done(((bf16[64,16,1024]{2,1,0:T(8,128)(2,1)}), bf16[64,16,1024]{2,1,0:T(8,128)(2,1)}, u32[]{:S(2)}, u32[]{:S(2)}) %all-to-all-start.1) | async-done | bytes 2097184 | tf_op jit(solution)/shard_map/all_to_all | solution.py:40
  199.6 3.5 %fusion.25 = bf16[64,1024]{1,0:T(8,128)(2,1)} fusion(f32[64,1024]{1,0:T(8,128)S(1)} %get-tuple-element.42, f32[1024,64]{0,1:T(8,128)S(1)} %select_reduce_fusion, bf16[1024,1024]{1,0:T(8,128)(2,1)} %bitcast.52), kind=kOutput, calls=%fused_computation.38 | convolution fusion | flops 805437440 | bytes 2752512 | tf_op jit(solution)/shard_map/dot_general | solution.py:205
  (124 shorter events, 29.1 us)
Async XLA Ops:
  0.6 64.5 %copy-start = (bf16[1024,1024]{1,0:T(8,128)(2,1)S(1)}, bf16[1024,1024]{1,0:T(8,128)(2,1)}, u32[]{:S(2)}) copy-start(bf16[1024,1024]{1,0:T(8,128)(2,1)} %param.20) | copy-start | bytes 6291460
  0.6 32.3 %collective-permute-start = (bf16[64,1024]{1,0:T(8,128)(2,1)}, bf16[64,1024]{1,0:T(8,128)(2,1)}, u32[]{:S(2)}, u32[]{:S(2)}) collective-permute-start(bf16[64,1024]{1,0:T(8,128)(2,1)} %param.14), channel_id=1, source_target_pairs={{0,1},{1,2},{2,3},{3,0},{4,5},{5,6},{6,7},{7,4},{8,9},{9,10},{10,1... | collective-permute-start | bytes 393224 | tf_op jit(solution)/shard_map/ppermute | solution.py:154
  2.2 20.5 %collective-permute-start.4 = (bf16[64,1024]{1,0:T(8,128)(2,1)}, bf16[64,1024]{1,0:T(8,128)(2,1)}, u32[]{:S(2)}, u32[]{:S(2)}) collective-permute-start(bf16[64,1024]{1,0:T(8,128)(2,1)} %param.14), channel_id=1, source_target_pairs={{0,3},{1,0},{2,1},{3,2},{4,7},{5,4},{6,5},{7,6},{8,11},{9,8},{10,9... | collective-permute-start | bytes 393224 | tf_op jit(solution)/shard_map/ppermute | solution.py:154
  4.0 24.3 %collective-permute-start.2 = (bf16[64,1024]{1,0:T(8,128)(2,1)}, bf16[64,1024]{1,0:T(8,128)(2,1)S(1)}, u32[]{:S(2)}, u32[]{:S(2)}) collective-permute-start(bf16[64,1024]{1,0:T(8,128)(2,1)} %param.14), channel_id=1, source_target_pairs={{0,2},{1,3},{2,0},{3,1},{4,6},{5,7},{6,4},{7,5},{8,10},{9,11},{10,... | collective-permute-start | bytes 393224 | tf_op jit(solution)/shard_map/ppermute | solution.py:154
  12.2 5.0 %copy-start.18 = (s32[32,5]{0,1:T(8,128)}, s32[32,5]{0,1:T(8,128)S(1)}, u32[]{:S(2)}) copy-start(s32[32,5]{0,1:T(8,128)S(1)} %reduce-window.9) | copy-start | bytes 1924
  17.2 2.1 %copy-start.3 = (bf16[576,512]{0,1:T(8,128)(2,1)}, bf16[576,512]{0,1:T(8,128)(2,1)S(1)}, u32[]{:S(2)}) copy-start(bf16[576,512]{0,1:T(8,128)(2,1)S(1)} %get-tuple-element.13) | copy-start | bytes 1769476
  19.4 1.8 slice-start
  21.9 6.5 %copy-start.9 = (pred[64,576]{1,0:T(8,128)(4,1)}, pred[64,576]{1,0:T(8,128)(4,1)S(1)}, u32[]{:S(2)}) copy-start(pred[64,576]{1,0:T(8,128)(4,1)S(1)} %pad_add_fusion.2) | copy-start | bytes 110596
  23.8 1.1 copy-start.4
  24.5 2.3 %copy-start.14 = (f32[64,8,2]{0,2,1:T(2,128)}, f32[64,8,2]{0,2,1:T(2,128)S(1)}, u32[]{:S(2)}) copy-start(f32[64,8,2]{0,2,1:T(2,128)S(1)} %get-tuple-element.33) | copy-start | bytes 12292
  29.5 1.9 copy-start.10
  34.0 1.5 copy-start.8
  34.0 3.0 %copy-start.6 = (bf16[576,512]{0,1:T(8,128)(2,1)S(1)}, bf16[576,512]{0,1:T(8,128)(2,1)}, u32[]{:S(2)}) copy-start(bf16[576,512]{0,1:T(8,128)(2,1)} %copy-done.3) | copy-start | bytes 1769476
  35.5 3.3 %copy-start.13 = (f32[64,8,2]{0,2,1:T(2,128)}, f32[64,8,2]{0,2,1:T(2,128)S(1)}, u32[]{:S(2)}) copy-start(f32[64,8,2]{0,2,1:T(2,128)S(1)} %get-tuple-element.37) | copy-start | bytes 12292
  37.0 1.9 copy-start.7
  37.0 2.0 %copy-start.17 = (f32[64,8,2]{0,2,1:T(2,128)S(1)}, f32[64,8,2]{0,2,1:T(2,128)}, u32[]{:S(2)}) copy-start(f32[64,8,2]{0,2,1:T(2,128)} %fusion.11) | copy-start | bytes 12292
  37.0 2.1 %copy-start.15 = (f32[64,8,2]{0,2,1:T(2,128)S(1)}, f32[64,8,2]{0,2,1:T(2,128)}, u32[]{:S(2)}) copy-start(f32[64,8,2]{0,2,1:T(2,128)} %copy-done.14) | copy-start | bytes 12292
  37.1 3.8 %copy-start.16 = (f32[64,8,2]{0,2,1:T(2,128)S(1)}, f32[64,8,2]{0,2,1:T(2,128)}, u32[]{:S(2)}) copy-start(f32[64,8,2]{0,2,1:T(2,128)} %fusion.9) | copy-start | bytes 12292
  39.3 13.2 %copy-start.2 = (f32[64,96]{1,0:T(8,128)}, f32[64,96]{1,0:T(8,128)S(1)}, u32[]{:S(2)}) copy-start(f32[64,96]{1,0:T(8,128)S(1)} %broadcast.121) | copy-start | bytes 73732
  40.1 16.8 %collective-permute-start.5 = (f32[64,1152]{1,0:T(8,128)}, f32[64,1152]{1,0:T(8,128)S(1)}, u32[]{:S(2)}, u32[]{:S(2)}) collective-permute-start(f32[64,1152]{1,0:T(8,128)} %concatenate.35), channel_id=1, source_target_pairs={{0,1},{1,2},{2,3},{3,0},{4,5},{5,6},{6,7},{7,4},{8,9},{9,10},{10,1... | collective-permute-start | bytes 884744 | tf_op jit(solution)/shard_map/ppermute | solution.py:163
  41.8 15.0 %collective-permute-start.3 = (f32[64,1152]{1,0:T(8,128)}, f32[64,1152]{1,0:T(8,128)S(1)}, u32[]{:S(2)}, u32[]{:S(2)}) collective-permute-start(f32[64,1152]{1,0:T(8,128)} %concatenate.33), channel_id=1, source_target_pairs={{0,2},{1,3},{2,0},{3,1},{4,6},{5,7},{6,4},{7,5},{8,10},{9,11},{10,... | collective-permute-start | bytes 884744 | tf_op jit(solution)/shard_map/ppermute | solution.py:163
  47.4 10.0 %collective-permute-start.1 = (f32[64,1152]{1,0:T(8,128)}, f32[64,1152]{1,0:T(8,128)S(1)}, u32[]{:S(2)}, u32[]{:S(2)}) collective-permute-start(f32[64,1152]{1,0:T(8,128)} %concatenate.31), channel_id=1, source_target_pairs={{0,3},{1,0},{2,1},{3,2},{4,7},{5,4},{6,5},{7,6},{8,11},{9,8},{10,9... | collective-permute-start | bytes 884744 | tf_op jit(solution)/shard_map/ppermute | solution.py:163
  58.8 4.7 %copy-start.1 = (f32[4,64,1152]{2,1,0:T(8,128)S(1)}, f32[4,64,1152]{2,1,0:T(8,128)}, u32[]{:S(2)}) copy-start(f32[4,64,1152]{2,1,0:T(8,128)} %pad_maximum_fusion) | copy-start | bytes 3538948
  64.9 1.8 copy-start.12
  64.9 1.8 copy-start.19
  68.8 12.7 %copy-start.21 = (bf16[1,256,1024]{2,1,0:T(8,128)(2,1)S(1)}, bf16[1,256,1024]{2,1,0:T(8,128)(2,1)}, u32[]{:S(2)}) copy-start(bf16[1,256,1024]{2,1,0:T(8,128)(2,1)} %param.23) | copy-start | bytes 1572868
  68.8 63.6 %all-to-all-start = ((bf16[64,16,1024]{2,1,0:T(8,128)(2,1)}), bf16[64,16,1024]{2,1,0:T(8,128)(2,1)}, u32[]{:S(2)}, u32[]{:S(2)}) async-start(bf16[64,16,1024]{2,1,0:T(8,128)(2,1)} %bitcast.152), calls=%async_computation | async-start | bytes 4194304 | tf_op jit(solution)/shard_map/all_to_all | solution.py:38
  81.2 55.0 %collective-permute-start.6 = (bf16[1,1024,512]{2,1,0:T(8,128)(2,1)}, bf16[1,1024,512]{2,1,0:T(8,128)(2,1)}, u32[]{:S(2)}, u32[]{:S(2)}) collective-permute-start(bf16[1,1024,512]{2,1,0:T(8,128)(2,1)} %param.22), channel_id=1, source_target_pairs={{0,4},{4,0},{8,12},{12,8},{16,20},{20,16},{24,28},{28,24},{32,36},... | collective-permute-start | bytes 3145736 | tf_op jit(solution)/shard_map/ppermute | solution.py:68
  81.5 58.0 %collective-permute-start.7 = (bf16[1,256,1024]{2,1,0:T(8,128)(2,1)S(1)}, bf16[1,256,1024]{2,1,0:T(8,128)(2,1)}, u32[]{:S(2)}, u32[]{:S(2)}) collective-permute-start(bf16[1,256,1024]{2,1,0:T(8,128)(2,1)S(1)} %copy-done.21), channel_id=1, source_target_pairs={{0,4},{4,0},{8,12},{12,8},{16,20},{20,16},{24,28},{28,24},{32,36},... | collective-permute-start | bytes 1572872 | tf_op jit(solution)/shard_map/ppermute | solution.py:69
  142.7 5.7 %copy-start.20 = (f32[64,8]{0,1:T(8,128)S(1)}, f32[64,8]{0,1:T(8,128)}, u32[]{:S(2)}) copy-start(f32[64,8]{0,1:T(8,128)} %param.25) | copy-start | bytes 6148
  142.7 5.8 %copy-start.11 = (s32[64,8]{1,0:T(8,128)S(1)}, s32[64,8]{1,0:T(8,128)}, u32[]{:S(2)}) copy-start(s32[64,8]{1,0:T(8,128)} %copy.133) | copy-start | bytes 6148
  142.7 56.9 %all-to-all-start.1 = ((bf16[64,16,1024]{2,1,0:T(8,128)(2,1)}), bf16[64,16,1024]{2,1,0:T(8,128)(2,1)}, u32[]{:S(2)}, u32[]{:S(2)}) async-start(bf16[64,16,1024]{2,1,0:T(8,128)(2,1)} %bitcast.165), calls=%async_computation.1 | async-start | bytes 4194304 | tf_op jit(solution)/shard_map/all_to_all | solution.py:40
  (1 other events, 1.1 us)

commit v5 on v4

--- a/solution.py
+++ b/solution.py
@@ -1,6 +1,8 @@
 import jax
 import jax.numpy as jnp
 from jax import lax
+from jax.experimental import pallas as pl
+from jax.experimental.pallas import tpu as pltpu
 from jax.sharding import PartitionSpec as P
 
 QUERY_HEADS = 16
@@ -14,6 +16,51 @@
 
 score_scale = 0.015625
 masked_filler = -1e30
+
+
+def _attend_kernel(q_ref, kv_ref, mask_ref, out_ref):
+    rows = q_ref.shape[0]
+    visible = mask_ref[...] > 0.5
+    lane = lax.broadcasted_iota(jnp.int32, (rows, 128), 1)
+    low_half = lane < HEAD_SIZE
+    stats = jnp.zeros((rows, 128), jnp.float32)
+    for h in range(KEY_VALUE_HEADS):
+        q_tile = q_ref[:, h * 128:(h + 1) * 128].astype(jnp.float32)
+        k_tile = kv_ref[:, (h // 2) * 128:(h // 2 + 1) * 128]
+        v_tile = kv_ref[:, KEY_VALUE_HEADS * HEAD_SIZE + (h // 2) * 128:KEY_VALUE_HEADS * HEAD_SIZE + (h // 2 + 1) * 128]
+        out_tile = jnp.zeros((rows, 128), jnp.float32)
+        for g in range(2):
+            j = 2 * h + g
+            q_half = jnp.where(low_half if g == 0 else ~low_half, q_tile, 0.0)
+            if g != h % 2:
+                q_half = pltpu.roll(q_half, HEAD_SIZE, 1)
+            if h % 2 == 0:
+                q_half = jnp.where(low_half, q_half, 0.0)
+            else:
+                q_half = jnp.where(low_half, 0.0, q_half)
+            scores = lax.dot_general(
+                q_half.astype(jnp.bfloat16), k_tile, (((1,), (1,)), ((), ())),
+                preferred_element_type=jnp.float32) * score_scale
+            scores = jnp.where(visible, scores, masked_filler)
+            highest = jnp.max(scores, axis=1, keepdims=True)
+            weights = jnp.where(visible, jnp.exp(scores - highest), 0.0)
+            total = jnp.sum(weights, axis=1, keepdims=True)
+            acc = jnp.dot(weights.astype(jnp.bfloat16), v_tile, preferred_element_type=jnp.float32)
+            if g != h % 2:
+                acc = pltpu.roll(acc, HEAD_SIZE, 1)
+            out_tile = jnp.where(low_half if g == 0 else ~low_half, acc, out_tile)
+            stats = jnp.where(lane == j, highest, stats)
+            stats = jnp.where(lane == QUERY_HEADS + j, total, stats)
+        out_ref[:, h * 128:(h + 1) * 128] = out_tile
+    out_ref[:, QUERY_HEADS * HEAD_SIZE:QUERY_HEADS * HEAD_SIZE + 128] = stats
+
+
+def attend_partial(q_block, kv, mask):
+    rows = q_block.shape[0]
+    return pl.pallas_call(
+        _attend_kernel,
+        out_shape=jax.ShapeDtypeStruct((rows, QUERY_HEADS * HEAD_SIZE + 128), jnp.float32),
+    )(q_block, kv, mask)
 
 
 def pair_ffn(rows_in, gate_up_pair, down_pair):
@@ -67,7 +114,6 @@
     sibling = [(t, t ^ 1) for t in range(tok_size)]
     sibling_gate_up = lax.ppermute(expert_gate_up, "tok", sibling)
     sibling_down = lax.ppermute(expert_down, "tok", sibling)
-    heads_per_group = QUERY_HEADS // KEY_VALUE_HEADS
     kv_width = KEY_VALUE_HEADS * HEAD_SIZE
     pool_size = lax.axis_size("pool")
     pool_idx = lax.axis_index("pool")
@@ -102,10 +148,6 @@
     key_value_pairs = jnp.concatenate(
         [cache_block_pool.reshape(pool_blocks * block_len, 2 * kv_width), fresh_kv], axis=0
     )
-    key_count = key_value_pairs.shape[0]
-    key_row_block = key_value_pairs[:, :kv_width].reshape(key_count, KEY_VALUE_HEADS, HEAD_SIZE)
-    value_row_block = key_value_pairs[:, kv_width:].reshape(key_count, KEY_VALUE_HEADS, HEAD_SIZE)
-    stat_pad = 128 - 2 * QUERY_HEADS
 
     def attend_block(query_block, source):
         first = source * tokens_per_device
@@ -117,38 +159,7 @@
             fresh_order[None, :] <= query_order[:, None]
         )
         visible = jnp.concatenate([cache_visible, fresh_visible], axis=1)
-        query_row_block = query_block.reshape(
-            tokens_per_device, KEY_VALUE_HEADS, heads_per_group, HEAD_SIZE
-        )
-        scores = (
-            jnp.einsum(
-                "qhgd,khd->qhgk",
-                query_row_block,
-                key_row_block,
-                preferred_element_type=jnp.float32,
-            )
-            * score_scale
-        )
-        shown_keys = visible[:, None, None, :]
-        scores = jnp.where(shown_keys, scores, masked_filler)
-        highest = jnp.max(scores, axis=-1)
-        weights = jnp.where(shown_keys, jnp.exp(scores - highest[..., None]), 0.0)
-        denominator = jnp.sum(weights, axis=-1)
-        summed = jnp.einsum(
-            "qhgk,khd->qhgd",
-            weights.astype(jnp.bfloat16),
-            value_row_block,
-            preferred_element_type=jnp.float32,
-        )
-        return jnp.concatenate(
-            [
-                summed.reshape(tokens_per_device, QUERY_HEADS * HEAD_SIZE),
-                highest.reshape(tokens_per_device, QUERY_HEADS),
-                denominator.reshape(tokens_per_device, QUERY_HEADS),
-                jnp.zeros((tokens_per_device, stat_pad), jnp.float32),
-            ],
-            axis=1,
-        )
+        return attend_partial(query_block, key_value_pairs, visible.astype(jnp.float32))
 
     query_blocks = [queries] + [
         lax.ppermute(

time: 204 us -> 205 us (level)
  Pallas kernels: 0 us -> 26.6 us
  local copies, waits for them, and re-layouts: 27.6 us -> 14.6 us
  matrix products: 28.1 us -> 16.1 us
    pallas_call x0 -> x4, Pallas kernels: none -> 26.6 us  [attend_partial(): pl.pallas_call(_attend_kernel, out_shape=jax.ShapeDtypeStruct((rows, QUER...]
    reshape x17 -> x1, local copies, waits for them, and re-layouts: 12.6 us -> 1.18 us  [body(): denominator = jnp.repeat(denominator, HEAD_SIZE, axis=1)]
    dot_general x8 -> x0, matrix products: 10.8 us -> none  [the longest x4 7.37 us: attend_block(): jnp.einsum('qhgk,khd->qhgd', weights.astype(jnp.bfloat16), value_row_bloc...]
    reduce_sum x4 -> x0, other arithmetic: 5.89 us -> none  [attend_block(): denominator = jnp.sum(weights, axis=-1)]
    concatenate x4 -> x0, local copies, waits for them, and re-layouts: 3.28 us -> none  [attend_block(): jnp.concatenate([summed.reshape(tokens_per_device, QUERY_HEADS * HEAD_SIZ...]
    convert_element_type x0 -> x4, other arithmetic: none -> 2.72 us  [attend_block(): visible.astype(jnp.float32)]
  transfers between devices with their start and end apart: 10 -> 10, of which waited for: 3 -> 2; matrix products, arithmetic and copies ran while one was open for 23% -> 12% of each run, Pallas kernels for 0% -> 13%
where the time goes in v5:
time: 205 us; the launch traced here: 204 us
  waiting for transfers between devices  101 us (49%)
  starting transfers between devices  27 us (13%)
  Pallas kernels  26.6 us (13%)
  other arithmetic  17.5 us (9%)
  matrix products  16.1 us (8%)
  local copies, waits for them, and re-layouts  14.6 us (7%)
    all_to_all x1, waiting for transfers between devices, direct_dispatch(): lax.all_to_all(unit_rows, 'tok', split_axis=0, concat_axis=0, tiled=True)  50.5 us
    all_to_all x1, waiting for transfers between devices, direct_dispatch(): lax.all_to_all(produced.reshape(EXPERTS * split, CAP // split, width), 't...  50.3 us
    pallas_call x4, Pallas kernels, attend_partial(): pl.pallas_call(_attend_kernel, out_shape=jax.ShapeDtypeStruct((rows, QUER...  26.6 us
    all_to_all x1, starting transfers between devices, direct_dispatch(): lax.all_to_all(unit_rows, 'tok', split_axis=0, concat_axis=0, tiled=True)  12.4 us
    dot_general x2, matrix products, pair_ffn(): jnp.dot(rows_in, gate_up_pair[part], preferred_element_type=jnp.float32)  6.01 us
    all_to_all x1, starting transfers between devices, direct_dispatch(): lax.all_to_all(produced.reshape(EXPERTS * split, CAP // split, width), 't...  5.75 us
    ppermute x3, starting transfers between devices, body(): lax.ppermute(queries, 'pool', [(i, (i + shift) % pool_size) for i in rang...  5.13 us
  transfers between devices with their start and end apart: 10, of which 2 were waited for; matrix products, arithmetic and copies ran while one was open for 12% of the time, Pallas kernels for 13%

profile of v5, /device:TPU:8, one launch (start us, length us, event | category | flops | bytes accessed | tf_op | source)
XLA Modules:
  0.0 203.7 jit_solution(9555034477900586203)
XLA Ops:
  0.7 1.6 collective-permute-start
  2.2 1.7 collective-permute-start.4
  4.0 1.8 collective-permute-start.2
  7.5 0.8 select_reduce_fusion.2
  9.9 0.8 select_reduce_fusion.1
  11.4 1.4 fusion.24
  12.9 1.2 reduce-window.6
  14.6 0.8 compare_and_fusion.3
  15.5 0.9 compare_and_fusion.7
  18.4 2.0 pad_maximum_fusion.kv_ref
  20.4 6.7 %shard_map.141 = f32[64,1152]{1,0:T(8,128)} custom-call(bf16[64,1024]{1,0:T(8,128)(2,1)} %collective-permute-done.q_ref, bf16[576,1024]{1,0:T(8,128)(2,1)} %pad_maximum_fusion.kv_ref, f32[64,576]{1,0:T(8,128)} %add_convert_fusion.2.mask_ref), custom_call_target="tpu_custom_call" | custom-call | tf_op jit(solution)/shard_map/pallas_call | solution.py:60
  27.1 1.1 collective-permute-start.1
  28.9 6.7 %shard_map.142 = f32[64,1152]{1,0:T(8,128)} custom-call(bf16[64,1024]{1,0:T(8,128)(2,1)} %copy-done.15, bf16[576,1024]{1,0:T(8,128)(2,1)} %pad_maximum_fusion.kv_ref, f32[64,576]{1,0:T(8,128)} %add_convert_fusion.3.mask_ref), custom_call_target="tpu_custom_call" | custom-call | tf_op jit(solution)/shard_map/pallas_call | solution.py:60
  35.6 1.5 collective-permute-start.3
  37.8 6.6 %shard_map.143 = f32[64,1152]{1,0:T(8,128)} custom-call(bf16[64,1024]{1,0:T(8,128)(2,1)} %copy-done.14, bf16[576,1024]{1,0:T(8,128)(2,1)} %pad_maximum_fusion.kv_ref, f32[64,576]{1,0:T(8,128)} %add_convert_fusion.4.mask_ref), custom_call_target="tpu_custom_call" | custom-call | tf_op jit(solution)/shard_map/pallas_call | solution.py:60
  45.7 6.6 %shard_map.140 = f32[64,1152]{1,0:T(8,128)} custom-call(bf16[64,1024]{1,0:T(8,128)(2,1)} %q_ref.1, bf16[576,1024]{1,0:T(8,128)(2,1)} %pad_maximum_fusion.kv_ref, f32[64,576]{1,0:T(8,128)} %add_convert_fusion.1.mask_ref), custom_call_target="tpu_custom_call" | custom-call | tf_op jit(solution)/shard_map/pallas_call | solution.py:60
  52.3 1.3 fusion
  55.4 1.4 pad_maximum_fusion.1
  57.5 1.0 broadcast_in_dim.47
  58.5 1.2 reshape.130
  59.7 2.9 %broadcast_in_dim.46 = f32[4,64,16,64]{3,2,1,0:T(8,128)} broadcast(f32[4,64,16]{2,1,0:T(8,128)} %get-tuple-element.5), dimensions={0,1,2} | broadcast | bytes 1064960 | tf_op jit(solution)/shard_map/broadcast_in_dim | solution.py:186
  62.6 2.8 %reshape.129 = f32[4,64,1024]{2,1,0:T(8,128)} reshape(f32[4,64,16,64]{3,2,1,0:T(8,128)} %broadcast_in_dim.46) | data formatting | bytes 2097152 | tf_op jit(solution)/shard_map/reshape | solution.py:186
  65.4 1.4 fusion.4
  67.6 2.1 %convolution_convert_fusion = bf16[1024,1024]{1,0:T(8,128)(2,1)} fusion(pred[1024,64]{0,1:T(8,128)(4,1)S(1)} %copy-done.12, f32[64,1024]{1,0:T(8,128)S(1)} %get-tuple-element.24, f32[1024]{0:T(1024)S(1)} %copy-done.17, f32[64]{0:T(128)S(1)} %add_rsqrt_fusion), kind=kOutput, calls=%fused_computation.4 | convolution fusion | flops 135462912 | bytes 2429184 | tf_op jit(solution)/shard_map/dot_general | solution.py:205
  69.7 12.4 %all-to-all-start = ((bf16[64,16,1024]{2,1,0:T(8,128)(2,1)}), bf16[64,16,1024]{2,1,0:T(8,128)(2,1)}, u32[]{:S(2)}, u32[]{:S(2)}) async-start(bf16[64,16,1024]{2,1,0:T(8,128)(2,1)} %bitcast.62), calls=%async_computation | async-start | bytes 4194304 | tf_op jit(solution)/shard_map/all_to_all | solution.py:85
  82.8 50.5 %all-to-all-done = bf16[64,16,1024]{2,1,0:T(8,128)(2,1)} async-done(((bf16[64,16,1024]{2,1,0:T(8,128)(2,1)}), bf16[64,16,1024]{2,1,0:T(8,128)(2,1)}, u32[]{:S(2)}, u32[]{:S(2)}) %all-to-all-start) | async-done | bytes 2097184 | tf_op jit(solution)/shard_map/all_to_all | solution.py:85
  133.3 2.9 %fusion.7 = f32[1024,512]{1,0:T(8,128)S(1)} fusion(bf16[1024,1024]{1,0:T(8,128)(2,1)} %bitcast.15, bf16[1,1024,512]{2,1,0:T(8,128)(2,1)S(1)} %copy-done.19), kind=kOutput, calls=%fused_computation.18 | convolution fusion | flops 1073741824 | bytes 5242880 | tf_op jit(solution)/shard_map/dot_general | solution.py:70
  137.0 3.1 %fusion.5 = f32[1024,512]{1,0:T(8,128)S(1)} fusion(bf16[1024,1024]{1,0:T(8,128)(2,1)} %bitcast.15, bf16[1,1024,512]{2,1,0:T(8,128)(2,1)} %collective-permute-done.6), kind=kOutput, calls=%fused_computation.16 | convolution fusion | flops 1073741824 | bytes 5242880 | tf_op jit(solution)/shard_map/dot_general | solution.py:70
  140.1 3.2 %add_convert_fusion = bf16[1024,1024]{1,0:T(8,128)(2,1)} fusion(bf16[1024,1024]{1,0:T(8,128)(2,1)S(1)} %fusion.9, f32[1024,512]{1,0:T(8,128)S(1)} %fusion.5, bf16[1,256,1024]{2,1,0:T(8,128)(2,1)} %collective-permute-done.7), kind=kOutput, calls=%fused_computation | convolution fusion | flops 543686656 | bytes 6815744 | tf_op jit(solution)/shard_map/dot_general | solution.py:74
  143.3 5.8 %all-to-all-start.1 = ((bf16[64,16,1024]{2,1,0:T(8,128)(2,1)}), bf16[64,16,1024]{2,1,0:T(8,128)(2,1)}, u32[]{:S(2)}, u32[]{:S(2)}) async-start(bf16[64,16,1024]{2,1,0:T(8,128)(2,1)} %bitcast.75), calls=%async_computation.1 | async-start | bytes 4194304 | tf_op jit(solution)/shard_map/all_to_all | solution.py:87
  149.9 50.3 %all-to-all-done.1 = bf16[64,16,1024]{2,1,0:T(8,128)(2,1)} async-done(((bf16[64,16,1024]{2,1,0:T(8,128)(2,1)}), bf16[64,16,1024]{2,1,0:T(8,128)(2,1)}, u32[]{:S(2)}, u32[]{:S(2)}) %all-to-all-start.1) | async-done | bytes 2097184 | tf_op jit(solution)/shard_map/all_to_all | solution.py:87
  200.3 3.5 %fusion.1 = bf16[64,1024]{1,0:T(8,128)(2,1)} fusion(f32[64,1024]{1,0:T(8,128)S(1)} %get-tuple-element.24, f32[1024,64]{0,1:T(8,128)S(1)} %select_reduce_fusion, bf16[1024,1024]{1,0:T(8,128)(2,1)} %bitcast.21), kind=kOutput, calls=%fused_computation.9 | convolution fusion | flops 805437440 | bytes 2752512 | tf_op jit(solution)/shard_map/dot_general | solution.py:216
  (89 shorter events, 14.6 us)
Async XLA Ops:
  0.6 66.2 %copy-start = (bf16[1024,1024]{1,0:T(8,128)(2,1)S(1)}, bf16[1024,1024]{1,0:T(8,128)(2,1)}, u32[]{:S(2)}) copy-start(bf16[1024,1024]{1,0:T(8,128)(2,1)} %param.20) | copy-start | bytes 6291460
  0.6 17.8 %copy-start.8 = (bf16[8,64,1024]{2,1,0:T(8,128)(2,1)S(1)}, bf16[8,64,1024]{2,1,0:T(8,128)(2,1)}, u32[]{:S(2)}) copy-start(bf16[8,64,1024]{2,1,0:T(8,128)(2,1)} %param.16) | copy-start | bytes 3145732
  0.7 19.8 %collective-permute-start = (bf16[64,1024]{1,0:T(8,128)(2,1)}, bf16[64,1024]{1,0:T(8,128)(2,1)}, u32[]{:S(2)}, u32[]{:S(2)}) collective-permute-start(bf16[64,1024]{1,0:T(8,128)(2,1)} %q_ref.1), channel_id=1, source_target_pairs={{0,1},{1,2},{2,3},{3,0},{4,5},{5,6},{6,7},{7,4},{8,9},{9,10},{10,1... | collective-permute-start | bytes 393224 | tf_op jit(solution)/shard_map/ppermute | solution.py:165
  2.2 34.9 %collective-permute-start.4 = (bf16[64,1024]{1,0:T(8,128)(2,1)}, bf16[64,1024]{1,0:T(8,128)(2,1)S(1)}, u32[]{:S(2)}, u32[]{:S(2)}) collective-permute-start(bf16[64,1024]{1,0:T(8,128)(2,1)} %q_ref.1), channel_id=1, source_target_pairs={{0,3},{1,0},{2,1},{3,2},{4,7},{5,4},{6,5},{7,6},{8,11},{9,8},{10,9... | collective-permute-start | bytes 393224 | tf_op jit(solution)/shard_map/ppermute | solution.py:165
  4.0 24.3 %collective-permute-start.2 = (bf16[64,1024]{1,0:T(8,128)(2,1)}, bf16[64,1024]{1,0:T(8,128)(2,1)S(1)}, u32[]{:S(2)}, u32[]{:S(2)}) collective-permute-start(bf16[64,1024]{1,0:T(8,128)(2,1)} %q_ref.1), channel_id=1, source_target_pairs={{0,2},{1,3},{2,0},{3,1},{4,6},{5,7},{6,4},{7,5},{8,10},{9,11},{10,... | collective-permute-start | bytes 393224 | tf_op jit(solution)/shard_map/ppermute | solution.py:165
  27.1 17.8 %copy-start.16 = (s32[64,8]{0,1:T(8,128)S(1)}, s32[64,8]{0,1:T(8,128)}, u32[]{:S(2)}) copy-start(s32[64,8]{0,1:T(8,128)} %param.24) | copy-start | bytes 6148
  27.1 26.5 %collective-permute-start.1 = (f32[64,1152]{1,0:T(8,128)}, f32[64,1152]{1,0:T(8,128)S(1)}, u32[]{:S(2)}, u32[]{:S(2)}) collective-permute-start(f32[64,1152]{1,0:T(8,128)} %shard_map.141), channel_id=1, source_target_pairs={{0,3},{1,0},{2,1},{3,2},{4,7},{5,4},{6,5},{7,6},{8,11},{9,8},{10,9... | collective-permute-start | bytes 884744 | tf_op jit(solution)/shard_map/ppermute | solution.py:174
  28.3 0.7 copy-start.15
  35.6 18.1 %collective-permute-start.3 = (f32[64,1152]{1,0:T(8,128)}, f32[64,1152]{1,0:T(8,128)S(1)}, u32[]{:S(2)}, u32[]{:S(2)}) collective-permute-start(f32[64,1152]{1,0:T(8,128)} %shard_map.142), channel_id=1, source_target_pairs={{0,2},{1,3},{2,0},{3,1},{4,6},{5,7},{6,4},{7,5},{8,10},{9,11},{10,... | collective-permute-start | bytes 884744 | tf_op jit(solution)/shard_map/ppermute | solution.py:174
  37.1 0.7 copy-start.14
  44.4 9.3 %collective-permute-start.5 = (f32[64,1152]{1,0:T(8,128)}, f32[64,1152]{1,0:T(8,128)S(1)}, u32[]{:S(2)}, u32[]{:S(2)}) collective-permute-start(f32[64,1152]{1,0:T(8,128)} %shard_map.143), channel_id=1, source_target_pairs={{0,1},{1,2},{2,3},{3,0},{4,5},{5,6},{6,7},{7,4},{8,9},{9,10},{10,1... | collective-permute-start | bytes 884744 | tf_op jit(solution)/shard_map/ppermute | solution.py:174
  45.0 8.7 %copy-start.10 = (s32[64,8]{1,0:T(8,128)}, s32[64,8]{1,0:T(8,128)S(1)}, u32[]{:S(2)}) copy-start(s32[64,8]{1,0:T(8,128)S(1)} %copy.33) | copy-start | bytes 6148
  52.3 4.5 %copy-start.1 = (f32[64,1152]{1,0:T(8,128)S(1)}, f32[64,1152]{1,0:T(8,128)}, u32[]{:S(2)}) copy-start(f32[64,1152]{1,0:T(8,128)} %shard_map.140) | copy-start | bytes 884740
  53.7 0.7 copy-start.2
  53.7 0.8 copy-start.4
  53.7 0.9 copy-start.6
  55.4 1.4 copy-start.3
  55.4 1.4 copy-start.5
  55.4 1.5 copy-start.7
  65.4 1.5 copy-start.13
  66.8 0.8 copy-start.12
  66.8 0.8 copy-start.17
  66.9 2.8 %copy-start.9 = (bf16[64,1024]{1,0:T(8,128)(2,1)}, bf16[64,1024]{1,0:T(8,128)(2,1)S(1)}, u32[]{:S(2)}) copy-start(bf16[64,1024]{1,0:T(8,128)(2,1)S(1)} %divide_convert_fusion) | copy-start | bytes 393220
  69.7 12.4 %copy-start.19 = (bf16[1,1024,512]{2,1,0:T(8,128)(2,1)S(1)}, bf16[1,1024,512]{2,1,0:T(8,128)(2,1)}, u32[]{:S(2)}) copy-start(bf16[1,1024,512]{2,1,0:T(8,128)(2,1)} %param.22) | copy-start | bytes 3145732
  69.7 63.6 %all-to-all-start = ((bf16[64,16,1024]{2,1,0:T(8,128)(2,1)}), bf16[64,16,1024]{2,1,0:T(8,128)(2,1)}, u32[]{:S(2)}, u32[]{:S(2)}) async-start(bf16[64,16,1024]{2,1,0:T(8,128)(2,1)} %bitcast.62), calls=%async_computation | async-start | bytes 4194304 | tf_op jit(solution)/shard_map/all_to_all | solution.py:85
  82.2 54.8 %collective-permute-start.6 = (bf16[1,1024,512]{2,1,0:T(8,128)(2,1)S(1)}, bf16[1,1024,512]{2,1,0:T(8,128)(2,1)}, u32[]{:S(2)}, u32[]{:S(2)}) collective-permute-start(bf16[1,1024,512]{2,1,0:T(8,128)(2,1)S(1)} %copy-done.19), channel_id=1, source_target_pairs={{0,4},{4,0},{8,12},{12,8},{16,20},{20,16},{24,28},{28,24},{32,36},... | collective-permute-start | bytes 3145736 | tf_op jit(solution)/shard_map/ppermute | solution.py:115
  82.4 57.7 %collective-permute-start.7 = (bf16[1,256,1024]{2,1,0:T(8,128)(2,1)}, bf16[1,256,1024]{2,1,0:T(8,128)(2,1)}, u32[]{:S(2)}, u32[]{:S(2)}) collective-permute-start(bf16[1,256,1024]{2,1,0:T(8,128)(2,1)} %param.23), channel_id=1, source_target_pairs={{0,4},{4,0},{8,12},{12,8},{16,20},{20,16},{24,28},{28,24},{32,36},... | collective-permute-start | bytes 1572872 | tf_op jit(solution)/shard_map/ppermute | solution.py:116
  133.3 2.9 %copy-start.20 = (bf16[1,256,1024]{2,1,0:T(8,128)(2,1)S(1)}, bf16[1,256,1024]{2,1,0:T(8,128)(2,1)}, u32[]{:S(2)}) copy-start(bf16[1,256,1024]{2,1,0:T(8,128)(2,1)} %param.23) | copy-start | bytes 1572868
  143.3 5.8 %copy-start.18 = (f32[64,8]{0,1:T(8,128)S(1)}, f32[64,8]{0,1:T(8,128)}, u32[]{:S(2)}) copy-start(f32[64,8]{0,1:T(8,128)} %param.25) | copy-start | bytes 6148
  143.3 5.9 %copy-start.11 = (s32[64,8]{1,0:T(8,128)S(1)}, s32[64,8]{1,0:T(8,128)}, u32[]{:S(2)}) copy-start(s32[64,8]{1,0:T(8,128)} %copy-done.10) | copy-start | bytes 6148
  143.3 56.9 %all-to-all-start.1 = ((bf16[64,16,1024]{2,1,0:T(8,128)(2,1)}), bf16[64,16,1024]{2,1,0:T(8,128)(2,1)}, u32[]{:S(2)}, u32[]{:S(2)}) async-start(bf16[64,16,1024]{2,1,0:T(8,128)(2,1)} %bitcast.75), calls=%async_computation.1 | async-start | bytes 4194304 | tf_op jit(solution)/shard_map/all_to_all | solution.py:87

commit v6 on v5

--- a/solution.py
+++ b/solution.py
@@ -20,37 +20,40 @@
 
 def _attend_kernel(q_ref, kv_ref, mask_ref, out_ref):
     rows = q_ref.shape[0]
-    visible = mask_ref[...] > 0.5
+    shown = mask_ref[...] > 0.5
+    visible = jnp.concatenate([shown, shown], axis=0)
     lane = lax.broadcasted_iota(jnp.int32, (rows, 128), 1)
     low_half = lane < HEAD_SIZE
     stats = jnp.zeros((rows, 128), jnp.float32)
     for h in range(KEY_VALUE_HEADS):
         q_tile = q_ref[:, h * 128:(h + 1) * 128].astype(jnp.float32)
         k_tile = kv_ref[:, (h // 2) * 128:(h // 2 + 1) * 128]
-        v_tile = kv_ref[:, KEY_VALUE_HEADS * HEAD_SIZE + (h // 2) * 128:KEY_VALUE_HEADS * HEAD_SIZE + (h // 2 + 1) * 128]
-        out_tile = jnp.zeros((rows, 128), jnp.float32)
+        v_start = KEY_VALUE_HEADS * HEAD_SIZE + (h // 2) * 128
+        v_tile = kv_ref[:, v_start:v_start + 128]
+        halves = []
         for g in range(2):
-            j = 2 * h + g
             q_half = jnp.where(low_half if g == 0 else ~low_half, q_tile, 0.0)
             if g != h % 2:
                 q_half = pltpu.roll(q_half, HEAD_SIZE, 1)
-            if h % 2 == 0:
-                q_half = jnp.where(low_half, q_half, 0.0)
-            else:
-                q_half = jnp.where(low_half, 0.0, q_half)
-            scores = lax.dot_general(
-                q_half.astype(jnp.bfloat16), k_tile, (((1,), (1,)), ((), ())),
-                preferred_element_type=jnp.float32) * score_scale
-            scores = jnp.where(visible, scores, masked_filler)
-            highest = jnp.max(scores, axis=1, keepdims=True)
-            weights = jnp.where(visible, jnp.exp(scores - highest), 0.0)
-            total = jnp.sum(weights, axis=1, keepdims=True)
-            acc = jnp.dot(weights.astype(jnp.bfloat16), v_tile, preferred_element_type=jnp.float32)
+            halves.append(q_half)
+        q_pair = jnp.concatenate(halves, axis=0).astype(jnp.bfloat16)
+        scores = lax.dot_general(
+            q_pair, k_tile, (((1,), (1,)), ((), ())), preferred_element_type=jnp.float32
+        ) * score_scale
+        scores = jnp.where(visible, scores, masked_filler)
+        highest = jnp.max(scores, axis=1, keepdims=True)
+        weights = jnp.where(visible, jnp.exp(scores - highest), 0.0)
+        total = jnp.sum(weights, axis=1, keepdims=True)
+        acc = jnp.dot(weights.astype(jnp.bfloat16), v_tile, preferred_element_type=jnp.float32)
+        out_tile = jnp.zeros((rows, 128), jnp.float32)
+        for g in range(2):
+            part = acc[g * rows:(g + 1) * rows]
             if g != h % 2:
-                acc = pltpu.roll(acc, HEAD_SIZE, 1)
-            out_tile = jnp.where(low_half if g == 0 else ~low_half, acc, out_tile)
-            stats = jnp.where(lane == j, highest, stats)
-            stats = jnp.where(lane == QUERY_HEADS + j, total, stats)
+                part = pltpu.roll(part, HEAD_SIZE, 1)
+            out_tile = jnp.where(low_half if g == 0 else ~low_half, part, out_tile)
+            j = 2 * h + g
+            stats = jnp.where(lane == j, highest[g * rows:(g + 1) * rows], stats)
+            stats = jnp.where(lane == QUERY_HEADS + j, total[g * rows:(g + 1) * rows], stats)
         out_ref[:, h * 128:(h + 1) * 128] = out_tile
     out_ref[:, QUERY_HEADS * HEAD_SIZE:QUERY_HEADS * HEAD_SIZE + 128] = stats
 
@@ -182,10 +185,18 @@
     running = jnp.max(part_max, axis=0)
     rescale = jnp.exp(part_max - running[None])
     denominator = jnp.sum(part_sum * rescale, axis=0)
-    summed = jnp.sum(
-        gathered[:, :, :acc_width] * jnp.repeat(rescale, HEAD_SIZE, axis=2), axis=0
-    )
-    denominator = jnp.repeat(denominator, HEAD_SIZE, axis=1)
+    spread = (
+        jnp.arange(acc_width, dtype=jnp.int32)[None, :] // HEAD_SIZE
+        == jnp.arange(QUERY_HEADS, dtype=jnp.int32)[:, None]
+    ).astype(jnp.float32)
+
+    def widen(per_head):
+        return jnp.dot(
+            per_head, spread, precision=lax.Precision.HIGHEST, preferred_element_type=jnp.float32
+        )
+
+    summed = sum(gathered[p, :, :acc_width] * widen(rescale[p]) for p in range(pool_size))
+    denominator = widen(denominator)
     context = summed / denominator
     attended = context.reshape(tokens_per_device, QUERY_HEADS * HEAD_SIZE).astype(jnp.bfloat16)
     residual = stream.astype(jnp.float32) + jnp.dot(

time: 205 us -> 189 us (0.922)
  local copies, waits for them, and re-layouts: 14.6 us -> 5.73 us
  Pallas kernels: 26.6 us -> 19.2 us
  other arithmetic: 17.5 us -> 14.9 us
    pallas_call x4, Pallas kernels: 26.6 us -> 19.2 us  [attend_partial(): pl.pallas_call(_attend_kernel, out_shape=jax.ShapeDtypeStruct((rows, QUER...]
    reshape x2 -> x0, local copies, waits for them, and re-layouts: 3.96 us -> none  [the longest x1 2.78 us: body(): jnp.repeat(rescale, HEAD_SIZE, axis=2)]
    broadcast_in_dim x2 -> x0, local copies, waits for them, and re-layouts: 3.86 us -> none  [the longest x1 2.86 us: body(): jnp.repeat(rescale, HEAD_SIZE, axis=2)]
    reduce_sum x2 -> x0, other arithmetic: 2.09 us -> none  [the longest x1 1.39 us: body(): jnp.sum(gathered[:, :, :acc_width] * jnp.repeat(rescale, HEAD_SIZE, axis=...]
  transfers between devices with their start and end apart: 10 -> 10, of which waited for: 2 -> 3; matrix products, arithmetic and copies ran while one was open for 12% -> 13% of each run, Pallas kernels for 13% -> 10%
where the time goes in v6:
time: 189 us; the launch traced here: 188 us
  waiting for transfers between devices  103 us (54%)
  starting transfers between devices  27 us (14%)
  Pallas kernels  19.2 us (10%)
  matrix products  17.6 us (9%)
  other arithmetic  14.9 us (8%)
  local copies, waits for them, and re-layouts  5.73 us (3%)
    all_to_all x1, waiting for transfers between devices, direct_dispatch(): lax.all_to_all(unit_rows, 'tok', split_axis=0, concat_axis=0, tiled=True)  50.6 us
    all_to_all x1, waiting for transfers between devices, direct_dispatch(): lax.all_to_all(produced.reshape(EXPERTS * split, CAP // split, width), 't...  50.3 us
    pallas_call x4, Pallas kernels, attend_partial(): pl.pallas_call(_attend_kernel, out_shape=jax.ShapeDtypeStruct((rows, QUER...  19.2 us
    all_to_all x1, starting transfers between devices, direct_dispatch(): lax.all_to_all(unit_rows, 'tok', split_axis=0, concat_axis=0, tiled=True)  12.4 us
    dot_general x2, matrix products, pair_ffn(): jnp.dot(rows_in, gate_up_pair[part], preferred_element_type=jnp.float32)  6.2 us
    all_to_all x1, starting transfers between devices, direct_dispatch(): lax.all_to_all(produced.reshape(EXPERTS * split, CAP // split, width), 't...  5.73 us
    ppermute x3, starting transfers between devices, body(): lax.ppermute(queries, 'pool', [(i, (i + shift) % pool_size) for i in rang...  5.13 us
    dot_general x2, matrix products, pair_ffn(): jnp.dot(inner, down_pair[part], preferred_element_type=jnp.float32)  4.02 us
  transfers between devices with their start and end apart: 10, of which 3 were waited for; matrix products, arithmetic and copies ran while one was open for 13% of the time, Pallas kernels for 10%

profile of v6, /device:TPU:8, one launch (start us, length us, event | category | flops | bytes accessed | tf_op | source)
XLA Modules:
  0.0 188.3 jit_solution(2580665285143423631)
XLA Ops:
  0.7 1.6 collective-permute-start
  2.2 1.7 collective-permute-start.4
  4.0 1.8 collective-permute-start.2
  7.5 0.8 select_reduce_fusion.2
  8.3 0.8 copy.29
  10.0 0.8 select_reduce_fusion.1
  11.4 1.4 fusion.44
  13.0 1.2 reduce-window.6
  14.7 0.7 multiply_add_fusion
  15.4 0.8 compare_and_fusion.3
  16.3 0.9 compare_and_fusion.7
  19.2 2.0 %pad_maximum_fusion.kv_ref = bf16[576,1024]{1,0:T(8,128)(2,1)} fusion(bf16[64,1024]{1,0:T(8,128)(2,1)} %param.15, bf16[512,1024]{1,0:T(8,128)(2,1)S(1)} %bitcast.125), kind=kLoop, calls=%fused_computation.5 | loop fusion | flops 2359296 | bytes 2359296 | tf_op jit(solution)/shard_map/concatenate | solution.py:151
  21.2 4.8 %shard_map.141 = f32[64,1152]{1,0:T(8,128)} custom-call(bf16[64,1024]{1,0:T(8,128)(2,1)} %collective-permute-done.q_ref, bf16[576,1024]{1,0:T(8,128)(2,1)} %pad_maximum_fusion.kv_ref, f32[64,576]{1,0:T(8,128)} %add_convert_fusion.2.mask_ref), custom_call_target="tpu_custom_call" | custom-call | tf_op jit(solution)/shard_map/pallas_call | solution.py:63
  26.0 1.1 collective-permute-start.1
  27.8 4.8 %shard_map.142 = f32[64,1152]{1,0:T(8,128)} custom-call(bf16[64,1024]{1,0:T(8,128)(2,1)} %copy-done.6, bf16[576,1024]{1,0:T(8,128)(2,1)} %pad_maximum_fusion.kv_ref, f32[64,576]{1,0:T(8,128)} %add_convert_fusion.3.mask_ref), custom_call_target="tpu_custom_call" | custom-call | tf_op jit(solution)/shard_map/pallas_call | solution.py:63
  32.6 1.5 collective-permute-start.3
  34.8 4.8 %shard_map.143 = f32[64,1152]{1,0:T(8,128)} custom-call(bf16[64,1024]{1,0:T(8,128)(2,1)} %copy-done.5, bf16[576,1024]{1,0:T(8,128)(2,1)} %pad_maximum_fusion.kv_ref, f32[64,576]{1,0:T(8,128)} %add_convert_fusion.4.mask_ref), custom_call_target="tpu_custom_call" | custom-call | tf_op jit(solution)/shard_map/pallas_call | solution.py:63
  40.8 4.8 %shard_map.140 = f32[64,1152]{1,0:T(8,128)} custom-call(bf16[64,1024]{1,0:T(8,128)(2,1)} %q_ref.1, bf16[576,1024]{1,0:T(8,128)(2,1)} %pad_maximum_fusion.kv_ref, f32[64,576]{1,0:T(8,128)} %add_convert_fusion.1.mask_ref), custom_call_target="tpu_custom_call" | custom-call | tf_op jit(solution)/shard_map/pallas_call | solution.py:63
  46.4 2.0 %collective-permute-done.5 = f32[64,1152]{1,0:T(8,128)S(1)} collective-permute-done((f32[64,1152]{1,0:T(8,128)}, f32[64,1152]{1,0:T(8,128)S(1)}, u32[]{:S(2)}, u32[]{:S(2)}) %collective-permute-start.5) | collective-permute-done | bytes 294944 | tf_op jit(solution)/shard_map/ppermute | solution.py:177
  48.3 0.8 fusion.50
  49.1 0.9 subtract_exponential_fusion
  52.0 2.1 %convolution_convert_fusion = bf16[1024,1024]{1,0:T(8,128)(2,1)} fusion(pred[1024,64]{0,1:T(8,128)(4,1)S(1)} %fusion, f32[64,1024]{1,0:T(8,128)S(1)} %get-tuple-element.24, f32[1024]{0:T(1024)S(1)} %copy-done.7, f32[64]{0:T(128)S(1)} %add_rsqrt_fusion), kind=kOutput, calls=%fused_computation.4 | convolution fusion | flops 135462912 | bytes 2429184 | tf_op jit(solution)/shard_map/dot_general | solution.py:216
  54.1 12.4 %all-to-all-start = ((bf16[64,16,1024]{2,1,0:T(8,128)(2,1)}), bf16[64,16,1024]{2,1,0:T(8,128)(2,1)}, u32[]{:S(2)}, u32[]{:S(2)}) async-start(bf16[64,16,1024]{2,1,0:T(8,128)(2,1)} %bitcast.111), calls=%async_computation | async-start | bytes 4194304 | tf_op jit(solution)/shard_map/all_to_all | solution.py:88
  67.1 50.6 %all-to-all-done = bf16[64,16,1024]{2,1,0:T(8,128)(2,1)} async-done(((bf16[64,16,1024]{2,1,0:T(8,128)(2,1)}), bf16[64,16,1024]{2,1,0:T(8,128)(2,1)}, u32[]{:S(2)}, u32[]{:S(2)}) %all-to-all-start) | async-done | bytes 2097184 | tf_op jit(solution)/shard_map/all_to_all | solution.py:88
  117.7 3.1 %fusion.6 = f32[1024,512]{1,0:T(8,128)S(1)} fusion(bf16[1024,1024]{1,0:T(8,128)(2,1)} %bitcast.23, bf16[1,1024,512]{2,1,0:T(8,128)(2,1)} %param.22), kind=kOutput, calls=%fused_computation.16 | convolution fusion | flops 1073741824 | bytes 5242880 | tf_op jit(solution)/shard_map/dot_general | solution.py:73
  120.8 0.8 fusion.8
  121.6 3.1 %fusion.4 = f32[1024,512]{1,0:T(8,128)S(1)} fusion(bf16[1024,1024]{1,0:T(8,128)(2,1)} %bitcast.23, bf16[1,1024,512]{2,1,0:T(8,128)(2,1)} %collective-permute-done.6), kind=kOutput, calls=%fused_computation.14 | convolution fusion | flops 1073741824 | bytes 5242880 | tf_op jit(solution)/shard_map/dot_general | solution.py:73
  124.7 3.2 %add_convert_fusion = bf16[1024,1024]{1,0:T(8,128)(2,1)} fusion(bf16[1024,1024]{1,0:T(8,128)(2,1)S(1)} %fusion.8, f32[1024,512]{1,0:T(8,128)S(1)} %fusion.4, bf16[1,256,1024]{2,1,0:T(8,128)(2,1)} %collective-permute-done.7), kind=kOutput, calls=%fused_computation | convolution fusion | flops 543686656 | bytes 6815744 | tf_op jit(solution)/shard_map/dot_general | solution.py:77
  127.9 5.7 %all-to-all-start.1 = ((bf16[64,16,1024]{2,1,0:T(8,128)(2,1)}), bf16[64,16,1024]{2,1,0:T(8,128)(2,1)}, u32[]{:S(2)}, u32[]{:S(2)}) async-start(bf16[64,16,1024]{2,1,0:T(8,128)(2,1)} %bitcast.124), calls=%async_computation.1 | async-start | bytes 4194304 | tf_op jit(solution)/shard_map/all_to_all | solution.py:90
  133.8 0.7 select_reduce_fusion
  134.5 50.3 %all-to-all-done.1 = bf16[64,16,1024]{2,1,0:T(8,128)(2,1)} async-done(((bf16[64,16,1024]{2,1,0:T(8,128)(2,1)}), bf16[64,16,1024]{2,1,0:T(8,128)(2,1)}, u32[]{:S(2)}, u32[]{:S(2)}) %all-to-all-start.1) | async-done | bytes 2097184 | tf_op jit(solution)/shard_map/all_to_all | solution.py:90
  184.8 3.5 %fusion.1 = bf16[64,1024]{1,0:T(8,128)(2,1)} fusion(f32[64,1024]{1,0:T(8,128)S(1)} %get-tuple-element.24, f32[1024,64]{0,1:T(8,128)S(1)} %select_reduce_fusion, bf16[1024,1024]{1,0:T(8,128)(2,1)} %bitcast.29), kind=kOutput, calls=%fused_computation.9 | convolution fusion | flops 805437440 | bytes 2752512 | tf_op jit(solution)/shard_map/dot_general | solution.py:227
  (66 shorter events, 11.8 us)
Async XLA Ops:
  0.6 50.7 %copy-start = (bf16[1024,1024]{1,0:T(8,128)(2,1)S(1)}, bf16[1024,1024]{1,0:T(8,128)(2,1)}, u32[]{:S(2)}) copy-start(bf16[1024,1024]{1,0:T(8,128)(2,1)} %param.20) | copy-start | bytes 6291460
  0.6 18.5 %copy-start.2 = (bf16[8,64,1024]{2,1,0:T(8,128)(2,1)S(1)}, bf16[8,64,1024]{2,1,0:T(8,128)(2,1)}, u32[]{:S(2)}) copy-start(bf16[8,64,1024]{2,1,0:T(8,128)(2,1)} %param.16) | copy-start | bytes 3145732
  0.7 20.5 %collective-permute-start = (bf16[64,1024]{1,0:T(8,128)(2,1)}, bf16[64,1024]{1,0:T(8,128)(2,1)}, u32[]{:S(2)}, u32[]{:S(2)}) collective-permute-start(bf16[64,1024]{1,0:T(8,128)(2,1)} %q_ref.1), channel_id=1, source_target_pairs={{0,1},{1,2},{2,3},{3,0},{4,5},{5,6},{6,7},{7,4},{8,9},{9,10},{10,1... | collective-permute-start | bytes 393224 | tf_op jit(solution)/shard_map/ppermute | solution.py:168
  2.2 31.9 %collective-permute-start.4 = (bf16[64,1024]{1,0:T(8,128)(2,1)}, bf16[64,1024]{1,0:T(8,128)(2,1)S(1)}, u32[]{:S(2)}, u32[]{:S(2)}) collective-permute-start(bf16[64,1024]{1,0:T(8,128)(2,1)} %q_ref.1), channel_id=1, source_target_pairs={{0,3},{1,0},{2,1},{3,2},{4,7},{5,4},{6,5},{7,6},{8,11},{9,8},{10,9... | collective-permute-start | bytes 393224 | tf_op jit(solution)/shard_map/ppermute | solution.py:168
  4.0 23.2 %collective-permute-start.2 = (bf16[64,1024]{1,0:T(8,128)(2,1)}, bf16[64,1024]{1,0:T(8,128)(2,1)S(1)}, u32[]{:S(2)}, u32[]{:S(2)}) collective-permute-start(bf16[64,1024]{1,0:T(8,128)(2,1)} %q_ref.1), channel_id=1, source_target_pairs={{0,2},{1,3},{2,0},{3,1},{4,6},{5,7},{6,4},{7,5},{8,10},{9,11},{10,... | collective-permute-start | bytes 393224 | tf_op jit(solution)/shard_map/ppermute | solution.py:168
  26.0 20.4 %collective-permute-start.1 = (f32[64,1152]{1,0:T(8,128)}, f32[64,1152]{1,0:T(8,128)S(1)}, u32[]{:S(2)}, u32[]{:S(2)}) collective-permute-start(f32[64,1152]{1,0:T(8,128)} %shard_map.141), channel_id=1, source_target_pairs={{0,3},{1,0},{2,1},{3,2},{4,7},{5,4},{6,5},{7,6},{8,11},{9,8},{10,9... | collective-permute-start | bytes 884744 | tf_op jit(solution)/shard_map/ppermute | solution.py:177
  27.1 0.7 copy-start.6
  32.6 13.8 %collective-permute-start.3 = (f32[64,1152]{1,0:T(8,128)}, f32[64,1152]{1,0:T(8,128)S(1)}, u32[]{:S(2)}, u32[]{:S(2)}) collective-permute-start(f32[64,1152]{1,0:T(8,128)} %shard_map.142), channel_id=1, source_target_pairs={{0,2},{1,3},{2,0},{3,1},{4,6},{5,7},{6,4},{7,5},{8,10},{9,11},{10,... | collective-permute-start | bytes 884744 | tf_op jit(solution)/shard_map/ppermute | solution.py:177
  34.1 0.7 copy-start.5
  39.6 8.8 %collective-permute-start.5 = (f32[64,1152]{1,0:T(8,128)}, f32[64,1152]{1,0:T(8,128)S(1)}, u32[]{:S(2)}, u32[]{:S(2)}) collective-permute-start(f32[64,1152]{1,0:T(8,128)} %shard_map.143), channel_id=1, source_target_pairs={{0,1},{1,2},{2,3},{3,0},{4,5},{5,6},{6,7},{7,4},{8,9},{9,10},{10,1... | collective-permute-start | bytes 884744 | tf_op jit(solution)/shard_map/ppermute | solution.py:177
  45.6 5.4 %copy-start.1 = (f32[64,1152]{1,0:T(8,128)S(1)}, f32[64,1152]{1,0:T(8,128)}, u32[]{:S(2)}) copy-start(f32[64,1152]{1,0:T(8,128)} %shard_map.140) | copy-start | bytes 884740
  50.0 1.4 copy-start.4
  51.0 1.0 copy-start.7
  51.4 2.7 %copy-start.3 = (bf16[64,1024]{1,0:T(8,128)(2,1)}, bf16[64,1024]{1,0:T(8,128)(2,1)S(1)}, u32[]{:S(2)}) copy-start(bf16[64,1024]{1,0:T(8,128)(2,1)S(1)} %fusion.22) | copy-start | bytes 393220
  54.1 12.6 %copy-start.9 = (bf16[1,256,1024]{2,1,0:T(8,128)(2,1)S(1)}, bf16[1,256,1024]{2,1,0:T(8,128)(2,1)}, u32[]{:S(2)}) copy-start(bf16[1,256,1024]{2,1,0:T(8,128)(2,1)} %param.23) | copy-start | bytes 1572868
  54.1 63.6 %all-to-all-start = ((bf16[64,16,1024]{2,1,0:T(8,128)(2,1)}), bf16[64,16,1024]{2,1,0:T(8,128)(2,1)}, u32[]{:S(2)}, u32[]{:S(2)}) async-start(bf16[64,16,1024]{2,1,0:T(8,128)(2,1)} %bitcast.111), calls=%async_computation | async-start | bytes 4194304 | tf_op jit(solution)/shard_map/all_to_all | solution.py:88
  66.5 55.0 %collective-permute-start.6 = (bf16[1,1024,512]{2,1,0:T(8,128)(2,1)}, bf16[1,1024,512]{2,1,0:T(8,128)(2,1)}, u32[]{:S(2)}, u32[]{:S(2)}) collective-permute-start(bf16[1,1024,512]{2,1,0:T(8,128)(2,1)} %param.22), channel_id=1, source_target_pairs={{0,4},{4,0},{8,12},{12,8},{16,20},{20,16},{24,28},{28,24},{32,36},... | collective-permute-start | bytes 3145736 | tf_op jit(solution)/shard_map/ppermute | solution.py:118
  66.7 58.0 %collective-permute-start.7 = (bf16[1,256,1024]{2,1,0:T(8,128)(2,1)S(1)}, bf16[1,256,1024]{2,1,0:T(8,128)(2,1)}, u32[]{:S(2)}, u32[]{:S(2)}) collective-permute-start(bf16[1,256,1024]{2,1,0:T(8,128)(2,1)S(1)} %copy-done.9), channel_id=1, source_target_pairs={{0,4},{4,0},{8,12},{12,8},{16,20},{20,16},{24,28},{28,24},{32,36},... | collective-permute-start | bytes 1572872 | tf_op jit(solution)/shard_map/ppermute | solution.py:119
  127.9 5.7 %copy-start.8 = (f32[64,8]{0,1:T(8,128)S(1)}, f32[64,8]{0,1:T(8,128)}, u32[]{:S(2)}) copy-start(f32[64,8]{0,1:T(8,128)} %param.25) | copy-start | bytes 6148
  127.9 56.9 %all-to-all-start.1 = ((bf16[64,16,1024]{2,1,0:T(8,128)(2,1)}), bf16[64,16,1024]{2,1,0:T(8,128)(2,1)}, u32[]{:S(2)}, u32[]{:S(2)}) async-start(bf16[64,16,1024]{2,1,0:T(8,128)(2,1)} %bitcast.124), calls=%async_computation.1 | async-start | bytes 4194304 | tf_op jit(solution)/shard_map/all_to_all | solution.py:90

commit v7 on v6

--- a/solution.py
+++ b/solution.py
@@ -12,15 +12,25 @@
 FF = 512
 TOPK = 8
 CAP = 32
+FRESH_BASE = 1 << 20
 
 
 score_scale = 0.015625
 masked_filler = -1e30
 
 
-def _attend_kernel(q_ref, kv_ref, mask_ref, out_ref):
+def _attend_kernel(
+    source_ref, q_ref, kv_ref, query_len_ref, query_seg_ref, key_pos_ref, key_seg_ref, out_ref
+):
     rows = q_ref.shape[0]
-    shown = mask_ref[...] > 0.5
+    first = pl.multiple_of(source_ref[0] * rows, rows)
+    query_len = query_len_ref[pl.ds(first, rows), :]
+    query_seg = query_seg_ref[pl.ds(first, rows), :]
+    query_order = first + lax.broadcasted_iota(jnp.int32, (rows, 1), 0)
+    key_pos = key_pos_ref[...]
+    shown = (key_pos < query_len) | (
+        (key_seg_ref[...] == query_seg) & (key_pos - FRESH_BASE <= query_order)
+    )
     visible = jnp.concatenate([shown, shown], axis=0)
     lane = lax.broadcasted_iota(jnp.int32, (rows, 128), 1)
     low_half = lane < HEAD_SIZE
@@ -58,12 +68,20 @@
     out_ref[:, QUERY_HEADS * HEAD_SIZE:QUERY_HEADS * HEAD_SIZE + 128] = stats
 
 
-def attend_partial(q_block, kv, mask):
+def attend_partial(source, q_block, kv, query_len, query_seg, key_pos, key_seg):
     rows = q_block.shape[0]
+    whole = lambda shape: pl.BlockSpec(shape, lambda i, s: (0,) * len(shape))
+    operands = (q_block, kv, query_len, query_seg, key_pos, key_seg)
     return pl.pallas_call(
         _attend_kernel,
         out_shape=jax.ShapeDtypeStruct((rows, QUERY_HEADS * HEAD_SIZE + 128), jnp.float32),
-    )(q_block, kv, mask)
+        grid_spec=pltpu.PrefetchScalarGridSpec(
+            num_scalar_prefetch=1,
+            grid=(1,),
+            in_specs=[whole(x.shape) for x in operands],
+            out_specs=whole((rows, QUERY_HEADS * HEAD_SIZE + 128)),
+        ),
+    )(jnp.reshape(source, (1,)).astype(jnp.int32), *operands)
 
 
 def pair_ffn(rows_in, gate_up_pair, down_pair):
@@ -152,17 +170,20 @@
         [cache_block_pool.reshape(pool_blocks * block_len, 2 * kv_width), fresh_kv], axis=0
     )
 
+    unlisted = jnp.int32(1 << 30)
+    key_pos = jnp.concatenate(
+        [jnp.where(cache_listed, cache_pos, unlisted), FRESH_BASE + fresh_order]
+    ).reshape(1, -1)
+    key_seg = jnp.concatenate(
+        [jnp.full((pool_blocks * block_len,), -1, jnp.int32), fresh_seg]
+    ).reshape(1, -1)
+    query_len_all = row_len.reshape(-1, 1)
+    query_seg_all = segments.reshape(-1, 1)
+
     def attend_block(query_block, source):
-        first = source * tokens_per_device
-        query_order = first + jnp.arange(tokens_per_device, dtype=jnp.int32)
-        query_seg = lax.dynamic_slice_in_dim(segments, first, tokens_per_device)
-        query_len = lax.dynamic_slice_in_dim(row_len, first, tokens_per_device)
-        cache_visible = cache_listed[None, :] & (cache_pos[None, :] < query_len[:, None])
-        fresh_visible = (fresh_seg[None, :] == query_seg[:, None]) & (
-            fresh_order[None, :] <= query_order[:, None]
-        )
-        visible = jnp.concatenate([cache_visible, fresh_visible], axis=1)
-        return attend_partial(query_block, key_value_pairs, visible.astype(jnp.float32))
+        return attend_partial(
+            source, query_block, key_value_pairs, query_len_all, query_seg_all, key_pos, key_seg
+        )
 
     query_blocks = [queries] + [
         lax.ppermute(

time: 189 us -> 185 us (0.979)
  other arithmetic: 14.9 us -> 8.51 us
  local copies, waits for them, and re-layouts: 5.73 us -> 7.79 us
    convert_element_type x4 -> x0, other arithmetic: 2.72 us -> none  [attend_block(): visible.astype(jnp.float32)]
    reshape x0 -> x3, local copies, waits for them, and re-layouts: none -> 2 us  [the longest x1 0.8 us: body(): query_len_all = row_len.reshape(-1, 1)]
  transfers between devices with their start and end apart: 10 -> 10, of which waited for: 3 -> 3; matrix products, arithmetic and copies ran while one was open for 13% -> 10% of each run, Pallas kernels for 10% -> 11%
where the time goes in v7:
time: 185 us
  waiting for transfers between devices  103 us (56%)
  starting transfers between devices  27 us (15%)
  Pallas kernels  19.6 us (11%)
  matrix products  17.4 us (9%)
  other arithmetic  8.51 us (5%)
  local copies, waits for them, and re-layouts  7.79 us (4%)
    all_to_all x1, waiting for transfers between devices, direct_dispatch(): lax.all_to_all(unit_rows, 'tok', split_axis=0, concat_axis=0, tiled=True)  50.5 us
    all_to_all x1, waiting for transfers between devices, direct_dispatch(): lax.all_to_all(produced.reshape(EXPERTS * split, CAP // split, width), 't...  50.3 us
    pallas_call x4, Pallas kernels, attend_partial(): pl.pallas_call(_attend_kernel, out_shape=jax.ShapeDtypeStruct((rows, QUER...  19.6 us
    all_to_all x1, starting transfers between devices, direct_dispatch(): lax.all_to_all(unit_rows, 'tok', split_axis=0, concat_axis=0, tiled=True)  12.4 us
    dot_general x2, matrix products, pair_ffn(): jnp.dot(rows_in, gate_up_pair[part], preferred_element_type=jnp.float32)  5.99 us
    all_to_all x1, starting transfers between devices, direct_dispatch(): lax.all_to_all(produced.reshape(EXPERTS * split, CAP // split, width), 't...  5.76 us
    ppermute x3, starting transfers between devices, body(): lax.ppermute(queries, 'pool', [(i, (i + shift) % pool_size) for i in rang...  5.13 us
    dot_general x2, matrix products, pair_ffn(): jnp.dot(inner, down_pair[part], preferred_element_type=jnp.float32)  3.99 us
  transfers between devices with their start and end apart: 10, of which 3 were waited for; matrix products, arithmetic and copies ran while one was open for 10% of the time, Pallas kernels for 11%

profile of v7, /device:TPU:8, one launch (start us, length us, event | category | flops | bytes accessed | tf_op | source)
XLA Modules:
  0.0 184.7 jit_solution(4200201977209868719)
XLA Ops:
  0.6 1.6 collective-permute-start
  2.2 1.7 collective-permute-start.4
  4.0 1.8 collective-permute-start.2
  5.8 0.8 select_reduce_fusion.1
  6.6 0.8 copy.53
  8.4 0.7 dynamic-slice_bitcast_fusion
  9.7 1.2 reduce-window.6
  11.4 0.8 select_reduce_fusion.2
  12.2 0.8 copy.45.query_len_ref
  13.0 1.5 copy.46.query_seg_ref
  14.5 2.4 %pad_maximum_fusion.kv_ref = bf16[576,1024]{1,0:T(8,128)(2,1)} fusion(bf16[64,1024]{1,0:T(8,128)(2,1)} %param.15, bf16[512,1024]{1,0:T(8,128)(2,1)} %bitcast.123), kind=kLoop, calls=%fused_computation.5 | loop fusion | flops 2359296 | bytes 2359296 | tf_op jit(solution)/shard_map/concatenate | solution.py:169
  17.5 4.9 %shard_map.141 = f32[64,1152]{1,0:T(8,128)} custom-call(s32[1]{0:T(128)} %bitcast.10.source_ref, bf16[64,1024]{1,0:T(8,128)(2,1)} %copy-done.6, bf16[576,1024]{1,0:T(8,128)(2,1)} %pad_maximum_fusion.kv_ref, s32[256,1]{1,0:T(8,128)} %copy.45.query_len_ref, s32[256,1]{1,0:T(8,128)} %copy.46.query_seg_ref, s32[1,576]{1,0:T(1,128)} %reshape.138.key_pos_ref, ...), custom_call_target="tpu_custom_call" | custom-call | tf_op jit(solution)/shard_map/pallas_call | solution.py:75
  22.4 1.1 collective-permute-start.1
  24.2 4.9 %shard_map.142 = f32[64,1152]{1,0:T(8,128)} custom-call(s32[1]{0:T(128)} %bitcast.12.source_ref, bf16[64,1024]{1,0:T(8,128)(2,1)} %copy-done.5, bf16[576,1024]{1,0:T(8,128)(2,1)} %pad_maximum_fusion.kv_ref, s32[256,1]{1,0:T(8,128)} %copy.45.query_len_ref, s32[256,1]{1,0:T(8,128)} %copy.46.query_seg_ref, s32[1,576]{1,0:T(1,128)} %reshape.138.key_pos_ref, ...), custom_call_target="tpu_custom_call" | custom-call | tf_op jit(solution)/shard_map/pallas_call | solution.py:75
  29.1 1.5 collective-permute-start.3
  31.3 4.9 %shard_map.143 = f32[64,1152]{1,0:T(8,128)} custom-call(s32[1]{0:T(128)} %bitcast.14.source_ref, bf16[64,1024]{1,0:T(8,128)(2,1)} %copy-done.4, bf16[576,1024]{1,0:T(8,128)(2,1)} %pad_maximum_fusion.kv_ref, s32[256,1]{1,0:T(8,128)} %copy.45.query_len_ref, s32[256,1]{1,0:T(8,128)} %copy.46.query_seg_ref, s32[1,576]{1,0:T(1,128)} %reshape.138.key_pos_ref, ...), custom_call_target="tpu_custom_call" | custom-call | tf_op jit(solution)/shard_map/pallas_call | solution.py:75
  36.7 4.9 %shard_map.140 = f32[64,1152]{1,0:T(8,128)} custom-call(s32[1]{0:T(128)} %bitcast.source_ref, bf16[64,1024]{1,0:T(8,128)(2,1)} %q_ref.1, bf16[576,1024]{1,0:T(8,128)(2,1)} %pad_maximum_fusion.kv_ref, s32[256,1]{1,0:T(8,128)} %copy.45.query_len_ref, s32[256,1]{1,0:T(8,128)} %copy.46.query_seg_ref, s32[1,576]{1,0:T(1,128)} %reshape.138.key_pos_ref, ...), custom_call_target="tpu_custom_call" | custom-call | tf_op jit(solution)/shard_map/pallas_call | solution.py:75
  41.7 0.7 fusion
  42.4 2.5 %collective-permute-done.5 = f32[64,1152]{1,0:T(8,128)S(1)} collective-permute-done((f32[64,1152]{1,0:T(8,128)}, f32[64,1152]{1,0:T(8,128)S(1)}, u32[]{:S(2)}, u32[]{:S(2)}) %collective-permute-start.5) | collective-permute-done | bytes 294944 | tf_op jit(solution)/shard_map/ppermute | solution.py:198
  44.9 0.8 fusion.45
  45.7 0.9 subtract_exponential_fusion
  48.6 2.1 %convolution_convert_fusion = bf16[1024,1024]{1,0:T(8,128)(2,1)} fusion(pred[1024,64]{0,1:T(8,128)(4,1)S(1)} %fusion, f32[64,1024]{1,0:T(8,128)S(1)} %get-tuple-element.7, f32[1024]{0:T(1024)S(1)} %copy-done.8, f32[64]{0:T(128)S(1)} %add_rsqrt_fusion), kind=kOutput, calls=%fused_computation.4 | convolution fusion | flops 135462912 | bytes 2429184 | tf_op jit(solution)/shard_map/dot_general | solution.py:237
  50.7 12.4 %all-to-all-start = ((bf16[64,16,1024]{2,1,0:T(8,128)(2,1)}), bf16[64,16,1024]{2,1,0:T(8,128)(2,1)}, u32[]{:S(2)}, u32[]{:S(2)}) async-start(bf16[64,16,1024]{2,1,0:T(8,128)(2,1)} %bitcast.109), calls=%async_computation | async-start | bytes 4194304 | tf_op jit(solution)/shard_map/all_to_all | solution.py:106
  63.7 50.5 %all-to-all-done = bf16[64,16,1024]{2,1,0:T(8,128)(2,1)} async-done(((bf16[64,16,1024]{2,1,0:T(8,128)(2,1)}), bf16[64,16,1024]{2,1,0:T(8,128)(2,1)}, u32[]{:S(2)}, u32[]{:S(2)}) %all-to-all-start) | async-done | bytes 2097184 | tf_op jit(solution)/shard_map/all_to_all | solution.py:106
  114.3 2.9 %fusion.6 = f32[1024,512]{1,0:T(8,128)S(1)} fusion(bf16[1024,1024]{1,0:T(8,128)(2,1)} %bitcast.25, bf16[1,1024,512]{2,1,0:T(8,128)(2,1)S(1)} %copy-done.10), kind=kOutput, calls=%fused_computation.16 | convolution fusion | flops 1073741824 | bytes 5242880 | tf_op jit(solution)/shard_map/dot_general | solution.py:91
  117.2 0.7 fusion.8
  117.9 3.1 %fusion.4 = f32[1024,512]{1,0:T(8,128)S(1)} fusion(bf16[1024,1024]{1,0:T(8,128)(2,1)} %bitcast.25, bf16[1,1024,512]{2,1,0:T(8,128)(2,1)} %collective-permute-done.6), kind=kOutput, calls=%fused_computation.14 | convolution fusion | flops 1073741824 | bytes 5242880 | tf_op jit(solution)/shard_map/dot_general | solution.py:91
  121.0 3.2 %add_convert_fusion = bf16[1024,1024]{1,0:T(8,128)(2,1)} fusion(bf16[1024,1024]{1,0:T(8,128)(2,1)S(1)} %fusion.8, f32[1024,512]{1,0:T(8,128)S(1)} %fusion.4, bf16[1,256,1024]{2,1,0:T(8,128)(2,1)} %collective-permute-done.7), kind=kOutput, calls=%fused_computation | convolution fusion | flops 543686656 | bytes 6815744 | tf_op jit(solution)/shard_map/dot_general | solution.py:95
  124.3 5.8 %all-to-all-start.1 = ((bf16[64,16,1024]{2,1,0:T(8,128)(2,1)}), bf16[64,16,1024]{2,1,0:T(8,128)(2,1)}, u32[]{:S(2)}, u32[]{:S(2)}) async-start(bf16[64,16,1024]{2,1,0:T(8,128)(2,1)} %bitcast.122), calls=%async_computation.1 | async-start | bytes 4194304 | tf_op jit(solution)/shard_map/all_to_all | solution.py:108
  130.1 0.7 select_reduce_fusion
  130.9 50.3 %all-to-all-done.1 = bf16[64,16,1024]{2,1,0:T(8,128)(2,1)} async-done(((bf16[64,16,1024]{2,1,0:T(8,128)(2,1)}), bf16[64,16,1024]{2,1,0:T(8,128)(2,1)}, u32[]{:S(2)}, u32[]{:S(2)}) %all-to-all-start.1) | async-done | bytes 2097184 | tf_op jit(solution)/shard_map/all_to_all | solution.py:108
  181.2 3.5 %fusion.1 = bf16[64,1024]{1,0:T(8,128)(2,1)} fusion(f32[64,1024]{1,0:T(8,128)S(1)} %get-tuple-element.7, f32[1024,64]{0,1:T(8,128)S(1)} %select_reduce_fusion, bf16[1024,1024]{1,0:T(8,128)(2,1)} %bitcast.31), kind=kOutput, calls=%fused_computation.9 | convolution fusion | flops 805437440 | bytes 2752512 | tf_op jit(solution)/shard_map/dot_general | solution.py:248
  (65 shorter events, 7.3 us)
Async XLA Ops:
  0.6 47.3 %copy-start = (bf16[1024,1024]{1,0:T(8,128)(2,1)S(1)}, bf16[1024,1024]{1,0:T(8,128)(2,1)}, u32[]{:S(2)}) copy-start(bf16[1024,1024]{1,0:T(8,128)(2,1)} %param.20) | copy-start | bytes 6291460
  0.6 16.2 %collective-permute-start = (bf16[64,1024]{1,0:T(8,128)(2,1)}, bf16[64,1024]{1,0:T(8,128)(2,1)S(1)}, u32[]{:S(2)}, u32[]{:S(2)}) collective-permute-start(bf16[64,1024]{1,0:T(8,128)(2,1)} %q_ref.1), channel_id=1, source_target_pairs={{0,1},{1,2},{2,3},{3,0},{4,5},{5,6},{6,7},{7,4},{8,9},{9,10},{10,1... | collective-permute-start | bytes 393224 | tf_op jit(solution)/shard_map/ppermute | solution.py:189
  2.2 28.4 %collective-permute-start.4 = (bf16[64,1024]{1,0:T(8,128)(2,1)}, bf16[64,1024]{1,0:T(8,128)(2,1)S(1)}, u32[]{:S(2)}, u32[]{:S(2)}) collective-permute-start(bf16[64,1024]{1,0:T(8,128)(2,1)} %q_ref.1), channel_id=1, source_target_pairs={{0,3},{1,0},{2,1},{3,2},{4,7},{5,4},{6,5},{7,6},{8,11},{9,8},{10,9... | collective-permute-start | bytes 393224 | tf_op jit(solution)/shard_map/ppermute | solution.py:189
  4.0 19.6 %collective-permute-start.2 = (bf16[64,1024]{1,0:T(8,128)(2,1)}, bf16[64,1024]{1,0:T(8,128)(2,1)S(1)}, u32[]{:S(2)}, u32[]{:S(2)}) collective-permute-start(bf16[64,1024]{1,0:T(8,128)(2,1)} %q_ref.1), channel_id=1, source_target_pairs={{0,2},{1,3},{2,0},{3,1},{4,6},{5,7},{6,4},{7,5},{8,10},{9,11},{10,... | collective-permute-start | bytes 393224 | tf_op jit(solution)/shard_map/ppermute | solution.py:189
  16.9 0.7 copy-start.6
  22.4 14.3 %copy-start.7 = (s32[64,8]{0,1:T(8,128)S(1)}, s32[64,8]{0,1:T(8,128)}, u32[]{:S(2)}) copy-start(s32[64,8]{0,1:T(8,128)} %param.24) | copy-start | bytes 6148
  22.4 20.0 %collective-permute-start.1 = (f32[64,1152]{1,0:T(8,128)}, f32[64,1152]{1,0:T(8,128)S(1)}, u32[]{:S(2)}, u32[]{:S(2)}) collective-permute-start(f32[64,1152]{1,0:T(8,128)} %shard_map.141), channel_id=1, source_target_pairs={{0,3},{1,0},{2,1},{3,2},{4,7},{5,4},{6,5},{7,6},{8,11},{9,8},{10,9... | collective-permute-start | bytes 884744 | tf_op jit(solution)/shard_map/ppermute | solution.py:198
  23.6 0.7 copy-start.5
  29.1 13.3 %collective-permute-start.3 = (f32[64,1152]{1,0:T(8,128)}, f32[64,1152]{1,0:T(8,128)S(1)}, u32[]{:S(2)}, u32[]{:S(2)}) collective-permute-start(f32[64,1152]{1,0:T(8,128)} %shard_map.142), channel_id=1, source_target_pairs={{0,2},{1,3},{2,0},{3,1},{4,6},{5,7},{6,4},{7,5},{8,10},{9,11},{10,... | collective-permute-start | bytes 884744 | tf_op jit(solution)/shard_map/ppermute | solution.py:198
  30.6 0.7 copy-start.4
  36.2 8.8 %collective-permute-start.5 = (f32[64,1152]{1,0:T(8,128)}, f32[64,1152]{1,0:T(8,128)S(1)}, u32[]{:S(2)}, u32[]{:S(2)}) collective-permute-start(f32[64,1152]{1,0:T(8,128)} %shard_map.143), channel_id=1, source_target_pairs={{0,1},{1,2},{2,3},{3,0},{4,5},{5,6},{6,7},{7,4},{8,9},{9,10},{10,1... | collective-permute-start | bytes 884744 | tf_op jit(solution)/shard_map/ppermute | solution.py:198
  41.7 5.9 %copy-start.1 = (f32[64,1152]{1,0:T(8,128)S(1)}, f32[64,1152]{1,0:T(8,128)}, u32[]{:S(2)}) copy-start(f32[64,1152]{1,0:T(8,128)} %shard_map.140) | copy-start | bytes 884740
  46.6 1.4 copy-start.3
  47.6 1.0 copy-start.8
  48.0 2.7 %copy-start.2 = (bf16[64,1024]{1,0:T(8,128)(2,1)}, bf16[64,1024]{1,0:T(8,128)(2,1)S(1)}, u32[]{:S(2)}) copy-start(bf16[64,1024]{1,0:T(8,128)(2,1)S(1)} %fusion.22) | copy-start | bytes 393220
  50.7 12.4 %copy-start.10 = (bf16[1,1024,512]{2,1,0:T(8,128)(2,1)S(1)}, bf16[1,1024,512]{2,1,0:T(8,128)(2,1)}, u32[]{:S(2)}) copy-start(bf16[1,1024,512]{2,1,0:T(8,128)(2,1)} %param.22) | copy-start | bytes 3145732
  50.7 63.6 %all-to-all-start = ((bf16[64,16,1024]{2,1,0:T(8,128)(2,1)}), bf16[64,16,1024]{2,1,0:T(8,128)(2,1)}, u32[]{:S(2)}, u32[]{:S(2)}) async-start(bf16[64,16,1024]{2,1,0:T(8,128)(2,1)} %bitcast.109), calls=%async_computation | async-start | bytes 4194304 | tf_op jit(solution)/shard_map/all_to_all | solution.py:106
  63.1 54.8 %collective-permute-start.6 = (bf16[1,1024,512]{2,1,0:T(8,128)(2,1)S(1)}, bf16[1,1024,512]{2,1,0:T(8,128)(2,1)}, u32[]{:S(2)}, u32[]{:S(2)}) collective-permute-start(bf16[1,1024,512]{2,1,0:T(8,128)(2,1)S(1)} %copy-done.10), channel_id=1, source_target_pairs={{0,4},{4,0},{8,12},{12,8},{16,20},{20,16},{24,28},{28,24},{32,36},... | collective-permute-start | bytes 3145736 | tf_op jit(solution)/shard_map/ppermute | solution.py:136
  63.3 57.7 %collective-permute-start.7 = (bf16[1,256,1024]{2,1,0:T(8,128)(2,1)}, bf16[1,256,1024]{2,1,0:T(8,128)(2,1)}, u32[]{:S(2)}, u32[]{:S(2)}) collective-permute-start(bf16[1,256,1024]{2,1,0:T(8,128)(2,1)} %param.23), channel_id=1, source_target_pairs={{0,4},{4,0},{8,12},{12,8},{16,20},{20,16},{24,28},{28,24},{32,36},... | collective-permute-start | bytes 1572872 | tf_op jit(solution)/shard_map/ppermute | solution.py:137
  114.3 2.9 %copy-start.11 = (bf16[1,256,1024]{2,1,0:T(8,128)(2,1)S(1)}, bf16[1,256,1024]{2,1,0:T(8,128)(2,1)}, u32[]{:S(2)}) copy-start(bf16[1,256,1024]{2,1,0:T(8,128)(2,1)} %param.23) | copy-start | bytes 1572868
  124.3 5.8 %copy-start.9 = (f32[64,8]{0,1:T(8,128)S(1)}, f32[64,8]{0,1:T(8,128)}, u32[]{:S(2)}) copy-start(f32[64,8]{0,1:T(8,128)} %param.25) | copy-start | bytes 6148
  124.3 56.9 %all-to-all-start.1 = ((bf16[64,16,1024]{2,1,0:T(8,128)(2,1)}), bf16[64,16,1024]{2,1,0:T(8,128)(2,1)}, u32[]{:S(2)}, u32[]{:S(2)}) async-start(bf16[64,16,1024]{2,1,0:T(8,128)(2,1)} %bitcast.122), calls=%async_computation.1 | async-start | bytes 4194304 | tf_op jit(solution)/shard_map/all_to_all | solution.py:108

commit v8 on v7

--- a/solution.py
+++ b/solution.py
@@ -31,40 +31,44 @@
     shown = (key_pos < query_len) | (
         (key_seg_ref[...] == query_seg) & (key_pos - FRESH_BASE <= query_order)
     )
-    visible = jnp.concatenate([shown, shown], axis=0)
     lane = lax.broadcasted_iota(jnp.int32, (rows, 128), 1)
     low_half = lane < HEAD_SIZE
     stats = jnp.zeros((rows, 128), jnp.float32)
-    for h in range(KEY_VALUE_HEADS):
-        q_tile = q_ref[:, h * 128:(h + 1) * 128].astype(jnp.float32)
-        k_tile = kv_ref[:, (h // 2) * 128:(h // 2 + 1) * 128]
-        v_start = KEY_VALUE_HEADS * HEAD_SIZE + (h // 2) * 128
+    heads_per_tile = 128 // HEAD_SIZE
+    visible = jnp.concatenate([shown] * (2 * heads_per_tile), axis=0)
+    for t in range(KEY_VALUE_HEADS // heads_per_tile):
+        k_tile = kv_ref[:, t * 128:(t + 1) * 128]
+        v_start = KEY_VALUE_HEADS * HEAD_SIZE + t * 128
         v_tile = kv_ref[:, v_start:v_start + 128]
-        halves = []
-        for g in range(2):
-            q_half = jnp.where(low_half if g == 0 else ~low_half, q_tile, 0.0)
-            if g != h % 2:
-                q_half = pltpu.roll(q_half, HEAD_SIZE, 1)
-            halves.append(q_half)
-        q_pair = jnp.concatenate(halves, axis=0).astype(jnp.bfloat16)
+        pieces = []
+        for h in range(t * heads_per_tile, (t + 1) * heads_per_tile):
+            q_tile = q_ref[:, h * 128:(h + 1) * 128].astype(jnp.float32)
+            for g in range(2):
+                q_half = jnp.where(low_half if g == 0 else ~low_half, q_tile, 0.0)
+                if g != h % 2:
+                    q_half = pltpu.roll(q_half, HEAD_SIZE, 1)
+                pieces.append(q_half)
+        q_stack = jnp.concatenate(pieces, axis=0).astype(jnp.bfloat16)
         scores = lax.dot_general(
-            q_pair, k_tile, (((1,), (1,)), ((), ())), preferred_element_type=jnp.float32
+            q_stack, k_tile, (((1,), (1,)), ((), ())), preferred_element_type=jnp.float32
         ) * score_scale
         scores = jnp.where(visible, scores, masked_filler)
         highest = jnp.max(scores, axis=1, keepdims=True)
         weights = jnp.where(visible, jnp.exp(scores - highest), 0.0)
         total = jnp.sum(weights, axis=1, keepdims=True)
         acc = jnp.dot(weights.astype(jnp.bfloat16), v_tile, preferred_element_type=jnp.float32)
-        out_tile = jnp.zeros((rows, 128), jnp.float32)
-        for g in range(2):
-            part = acc[g * rows:(g + 1) * rows]
-            if g != h % 2:
-                part = pltpu.roll(part, HEAD_SIZE, 1)
-            out_tile = jnp.where(low_half if g == 0 else ~low_half, part, out_tile)
-            j = 2 * h + g
-            stats = jnp.where(lane == j, highest[g * rows:(g + 1) * rows], stats)
-            stats = jnp.where(lane == QUERY_HEADS + j, total[g * rows:(g + 1) * rows], stats)
-        out_ref[:, h * 128:(h + 1) * 128] = out_tile
+        for local, h in enumerate(range(t * heads_per_tile, (t + 1) * heads_per_tile)):
+            out_tile = jnp.zeros((rows, 128), jnp.float32)
+            for g in range(2):
+                at = (2 * local + g) * rows
+                part = acc[at:at + rows]
+                if g != h % 2:
+                    part = pltpu.roll(part, HEAD_SIZE, 1)
+                out_tile = jnp.where(low_half if g == 0 else ~low_half, part, out_tile)
+                j = 2 * h + g
+                stats = jnp.where(lane == j, highest[at:at + rows], stats)
+                stats = jnp.where(lane == QUERY_HEADS + j, total[at:at + rows], stats)
+            out_ref[:, h * 128:(h + 1) * 128] = out_tile
     out_ref[:, QUERY_HEADS * HEAD_SIZE:QUERY_HEADS * HEAD_SIZE + 128] = stats
 
 

time: 185 us -> 184 us (level)
  Pallas kernels: 19.6 us -> 16.3 us
  waiting for transfers between devices: 103 us -> 105 us
    pallas_call x4, Pallas kernels: 19.6 us -> 16.3 us  [attend_partial(): pl.pallas_call(_attend_kernel, out_shape=jax.ShapeDtypeStruct((rows, QUER...]
  transfers between devices with their start and end apart: 10 -> 10, of which waited for: 3 -> 3; matrix products, arithmetic and copies ran while one was open for 10% -> 11% of each run, Pallas kernels for 11% -> 9%
where the time goes in v8:
time: 184 us; the launch traced here: 183 us
  waiting for transfers between devices  105 us (57%)
  starting transfers between devices  27 us (15%)
  matrix products  17.4 us (9%)
  Pallas kernels  16.3 us (9%)
  other arithmetic  8.51 us (5%)
  local copies, waits for them, and re-layouts  7.79 us (4%)
    all_to_all x1, waiting for transfers between devices, direct_dispatch(): lax.all_to_all(unit_rows, 'tok', split_axis=0, concat_axis=0, tiled=True)  50.5 us
    all_to_all x1, waiting for transfers between devices, direct_dispatch(): lax.all_to_all(produced.reshape(EXPERTS * split, CAP // split, width), 't...  50.3 us
    pallas_call x4, Pallas kernels, attend_partial(): pl.pallas_call(_attend_kernel, out_shape=jax.ShapeDtypeStruct((rows, QUER...  16.3 us
    all_to_all x1, starting transfers between devices, direct_dispatch(): lax.all_to_all(unit_rows, 'tok', split_axis=0, concat_axis=0, tiled=True)  12.4 us
    dot_general x2, matrix products, pair_ffn(): jnp.dot(rows_in, gate_up_pair[part], preferred_element_type=jnp.float32)  5.99 us
    all_to_all x1, starting transfers between devices, direct_dispatch(): lax.all_to_all(produced.reshape(EXPERTS * split, CAP // split, width), 't...  5.76 us
    ppermute x3, starting transfers between devices, body(): lax.ppermute(queries, 'pool', [(i, (i + shift) % pool_size) for i in rang...  5.13 us
    ppermute x3, waiting for transfers between devices, body(): lax.ppermute(partial, 'pool', [(i, (i - shift) % pool_size) for i in rang...  4.01 us
  transfers between devices with their start and end apart: 10, of which 3 were waited for; matrix products, arithmetic and copies ran while one was open for 11% of the time, Pallas kernels for 9%

profile of v8, /device:TPU:8, one launch (start us, length us, event | category | flops | bytes accessed | tf_op | source)
XLA Modules:
  0.0 182.8 jit_solution(13887617721733306195)
XLA Ops:
  0.6 1.6 collective-permute-start
  2.2 1.7 collective-permute-start.4
  4.0 1.8 collective-permute-start.2
  5.8 0.8 select_reduce_fusion.1
  6.6 0.8 copy.53
  8.4 0.7 dynamic-slice_bitcast_fusion
  9.7 1.2 reduce-window.6
  11.4 0.8 select_reduce_fusion.2
  12.2 0.8 copy.45.query_len_ref
  13.0 1.5 copy.46.query_seg_ref
  14.5 2.4 %pad_maximum_fusion.kv_ref = bf16[576,1024]{1,0:T(8,128)(2,1)} fusion(bf16[64,1024]{1,0:T(8,128)(2,1)} %param.15, bf16[512,1024]{1,0:T(8,128)(2,1)} %bitcast.123), kind=kLoop, calls=%fused_computation.5 | loop fusion | flops 2359296 | bytes 2359296 | tf_op jit(solution)/shard_map/concatenate | solution.py:173
  17.5 4.1 %shard_map.141 = f32[64,1152]{1,0:T(8,128)} custom-call(s32[1]{0:T(128)} %bitcast.10.source_ref, bf16[64,1024]{1,0:T(8,128)(2,1)} %copy-done.6, bf16[576,1024]{1,0:T(8,128)(2,1)} %pad_maximum_fusion.kv_ref, s32[256,1]{1,0:T(8,128)} %copy.45.query_len_ref, s32[256,1]{1,0:T(8,128)} %copy.46.query_seg_ref, s32[1,576]{1,0:T(1,128)} %reshape.138.key_pos_ref, ...), custom_call_target="tpu_custom_call" | custom-call | tf_op jit(solution)/shard_map/pallas_call | solution.py:79
  21.6 1.1 collective-permute-start.1
  23.4 4.1 %shard_map.142 = f32[64,1152]{1,0:T(8,128)} custom-call(s32[1]{0:T(128)} %bitcast.12.source_ref, bf16[64,1024]{1,0:T(8,128)(2,1)} %copy-done.5, bf16[576,1024]{1,0:T(8,128)(2,1)} %pad_maximum_fusion.kv_ref, s32[256,1]{1,0:T(8,128)} %copy.45.query_len_ref, s32[256,1]{1,0:T(8,128)} %copy.46.query_seg_ref, s32[1,576]{1,0:T(1,128)} %reshape.138.key_pos_ref, ...), custom_call_target="tpu_custom_call" | custom-call | tf_op jit(solution)/shard_map/pallas_call | solution.py:79
  27.5 1.5 collective-permute-start.3
  29.6 4.1 %shard_map.143 = f32[64,1152]{1,0:T(8,128)} custom-call(s32[1]{0:T(128)} %bitcast.14.source_ref, bf16[64,1024]{1,0:T(8,128)(2,1)} %copy-done.4, bf16[576,1024]{1,0:T(8,128)(2,1)} %pad_maximum_fusion.kv_ref, s32[256,1]{1,0:T(8,128)} %copy.45.query_len_ref, s32[256,1]{1,0:T(8,128)} %copy.46.query_seg_ref, s32[1,576]{1,0:T(1,128)} %reshape.138.key_pos_ref, ...), custom_call_target="tpu_custom_call" | custom-call | tf_op jit(solution)/shard_map/pallas_call | solution.py:79
  34.3 4.1 %shard_map.140 = f32[64,1152]{1,0:T(8,128)} custom-call(s32[1]{0:T(128)} %bitcast.source_ref, bf16[64,1024]{1,0:T(8,128)(2,1)} %q_ref.1, bf16[576,1024]{1,0:T(8,128)(2,1)} %pad_maximum_fusion.kv_ref, s32[256,1]{1,0:T(8,128)} %copy.45.query_len_ref, s32[256,1]{1,0:T(8,128)} %copy.46.query_seg_ref, s32[1,576]{1,0:T(1,128)} %reshape.138.key_pos_ref, ...), custom_call_target="tpu_custom_call" | custom-call | tf_op jit(solution)/shard_map/pallas_call | solution.py:79
  38.4 0.7 fusion
  39.1 4.0 %collective-permute-done.5 = f32[64,1152]{1,0:T(8,128)S(1)} collective-permute-done((f32[64,1152]{1,0:T(8,128)}, f32[64,1152]{1,0:T(8,128)S(1)}, u32[]{:S(2)}, u32[]{:S(2)}) %collective-permute-start.5) | collective-permute-done | bytes 294944 | tf_op jit(solution)/shard_map/ppermute | solution.py:202
  43.1 0.8 fusion.45
  43.9 0.9 subtract_exponential_fusion
  46.8 2.1 %convolution_convert_fusion = bf16[1024,1024]{1,0:T(8,128)(2,1)} fusion(pred[1024,64]{0,1:T(8,128)(4,1)S(1)} %fusion, f32[64,1024]{1,0:T(8,128)S(1)} %get-tuple-element.7, f32[1024]{0:T(1024)S(1)} %copy-done.8, f32[64]{0:T(128)S(1)} %add_rsqrt_fusion), kind=kOutput, calls=%fused_computation.4 | convolution fusion | flops 135462912 | bytes 2429184 | tf_op jit(solution)/shard_map/dot_general | solution.py:241
  48.9 12.4 %all-to-all-start = ((bf16[64,16,1024]{2,1,0:T(8,128)(2,1)}), bf16[64,16,1024]{2,1,0:T(8,128)(2,1)}, u32[]{:S(2)}, u32[]{:S(2)}) async-start(bf16[64,16,1024]{2,1,0:T(8,128)(2,1)} %bitcast.109), calls=%async_computation | async-start | bytes 4194304 | tf_op jit(solution)/shard_map/all_to_all | solution.py:110
  61.9 50.5 %all-to-all-done = bf16[64,16,1024]{2,1,0:T(8,128)(2,1)} async-done(((bf16[64,16,1024]{2,1,0:T(8,128)(2,1)}), bf16[64,16,1024]{2,1,0:T(8,128)(2,1)}, u32[]{:S(2)}, u32[]{:S(2)}) %all-to-all-start) | async-done | bytes 2097184 | tf_op jit(solution)/shard_map/all_to_all | solution.py:110
  112.4 2.9 %fusion.6 = f32[1024,512]{1,0:T(8,128)S(1)} fusion(bf16[1024,1024]{1,0:T(8,128)(2,1)} %bitcast.25, bf16[1,1024,512]{2,1,0:T(8,128)(2,1)S(1)} %copy-done.10), kind=kOutput, calls=%fused_computation.16 | convolution fusion | flops 1073741824 | bytes 5242880 | tf_op jit(solution)/shard_map/dot_general | solution.py:95
  115.3 0.7 fusion.8
  116.1 3.1 %fusion.4 = f32[1024,512]{1,0:T(8,128)S(1)} fusion(bf16[1024,1024]{1,0:T(8,128)(2,1)} %bitcast.25, bf16[1,1024,512]{2,1,0:T(8,128)(2,1)} %collective-permute-done.6), kind=kOutput, calls=%fused_computation.14 | convolution fusion | flops 1073741824 | bytes 5242880 | tf_op jit(solution)/shard_map/dot_general | solution.py:95
  119.2 3.2 %add_convert_fusion = bf16[1024,1024]{1,0:T(8,128)(2,1)} fusion(bf16[1024,1024]{1,0:T(8,128)(2,1)S(1)} %fusion.8, f32[1024,512]{1,0:T(8,128)S(1)} %fusion.4, bf16[1,256,1024]{2,1,0:T(8,128)(2,1)} %collective-permute-done.7), kind=kOutput, calls=%fused_computation | convolution fusion | flops 543686656 | bytes 6815744 | tf_op jit(solution)/shard_map/dot_general | solution.py:99
  122.5 5.8 %all-to-all-start.1 = ((bf16[64,16,1024]{2,1,0:T(8,128)(2,1)}), bf16[64,16,1024]{2,1,0:T(8,128)(2,1)}, u32[]{:S(2)}, u32[]{:S(2)}) async-start(bf16[64,16,1024]{2,1,0:T(8,128)(2,1)} %bitcast.122), calls=%async_computation.1 | async-start | bytes 4194304 | tf_op jit(solution)/shard_map/all_to_all | solution.py:112
  128.3 0.7 select_reduce_fusion
  129.0 50.3 %all-to-all-done.1 = bf16[64,16,1024]{2,1,0:T(8,128)(2,1)} async-done(((bf16[64,16,1024]{2,1,0:T(8,128)(2,1)}), bf16[64,16,1024]{2,1,0:T(8,128)(2,1)}, u32[]{:S(2)}, u32[]{:S(2)}) %all-to-all-start.1) | async-done | bytes 2097184 | tf_op jit(solution)/shard_map/all_to_all | solution.py:112
  179.4 3.5 %fusion.1 = bf16[64,1024]{1,0:T(8,128)(2,1)} fusion(f32[64,1024]{1,0:T(8,128)S(1)} %get-tuple-element.7, f32[1024,64]{0,1:T(8,128)S(1)} %select_reduce_fusion, bf16[1024,1024]{1,0:T(8,128)(2,1)} %bitcast.31), kind=kOutput, calls=%fused_computation.9 | convolution fusion | flops 805437440 | bytes 2752512 | tf_op jit(solution)/shard_map/dot_general | solution.py:252
  (65 shorter events, 7.3 us)
Async XLA Ops:
  0.6 45.5 %copy-start = (bf16[1024,1024]{1,0:T(8,128)(2,1)S(1)}, bf16[1024,1024]{1,0:T(8,128)(2,1)}, u32[]{:S(2)}) copy-start(bf16[1024,1024]{1,0:T(8,128)(2,1)} %param.20) | copy-start | bytes 6291460
  0.6 16.2 %collective-permute-start = (bf16[64,1024]{1,0:T(8,128)(2,1)}, bf16[64,1024]{1,0:T(8,128)(2,1)S(1)}, u32[]{:S(2)}, u32[]{:S(2)}) collective-permute-start(bf16[64,1024]{1,0:T(8,128)(2,1)} %q_ref.1), channel_id=1, source_target_pairs={{0,1},{1,2},{2,3},{3,0},{4,5},{5,6},{6,7},{7,4},{8,9},{9,10},{10,1... | collective-permute-start | bytes 393224 | tf_op jit(solution)/shard_map/ppermute | solution.py:193
  2.2 26.8 %collective-permute-start.4 = (bf16[64,1024]{1,0:T(8,128)(2,1)}, bf16[64,1024]{1,0:T(8,128)(2,1)S(1)}, u32[]{:S(2)}, u32[]{:S(2)}) collective-permute-start(bf16[64,1024]{1,0:T(8,128)(2,1)} %q_ref.1), channel_id=1, source_target_pairs={{0,3},{1,0},{2,1},{3,2},{4,7},{5,4},{6,5},{7,6},{8,11},{9,8},{10,9... | collective-permute-start | bytes 393224 | tf_op jit(solution)/shard_map/ppermute | solution.py:193
  4.0 18.8 %collective-permute-start.2 = (bf16[64,1024]{1,0:T(8,128)(2,1)}, bf16[64,1024]{1,0:T(8,128)(2,1)S(1)}, u32[]{:S(2)}, u32[]{:S(2)}) collective-permute-start(bf16[64,1024]{1,0:T(8,128)(2,1)} %q_ref.1), channel_id=1, source_target_pairs={{0,2},{1,3},{2,0},{3,1},{4,6},{5,7},{6,4},{7,5},{8,10},{9,11},{10,... | collective-permute-start | bytes 393224 | tf_op jit(solution)/shard_map/ppermute | solution.py:193
  16.9 0.7 copy-start.6
  21.6 12.6 %copy-start.7 = (s32[64,8]{0,1:T(8,128)S(1)}, s32[64,8]{0,1:T(8,128)}, u32[]{:S(2)}) copy-start(s32[64,8]{0,1:T(8,128)} %param.24) | copy-start | bytes 6148
  21.6 17.5 %collective-permute-start.1 = (f32[64,1152]{1,0:T(8,128)}, f32[64,1152]{1,0:T(8,128)S(1)}, u32[]{:S(2)}, u32[]{:S(2)}) collective-permute-start(f32[64,1152]{1,0:T(8,128)} %shard_map.141), channel_id=1, source_target_pairs={{0,3},{1,0},{2,1},{3,2},{4,7},{5,4},{6,5},{7,6},{8,11},{9,8},{10,9... | collective-permute-start | bytes 884744 | tf_op jit(solution)/shard_map/ppermute | solution.py:202
  22.7 0.7 copy-start.5
  27.5 11.6 %collective-permute-start.3 = (f32[64,1152]{1,0:T(8,128)}, f32[64,1152]{1,0:T(8,128)S(1)}, u32[]{:S(2)}, u32[]{:S(2)}) collective-permute-start(f32[64,1152]{1,0:T(8,128)} %shard_map.142), channel_id=1, source_target_pairs={{0,2},{1,3},{2,0},{3,1},{4,6},{5,7},{6,4},{7,5},{8,10},{9,11},{10,... | collective-permute-start | bytes 884744 | tf_op jit(solution)/shard_map/ppermute | solution.py:202
  29.0 0.7 copy-start.4
  33.7 9.4 %collective-permute-start.5 = (f32[64,1152]{1,0:T(8,128)}, f32[64,1152]{1,0:T(8,128)S(1)}, u32[]{:S(2)}, u32[]{:S(2)}) collective-permute-start(f32[64,1152]{1,0:T(8,128)} %shard_map.143), channel_id=1, source_target_pairs={{0,1},{1,2},{2,3},{3,0},{4,5},{5,6},{6,7},{7,4},{8,9},{9,10},{10,1... | collective-permute-start | bytes 884744 | tf_op jit(solution)/shard_map/ppermute | solution.py:202
  38.4 7.4 %copy-start.1 = (f32[64,1152]{1,0:T(8,128)S(1)}, f32[64,1152]{1,0:T(8,128)}, u32[]{:S(2)}) copy-start(f32[64,1152]{1,0:T(8,128)} %shard_map.140) | copy-start | bytes 884740
  44.8 1.4 copy-start.3
  45.8 1.0 copy-start.8
  46.1 2.7 %copy-start.2 = (bf16[64,1024]{1,0:T(8,128)(2,1)}, bf16[64,1024]{1,0:T(8,128)(2,1)S(1)}, u32[]{:S(2)}) copy-start(bf16[64,1024]{1,0:T(8,128)(2,1)S(1)} %fusion.22) | copy-start | bytes 393220
  48.9 12.4 %copy-start.10 = (bf16[1,1024,512]{2,1,0:T(8,128)(2,1)S(1)}, bf16[1,1024,512]{2,1,0:T(8,128)(2,1)}, u32[]{:S(2)}) copy-start(bf16[1,1024,512]{2,1,0:T(8,128)(2,1)} %param.22) | copy-start | bytes 3145732
  48.9 63.6 %all-to-all-start = ((bf16[64,16,1024]{2,1,0:T(8,128)(2,1)}), bf16[64,16,1024]{2,1,0:T(8,128)(2,1)}, u32[]{:S(2)}, u32[]{:S(2)}) async-start(bf16[64,16,1024]{2,1,0:T(8,128)(2,1)} %bitcast.109), calls=%async_computation | async-start | bytes 4194304 | tf_op jit(solution)/shard_map/all_to_all | solution.py:110
  61.3 54.8 %collective-permute-start.6 = (bf16[1,1024,512]{2,1,0:T(8,128)(2,1)S(1)}, bf16[1,1024,512]{2,1,0:T(8,128)(2,1)}, u32[]{:S(2)}, u32[]{:S(2)}) collective-permute-start(bf16[1,1024,512]{2,1,0:T(8,128)(2,1)S(1)} %copy-done.10), channel_id=1, source_target_pairs={{0,4},{4,0},{8,12},{12,8},{16,20},{20,16},{24,28},{28,24},{32,36},... | collective-permute-start | bytes 3145736 | tf_op jit(solution)/shard_map/ppermute | solution.py:140
  61.5 57.7 %collective-permute-start.7 = (bf16[1,256,1024]{2,1,0:T(8,128)(2,1)}, bf16[1,256,1024]{2,1,0:T(8,128)(2,1)}, u32[]{:S(2)}, u32[]{:S(2)}) collective-permute-start(bf16[1,256,1024]{2,1,0:T(8,128)(2,1)} %param.23), channel_id=1, source_target_pairs={{0,4},{4,0},{8,12},{12,8},{16,20},{20,16},{24,28},{28,24},{32,36},... | collective-permute-start | bytes 1572872 | tf_op jit(solution)/shard_map/ppermute | solution.py:141
  112.4 2.9 %copy-start.11 = (bf16[1,256,1024]{2,1,0:T(8,128)(2,1)S(1)}, bf16[1,256,1024]{2,1,0:T(8,128)(2,1)}, u32[]{:S(2)}) copy-start(bf16[1,256,1024]{2,1,0:T(8,128)(2,1)} %param.23) | copy-start | bytes 1572868
  122.5 5.8 %copy-start.9 = (f32[64,8]{0,1:T(8,128)S(1)}, f32[64,8]{0,1:T(8,128)}, u32[]{:S(2)}) copy-start(f32[64,8]{0,1:T(8,128)} %param.25) | copy-start | bytes 6148
  122.5 56.9 %all-to-all-start.1 = ((bf16[64,16,1024]{2,1,0:T(8,128)(2,1)}), bf16[64,16,1024]{2,1,0:T(8,128)(2,1)}, u32[]{:S(2)}, u32[]{:S(2)}) async-start(bf16[64,16,1024]{2,1,0:T(8,128)(2,1)} %bitcast.122), calls=%async_computation.1 | async-start | bytes 4194304 | tf_op jit(solution)/shard_map/all_to_all | solution.py:112

commit v9 on v8

--- a/solution.py
+++ b/solution.py
@@ -196,7 +196,7 @@
         for shift in shifts[1:]
     ]
     partials = [None] * pool_size
-    for shift in list(shifts[1:]) + [0]:
+    for shift in ring_order(pool_size):
         partial = attend_block(query_blocks[shift], (pool_idx - shift) % pool_size)
         if shift:
             partial = lax.ppermute(
@@ -259,6 +259,11 @@
     return (attended, layer_out)
 
 
+def ring_order(pool_size):
+    farthest = pool_size // 2
+    return [farthest] + [s for s in range(1, pool_size) if s != farthest] + [0]
+
+
 def solution(mesh):
     placed = (
         P(("tok", "pool"), None),

time: 184 us -> 184 us (level)
  no operation moved by 1% of the time
where the time goes in v9:
time: 184 us; the launch traced here: 183 us
  waiting for transfers between devices  105 us (57%)
  starting transfers between devices  27 us (15%)
  matrix products  17.4 us (9%)
  Pallas kernels  16.3 us (9%)
  other arithmetic  8.51 us (5%)
  local copies, waits for them, and re-layouts  7.79 us (4%)
    all_to_all x1, waiting for transfers between devices, direct_dispatch(): lax.all_to_all(unit_rows, 'tok', split_axis=0, concat_axis=0, tiled=True)  50.5 us
    all_to_all x1, waiting for transfers between devices, direct_dispatch(): lax.all_to_all(produced.reshape(EXPERTS * split, CAP // split, width), 't...  50.3 us
    pallas_call x4, Pallas kernels, attend_partial(): pl.pallas_call(_attend_kernel, out_shape=jax.ShapeDtypeStruct((rows, QUER...  16.3 us
    all_to_all x1, starting transfers between devices, direct_dispatch(): lax.all_to_all(unit_rows, 'tok', split_axis=0, concat_axis=0, tiled=True)  12.4 us
    dot_general x2, matrix products, pair_ffn(): jnp.dot(rows_in, gate_up_pair[part], preferred_element_type=jnp.float32)  5.99 us
    all_to_all x1, starting transfers between devices, direct_dispatch(): lax.all_to_all(produced.reshape(EXPERTS * split, CAP // split, width), 't...  5.76 us
    ppermute x3, starting transfers between devices, body(): lax.ppermute(queries, 'pool', [(i, (i + shift) % pool_size) for i in rang...  5.13 us
    ppermute x3, waiting for transfers between devices, body(): lax.ppermute(partial, 'pool', [(i, (i - shift) % pool_size) for i in rang...  4.01 us
  transfers between devices with their start and end apart: 10, of which 3 were waited for; matrix products, arithmetic and copies ran while one was open for 11% of the time, Pallas kernels for 9%

profile of v9, /device:TPU:8, one launch (start us, length us, event | category | flops | bytes accessed | tf_op | source)
XLA Modules:
  0.0 182.8 jit_solution(13887617721733306195)
XLA Ops:
  0.6 1.6 collective-permute-start
  2.2 1.7 collective-permute-start.4
  4.0 1.8 collective-permute-start.2
  5.8 0.8 select_reduce_fusion.1
  6.6 0.8 copy.53
  8.4 0.7 dynamic-slice_bitcast_fusion
  9.7 1.2 reduce-window.6
  11.4 0.8 select_reduce_fusion.2
  12.2 0.8 copy.45.query_len_ref
  13.0 1.5 copy.46.query_seg_ref
  14.5 2.4 %pad_maximum_fusion.kv_ref = bf16[576,1024]{1,0:T(8,128)(2,1)} fusion(bf16[64,1024]{1,0:T(8,128)(2,1)} %param.15, bf16[512,1024]{1,0:T(8,128)(2,1)} %bitcast.123), kind=kLoop, calls=%fused_computation.5 | loop fusion | flops 2359296 | bytes 2359296 | tf_op jit(solution)/shard_map/concatenate | solution.py:173
  17.5 4.1 %shard_map.141 = f32[64,1152]{1,0:T(8,128)} custom-call(s32[1]{0:T(128)} %bitcast.10.source_ref, bf16[64,1024]{1,0:T(8,128)(2,1)} %copy-done.6, bf16[576,1024]{1,0:T(8,128)(2,1)} %pad_maximum_fusion.kv_ref, s32[256,1]{1,0:T(8,128)} %copy.45.query_len_ref, s32[256,1]{1,0:T(8,128)} %copy.46.query_seg_ref, s32[1,576]{1,0:T(1,128)} %reshape.138.key_pos_ref, ...), custom_call_target="tpu_custom_call" | custom-call | tf_op jit(solution)/shard_map/pallas_call | solution.py:79
  21.6 1.1 collective-permute-start.1
  23.4 4.1 %shard_map.142 = f32[64,1152]{1,0:T(8,128)} custom-call(s32[1]{0:T(128)} %bitcast.12.source_ref, bf16[64,1024]{1,0:T(8,128)(2,1)} %copy-done.5, bf16[576,1024]{1,0:T(8,128)(2,1)} %pad_maximum_fusion.kv_ref, s32[256,1]{1,0:T(8,128)} %copy.45.query_len_ref, s32[256,1]{1,0:T(8,128)} %copy.46.query_seg_ref, s32[1,576]{1,0:T(1,128)} %reshape.138.key_pos_ref, ...), custom_call_target="tpu_custom_call" | custom-call | tf_op jit(solution)/shard_map/pallas_call | solution.py:79
  27.5 1.5 collective-permute-start.3
  29.6 4.1 %shard_map.143 = f32[64,1152]{1,0:T(8,128)} custom-call(s32[1]{0:T(128)} %bitcast.14.source_ref, bf16[64,1024]{1,0:T(8,128)(2,1)} %copy-done.4, bf16[576,1024]{1,0:T(8,128)(2,1)} %pad_maximum_fusion.kv_ref, s32[256,1]{1,0:T(8,128)} %copy.45.query_len_ref, s32[256,1]{1,0:T(8,128)} %copy.46.query_seg_ref, s32[1,576]{1,0:T(1,128)} %reshape.138.key_pos_ref, ...), custom_call_target="tpu_custom_call" | custom-call | tf_op jit(solution)/shard_map/pallas_call | solution.py:79
  34.3 4.1 %shard_map.140 = f32[64,1152]{1,0:T(8,128)} custom-call(s32[1]{0:T(128)} %bitcast.source_ref, bf16[64,1024]{1,0:T(8,128)(2,1)} %q_ref.1, bf16[576,1024]{1,0:T(8,128)(2,1)} %pad_maximum_fusion.kv_ref, s32[256,1]{1,0:T(8,128)} %copy.45.query_len_ref, s32[256,1]{1,0:T(8,128)} %copy.46.query_seg_ref, s32[1,576]{1,0:T(1,128)} %reshape.138.key_pos_ref, ...), custom_call_target="tpu_custom_call" | custom-call | tf_op jit(solution)/shard_map/pallas_call | solution.py:79
  38.4 0.7 fusion
  39.1 4.0 %collective-permute-done.5 = f32[64,1152]{1,0:T(8,128)S(1)} collective-permute-done((f32[64,1152]{1,0:T(8,128)}, f32[64,1152]{1,0:T(8,128)S(1)}, u32[]{:S(2)}, u32[]{:S(2)}) %collective-permute-start.5) | collective-permute-done | bytes 294944 | tf_op jit(solution)/shard_map/ppermute | solution.py:202
  43.1 0.8 fusion.45
  43.9 0.9 subtract_exponential_fusion
  46.8 2.1 %convolution_convert_fusion = bf16[1024,1024]{1,0:T(8,128)(2,1)} fusion(pred[1024,64]{0,1:T(8,128)(4,1)S(1)} %fusion, f32[64,1024]{1,0:T(8,128)S(1)} %get-tuple-element.7, f32[1024]{0:T(1024)S(1)} %copy-done.8, f32[64]{0:T(128)S(1)} %add_rsqrt_fusion), kind=kOutput, calls=%fused_computation.4 | convolution fusion | flops 135462912 | bytes 2429184 | tf_op jit(solution)/shard_map/dot_general | solution.py:241
  48.9 12.4 %all-to-all-start = ((bf16[64,16,1024]{2,1,0:T(8,128)(2,1)}), bf16[64,16,1024]{2,1,0:T(8,128)(2,1)}, u32[]{:S(2)}, u32[]{:S(2)}) async-start(bf16[64,16,1024]{2,1,0:T(8,128)(2,1)} %bitcast.109), calls=%async_computation | async-start | bytes 4194304 | tf_op jit(solution)/shard_map/all_to_all | solution.py:110
  61.9 50.5 %all-to-all-done = bf16[64,16,1024]{2,1,0:T(8,128)(2,1)} async-done(((bf16[64,16,1024]{2,1,0:T(8,128)(2,1)}), bf16[64,16,1024]{2,1,0:T(8,128)(2,1)}, u32[]{:S(2)}, u32[]{:S(2)}) %all-to-all-start) | async-done | bytes 2097184 | tf_op jit(solution)/shard_map/all_to_all | solution.py:110
  112.4 2.9 %fusion.6 = f32[1024,512]{1,0:T(8,128)S(1)} fusion(bf16[1024,1024]{1,0:T(8,128)(2,1)} %bitcast.25, bf16[1,1024,512]{2,1,0:T(8,128)(2,1)S(1)} %copy-done.10), kind=kOutput, calls=%fused_computation.16 | convolution fusion | flops 1073741824 | bytes 5242880 | tf_op jit(solution)/shard_map/dot_general | solution.py:95
  115.3 0.7 fusion.8
  116.1 3.1 %fusion.4 = f32[1024,512]{1,0:T(8,128)S(1)} fusion(bf16[1024,1024]{1,0:T(8,128)(2,1)} %bitcast.25, bf16[1,1024,512]{2,1,0:T(8,128)(2,1)} %collective-permute-done.6), kind=kOutput, calls=%fused_computation.14 | convolution fusion | flops 1073741824 | bytes 5242880 | tf_op jit(solution)/shard_map/dot_general | solution.py:95
  119.2 3.2 %add_convert_fusion = bf16[1024,1024]{1,0:T(8,128)(2,1)} fusion(bf16[1024,1024]{1,0:T(8,128)(2,1)S(1)} %fusion.8, f32[1024,512]{1,0:T(8,128)S(1)} %fusion.4, bf16[1,256,1024]{2,1,0:T(8,128)(2,1)} %collective-permute-done.7), kind=kOutput, calls=%fused_computation | convolution fusion | flops 543686656 | bytes 6815744 | tf_op jit(solution)/shard_map/dot_general | solution.py:99
  122.5 5.8 %all-to-all-start.1 = ((bf16[64,16,1024]{2,1,0:T(8,128)(2,1)}), bf16[64,16,1024]{2,1,0:T(8,128)(2,1)}, u32[]{:S(2)}, u32[]{:S(2)}) async-start(bf16[64,16,1024]{2,1,0:T(8,128)(2,1)} %bitcast.122), calls=%async_computation.1 | async-start | bytes 4194304 | tf_op jit(solution)/shard_map/all_to_all | solution.py:112
  128.3 0.7 select_reduce_fusion
  129.0 50.3 %all-to-all-done.1 = bf16[64,16,1024]{2,1,0:T(8,128)(2,1)} async-done(((bf16[64,16,1024]{2,1,0:T(8,128)(2,1)}), bf16[64,16,1024]{2,1,0:T(8,128)(2,1)}, u32[]{:S(2)}, u32[]{:S(2)}) %all-to-all-start.1) | async-done | bytes 2097184 | tf_op jit(solution)/shard_map/all_to_all | solution.py:112
  179.4 3.5 %fusion.1 = bf16[64,1024]{1,0:T(8,128)(2,1)} fusion(f32[64,1024]{1,0:T(8,128)S(1)} %get-tuple-element.7, f32[1024,64]{0,1:T(8,128)S(1)} %select_reduce_fusion, bf16[1024,1024]{1,0:T(8,128)(2,1)} %bitcast.31), kind=kOutput, calls=%fused_computation.9 | convolution fusion | flops 805437440 | bytes 2752512 | tf_op jit(solution)/shard_map/dot_general | solution.py:252
  (65 shorter events, 7.3 us)
Async XLA Ops:
  0.6 45.5 %copy-start = (bf16[1024,1024]{1,0:T(8,128)(2,1)S(1)}, bf16[1024,1024]{1,0:T(8,128)(2,1)}, u32[]{:S(2)}) copy-start(bf16[1024,1024]{1,0:T(8,128)(2,1)} %param.20) | copy-start | bytes 6291460
  0.6 16.2 %collective-permute-start = (bf16[64,1024]{1,0:T(8,128)(2,1)}, bf16[64,1024]{1,0:T(8,128)(2,1)S(1)}, u32[]{:S(2)}, u32[]{:S(2)}) collective-permute-start(bf16[64,1024]{1,0:T(8,128)(2,1)} %q_ref.1), channel_id=1, source_target_pairs={{0,1},{1,2},{2,3},{3,0},{4,5},{5,6},{6,7},{7,4},{8,9},{9,10},{10,1... | collective-permute-start | bytes 393224 | tf_op jit(solution)/shard_map/ppermute | solution.py:193
  2.2 26.8 %collective-permute-start.4 = (bf16[64,1024]{1,0:T(8,128)(2,1)}, bf16[64,1024]{1,0:T(8,128)(2,1)S(1)}, u32[]{:S(2)}, u32[]{:S(2)}) collective-permute-start(bf16[64,1024]{1,0:T(8,128)(2,1)} %q_ref.1), channel_id=1, source_target_pairs={{0,3},{1,0},{2,1},{3,2},{4,7},{5,4},{6,5},{7,6},{8,11},{9,8},{10,9... | collective-permute-start | bytes 393224 | tf_op jit(solution)/shard_map/ppermute | solution.py:193
  4.0 18.8 %collective-permute-start.2 = (bf16[64,1024]{1,0:T(8,128)(2,1)}, bf16[64,1024]{1,0:T(8,128)(2,1)S(1)}, u32[]{:S(2)}, u32[]{:S(2)}) collective-permute-start(bf16[64,1024]{1,0:T(8,128)(2,1)} %q_ref.1), channel_id=1, source_target_pairs={{0,2},{1,3},{2,0},{3,1},{4,6},{5,7},{6,4},{7,5},{8,10},{9,11},{10,... | collective-permute-start | bytes 393224 | tf_op jit(solution)/shard_map/ppermute | solution.py:193
  16.9 0.7 copy-start.6
  21.6 12.6 %copy-start.7 = (s32[64,8]{0,1:T(8,128)S(1)}, s32[64,8]{0,1:T(8,128)}, u32[]{:S(2)}) copy-start(s32[64,8]{0,1:T(8,128)} %param.24) | copy-start | bytes 6148
  21.6 17.5 %collective-permute-start.1 = (f32[64,1152]{1,0:T(8,128)}, f32[64,1152]{1,0:T(8,128)S(1)}, u32[]{:S(2)}, u32[]{:S(2)}) collective-permute-start(f32[64,1152]{1,0:T(8,128)} %shard_map.141), channel_id=1, source_target_pairs={{0,3},{1,0},{2,1},{3,2},{4,7},{5,4},{6,5},{7,6},{8,11},{9,8},{10,9... | collective-permute-start | bytes 884744 | tf_op jit(solution)/shard_map/ppermute | solution.py:202
  22.7 0.7 copy-start.5
  27.5 11.6 %collective-permute-start.3 = (f32[64,1152]{1,0:T(8,128)}, f32[64,1152]{1,0:T(8,128)S(1)}, u32[]{:S(2)}, u32[]{:S(2)}) collective-permute-start(f32[64,1152]{1,0:T(8,128)} %shard_map.142), channel_id=1, source_target_pairs={{0,2},{1,3},{2,0},{3,1},{4,6},{5,7},{6,4},{7,5},{8,10},{9,11},{10,... | collective-permute-start | bytes 884744 | tf_op jit(solution)/shard_map/ppermute | solution.py:202
  29.0 0.7 copy-start.4
  33.7 9.4 %collective-permute-start.5 = (f32[64,1152]{1,0:T(8,128)}, f32[64,1152]{1,0:T(8,128)S(1)}, u32[]{:S(2)}, u32[]{:S(2)}) collective-permute-start(f32[64,1152]{1,0:T(8,128)} %shard_map.143), channel_id=1, source_target_pairs={{0,1},{1,2},{2,3},{3,0},{4,5},{5,6},{6,7},{7,4},{8,9},{9,10},{10,1... | collective-permute-start | bytes 884744 | tf_op jit(solution)/shard_map/ppermute | solution.py:202
  38.4 7.4 %copy-start.1 = (f32[64,1152]{1,0:T(8,128)S(1)}, f32[64,1152]{1,0:T(8,128)}, u32[]{:S(2)}) copy-start(f32[64,1152]{1,0:T(8,128)} %shard_map.140) | copy-start | bytes 884740
  44.8 1.4 copy-start.3
  45.8 1.0 copy-start.8
  46.1 2.7 %copy-start.2 = (bf16[64,1024]{1,0:T(8,128)(2,1)}, bf16[64,1024]{1,0:T(8,128)(2,1)S(1)}, u32[]{:S(2)}) copy-start(bf16[64,1024]{1,0:T(8,128)(2,1)S(1)} %fusion.22) | copy-start | bytes 393220
  48.9 12.4 %copy-start.10 = (bf16[1,1024,512]{2,1,0:T(8,128)(2,1)S(1)}, bf16[1,1024,512]{2,1,0:T(8,128)(2,1)}, u32[]{:S(2)}) copy-start(bf16[1,1024,512]{2,1,0:T(8,128)(2,1)} %param.22) | copy-start | bytes 3145732
  48.9 63.6 %all-to-all-start = ((bf16[64,16,1024]{2,1,0:T(8,128)(2,1)}), bf16[64,16,1024]{2,1,0:T(8,128)(2,1)}, u32[]{:S(2)}, u32[]{:S(2)}) async-start(bf16[64,16,1024]{2,1,0:T(8,128)(2,1)} %bitcast.109), calls=%async_computation | async-start | bytes 4194304 | tf_op jit(solution)/shard_map/all_to_all | solution.py:110
  61.3 54.8 %collective-permute-start.6 = (bf16[1,1024,512]{2,1,0:T(8,128)(2,1)S(1)}, bf16[1,1024,512]{2,1,0:T(8,128)(2,1)}, u32[]{:S(2)}, u32[]{:S(2)}) collective-permute-start(bf16[1,1024,512]{2,1,0:T(8,128)(2,1)S(1)} %copy-done.10), channel_id=1, source_target_pairs={{0,4},{4,0},{8,12},{12,8},{16,20},{20,16},{24,28},{28,24},{32,36},... | collective-permute-start | bytes 3145736 | tf_op jit(solution)/shard_map/ppermute | solution.py:140
  61.5 57.7 %collective-permute-start.7 = (bf16[1,256,1024]{2,1,0:T(8,128)(2,1)}, bf16[1,256,1024]{2,1,0:T(8,128)(2,1)}, u32[]{:S(2)}, u32[]{:S(2)}) collective-permute-start(bf16[1,256,1024]{2,1,0:T(8,128)(2,1)} %param.23), channel_id=1, source_target_pairs={{0,4},{4,0},{8,12},{12,8},{16,20},{20,16},{24,28},{28,24},{32,36},... | collective-permute-start | bytes 1572872 | tf_op jit(solution)/shard_map/ppermute | solution.py:141
  112.4 2.9 %copy-start.11 = (bf16[1,256,1024]{2,1,0:T(8,128)(2,1)S(1)}, bf16[1,256,1024]{2,1,0:T(8,128)(2,1)}, u32[]{:S(2)}) copy-start(bf16[1,256,1024]{2,1,0:T(8,128)(2,1)} %param.23) | copy-start | bytes 1572868
  122.5 5.8 %copy-start.9 = (f32[64,8]{0,1:T(8,128)S(1)}, f32[64,8]{0,1:T(8,128)}, u32[]{:S(2)}) copy-start(f32[64,8]{0,1:T(8,128)} %param.25) | copy-start | bytes 6148
  122.5 56.9 %all-to-all-start.1 = ((bf16[64,16,1024]{2,1,0:T(8,128)(2,1)}), bf16[64,16,1024]{2,1,0:T(8,128)(2,1)}, u32[]{:S(2)}, u32[]{:S(2)}) async-start(bf16[64,16,1024]{2,1,0:T(8,128)(2,1)} %bitcast.122), calls=%async_computation.1 | async-start | bytes 4194304 | tf_op jit(solution)/shard_map/all_to_all | solution.py:112

commit v10 on v9

--- a/solution.py
+++ b/solution.py
@@ -24,8 +24,17 @@
 ):
     rows = q_ref.shape[0]
     first = pl.multiple_of(source_ref[0] * rows, rows)
-    query_len = query_len_ref[pl.ds(first, rows), :]
-    query_seg = query_seg_ref[pl.ds(first, rows), :]
+    group = query_len_ref.shape[1]
+    pick = lax.broadcasted_iota(jnp.int32, (rows, group), 1) == (
+        first + lax.broadcasted_iota(jnp.int32, (rows, group), 0)
+    )
+
+    def column(row_ref):
+        row = row_ref[...].astype(jnp.float32)
+        return jnp.sum(jnp.where(pick, row, 0.0), axis=1, keepdims=True).astype(jnp.int32)
+
+    query_len = column(query_len_ref)
+    query_seg = column(query_seg_ref)
     query_order = first + lax.broadcasted_iota(jnp.int32, (rows, 1), 0)
     key_pos = key_pos_ref[...]
     shown = (key_pos < query_len) | (
@@ -181,8 +190,13 @@
     key_seg = jnp.concatenate(
         [jnp.full((pool_blocks * block_len,), -1, jnp.int32), fresh_seg]
     ).reshape(1, -1)
-    query_len_all = row_len.reshape(-1, 1)
-    query_seg_all = segments.reshape(-1, 1)
+    query_len_all = jnp.sum(
+        jnp.where(
+            request_ids[:, :, None] == request_range[None, None, :], lengths[None, None, :], 0
+        ),
+        axis=2,
+    )
+    query_seg_all = request_ids
 
     def attend_block(query_block, source):
         return attend_partial(

time: 184 us -> 182 us (0.989)
  local copies, waits for them, and re-layouts: 7.79 us -> 5.51 us
  transfers between devices with their start and end apart: 10 -> 10, of which waited for: 3 -> 3; matrix products, arithmetic and copies ran while one was open for 11% -> 10% of each run, Pallas kernels for 9% -> 9%
where the time goes in v10:
time: 182 us; the launch traced here: 181 us
  waiting for transfers between devices  105 us (58%)
  starting transfers between devices  27 us (15%)
  matrix products  17.4 us (10%)
  Pallas kernels  15.9 us (9%)
  other arithmetic  9.1 us (5%)
  local copies, waits for them, and re-layouts  5.51 us (3%)
    all_to_all x1, waiting for transfers between devices, direct_dispatch(): lax.all_to_all(unit_rows, 'tok', split_axis=0, concat_axis=0, tiled=True)  50.5 us
    all_to_all x1, waiting for transfers between devices, direct_dispatch(): lax.all_to_all(produced.reshape(EXPERTS * split, CAP // split, width), 't...  50.3 us
    pallas_call x4, Pallas kernels, attend_partial(): pl.pallas_call(_attend_kernel, out_shape=jax.ShapeDtypeStruct((rows, QUER...  15.9 us
    all_to_all x1, starting transfers between devices, direct_dispatch(): lax.all_to_all(unit_rows, 'tok', split_axis=0, concat_axis=0, tiled=True)  12.4 us
    dot_general x2, matrix products, pair_ffn(): jnp.dot(rows_in, gate_up_pair[part], preferred_element_type=jnp.float32)  5.99 us
    all_to_all x1, starting transfers between devices, direct_dispatch(): lax.all_to_all(produced.reshape(EXPERTS * split, CAP // split, width), 't...  5.77 us
    ppermute x3, starting transfers between devices, body(): lax.ppermute(queries, 'pool', [(i, (i + shift) % pool_size) for i in rang...  5.13 us
    ppermute x3, waiting for transfers between devices, body(): lax.ppermute(partial, 'pool', [(i, (i - shift) % pool_size) for i in rang...  4.21 us
  transfers between devices with their start and end apart: 10, of which 3 were waited for; matrix products, arithmetic and copies ran while one was open for 10% of the time, Pallas kernels for 9%

profile of v10, /device:TPU:8, one launch (start us, length us, event | category | flops | bytes accessed | tf_op | source)
XLA Modules:
  0.0 181.0 jit_solution(8670028970098112719)
XLA Ops:
  0.6 1.6 collective-permute-start
  2.2 1.7 collective-permute-start.4
  4.0 1.8 %collective-permute-start.2 = (bf16[64,1024]{1,0:T(8,128)(2,1)}, bf16[64,1024]{1,0:T(8,128)(2,1)S(1)}, u32[]{:S(2)}, u32[]{:S(2)}) collective-permute-start(bf16[64,1024]{1,0:T(8,128)(2,1)} %q_ref.1), channel_id=1, source_target_pairs={{0,2},{1,3},{2,0},{3,1},{4,6},{5,7},{6,4},{7,5},{8,10},{9,11},{10,... | collective-permute-start | bytes 393224 | tf_op jit(solution)/shard_map/ppermute | solution.py:207
  5.8 0.8 select_reduce_fusion.1
  6.6 0.8 copy.29
  8.3 0.7 dynamic-slice_bitcast_fusion
  9.7 1.2 reduce-window.6
  11.4 1.4 fusion.43
  12.8 2.4 %pad_maximum_fusion.kv_ref = bf16[576,1024]{1,0:T(8,128)(2,1)} fusion(bf16[64,1024]{1,0:T(8,128)(2,1)} %param.15, bf16[512,1024]{1,0:T(8,128)(2,1)} %bitcast.122), kind=kLoop, calls=%fused_computation.5 | loop fusion | flops 2359296 | bytes 2359296 | tf_op jit(solution)/shard_map/concatenate | solution.py:182
  15.2 0.7 copy-done.6
  15.8 4.0 %shard_map.144 = f32[64,1152]{1,0:T(8,128)} custom-call(s32[1]{0:T(128)} %bitcast.9.source_ref, bf16[64,1024]{1,0:T(8,128)(2,1)} %copy-done.6, bf16[576,1024]{1,0:T(8,128)(2,1)} %pad_maximum_fusion.kv_ref, s32[1,256]{1,0:T(1,128)} %bitcast.124, s32[1,256]{1,0:T(1,128)} %query_seg_ref.7, s32[1,576]{1,0:T(1,128)} %reshape.204.key_pos_ref, ...), custom_call_target="tpu_custom_call" | custom-call | tf_op jit(solution)/shard_map/pallas_call | solution.py:88
  19.8 1.1 collective-permute-start.1
  21.0 0.7 copy-done.5
  21.6 4.0 %shard_map.145 = f32[64,1152]{1,0:T(8,128)} custom-call(s32[1]{0:T(128)} %bitcast.11.source_ref, bf16[64,1024]{1,0:T(8,128)(2,1)} %copy-done.5, bf16[576,1024]{1,0:T(8,128)(2,1)} %pad_maximum_fusion.kv_ref, s32[1,256]{1,0:T(1,128)} %bitcast.125, s32[1,256]{1,0:T(1,128)} %query_seg_ref.7, s32[1,576]{1,0:T(1,128)} %reshape.204.key_pos_ref, ...), custom_call_target="tpu_custom_call" | custom-call | tf_op jit(solution)/shard_map/pallas_call | solution.py:88
  25.6 1.5 collective-permute-start.3
  27.8 4.0 %shard_map.146 = f32[64,1152]{1,0:T(8,128)} custom-call(s32[1]{0:T(128)} %bitcast.13.source_ref, bf16[64,1024]{1,0:T(8,128)(2,1)} %copy-done.4, bf16[576,1024]{1,0:T(8,128)(2,1)} %pad_maximum_fusion.kv_ref, s32[1,256]{1,0:T(1,128)} %bitcast.126, s32[1,256]{1,0:T(1,128)} %query_seg_ref.7, s32[1,576]{1,0:T(1,128)} %reshape.204.key_pos_ref, ...), custom_call_target="tpu_custom_call" | custom-call | tf_op jit(solution)/shard_map/pallas_call | solution.py:88
  32.3 4.0 %shard_map.143 = f32[64,1152]{1,0:T(8,128)} custom-call(s32[1]{0:T(128)} %bitcast.source_ref, bf16[64,1024]{1,0:T(8,128)(2,1)} %q_ref.1, bf16[576,1024]{1,0:T(8,128)(2,1)} %pad_maximum_fusion.kv_ref, s32[1,256]{1,0:T(1,128)} %bitcast.127, s32[1,256]{1,0:T(1,128)} %query_seg_ref.7, s32[1,576]{1,0:T(1,128)} %reshape.204.key_pos_ref, s32[1,576]{1,0:T(1,128)} %reshape.205.key_seg_ref), custom_call_target="tpu_custom_call" | custom-call | tf_op jit(solution)/shard_map/pallas_call | solution.py:88
  36.3 0.7 fusion
  37.0 4.2 %collective-permute-done.5 = f32[64,1152]{1,0:T(8,128)S(1)} collective-permute-done((f32[64,1152]{1,0:T(8,128)}, f32[64,1152]{1,0:T(8,128)S(1)}, u32[]{:S(2)}, u32[]{:S(2)}) %collective-permute-start.5) | collective-permute-done | bytes 294944 | tf_op jit(solution)/shard_map/ppermute | solution.py:216
  41.2 0.8 fusion.46
  42.0 0.9 subtract_exponential_fusion
  44.9 2.1 %convolution_convert_fusion = bf16[1024,1024]{1,0:T(8,128)(2,1)} fusion(pred[1024,64]{0,1:T(8,128)(4,1)S(1)} %fusion, f32[64,1024]{1,0:T(8,128)S(1)} %get-tuple-element.7, f32[1024]{0:T(1024)S(1)} %copy-done.8, f32[64]{0:T(128)S(1)} %add_rsqrt_fusion), kind=kOutput, calls=%fused_computation.4 | convolution fusion | flops 135462912 | bytes 2429184 | tf_op jit(solution)/shard_map/dot_general | solution.py:255
  47.0 12.4 %all-to-all-start = ((bf16[64,16,1024]{2,1,0:T(8,128)(2,1)}), bf16[64,16,1024]{2,1,0:T(8,128)(2,1)}, u32[]{:S(2)}, u32[]{:S(2)}) async-start(bf16[64,16,1024]{2,1,0:T(8,128)(2,1)} %bitcast.108), calls=%async_computation | async-start | bytes 4194304 | tf_op jit(solution)/shard_map/all_to_all | solution.py:119
  60.0 50.5 %all-to-all-done = bf16[64,16,1024]{2,1,0:T(8,128)(2,1)} async-done(((bf16[64,16,1024]{2,1,0:T(8,128)(2,1)}), bf16[64,16,1024]{2,1,0:T(8,128)(2,1)}, u32[]{:S(2)}, u32[]{:S(2)}) %all-to-all-start) | async-done | bytes 2097184 | tf_op jit(solution)/shard_map/all_to_all | solution.py:119
  110.5 2.9 %fusion.6 = f32[1024,512]{1,0:T(8,128)S(1)} fusion(bf16[1024,1024]{1,0:T(8,128)(2,1)} %bitcast.24, bf16[1,1024,512]{2,1,0:T(8,128)(2,1)S(1)} %copy-done.10), kind=kOutput, calls=%fused_computation.16 | convolution fusion | flops 1073741824 | bytes 5242880 | tf_op jit(solution)/shard_map/dot_general | solution.py:104
  113.4 0.7 fusion.8
  114.2 3.1 %fusion.4 = f32[1024,512]{1,0:T(8,128)S(1)} fusion(bf16[1024,1024]{1,0:T(8,128)(2,1)} %bitcast.24, bf16[1,1024,512]{2,1,0:T(8,128)(2,1)} %collective-permute-done.6), kind=kOutput, calls=%fused_computation.14 | convolution fusion | flops 1073741824 | bytes 5242880 | tf_op jit(solution)/shard_map/dot_general | solution.py:104
  117.3 3.2 %add_convert_fusion = bf16[1024,1024]{1,0:T(8,128)(2,1)} fusion(bf16[1024,1024]{1,0:T(8,128)(2,1)S(1)} %fusion.8, f32[1024,512]{1,0:T(8,128)S(1)} %fusion.4, bf16[1,256,1024]{2,1,0:T(8,128)(2,1)} %collective-permute-done.7), kind=kOutput, calls=%fused_computation | convolution fusion | flops 543686656 | bytes 6815744 | tf_op jit(solution)/shard_map/dot_general | solution.py:108
  120.6 5.8 %all-to-all-start.1 = ((bf16[64,16,1024]{2,1,0:T(8,128)(2,1)}), bf16[64,16,1024]{2,1,0:T(8,128)(2,1)}, u32[]{:S(2)}, u32[]{:S(2)}) async-start(bf16[64,16,1024]{2,1,0:T(8,128)(2,1)} %bitcast.121), calls=%async_computation.1 | async-start | bytes 4194304 | tf_op jit(solution)/shard_map/all_to_all | solution.py:121
  126.4 0.7 select_reduce_fusion
  127.2 50.3 %all-to-all-done.1 = bf16[64,16,1024]{2,1,0:T(8,128)(2,1)} async-done(((bf16[64,16,1024]{2,1,0:T(8,128)(2,1)}), bf16[64,16,1024]{2,1,0:T(8,128)(2,1)}, u32[]{:S(2)}, u32[]{:S(2)}) %all-to-all-start.1) | async-done | bytes 2097184 | tf_op jit(solution)/shard_map/all_to_all | solution.py:121
  177.5 3.5 %fusion.1 = bf16[64,1024]{1,0:T(8,128)(2,1)} fusion(f32[64,1024]{1,0:T(8,128)S(1)} %get-tuple-element.7, f32[1024,64]{0,1:T(8,128)S(1)} %select_reduce_fusion, bf16[1024,1024]{1,0:T(8,128)(2,1)} %bitcast.30), kind=kOutput, calls=%fused_computation.9 | convolution fusion | flops 805437440 | bytes 2752512 | tf_op jit(solution)/shard_map/dot_general | solution.py:266
  (63 shorter events, 5.9 us)
Async XLA Ops:
  0.6 43.6 %copy-start = (bf16[1024,1024]{1,0:T(8,128)(2,1)S(1)}, bf16[1024,1024]{1,0:T(8,128)(2,1)}, u32[]{:S(2)}) copy-start(bf16[1024,1024]{1,0:T(8,128)(2,1)} %param.20) | copy-start | bytes 6291460
  0.6 14.5 %collective-permute-start = (bf16[64,1024]{1,0:T(8,128)(2,1)}, bf16[64,1024]{1,0:T(8,128)(2,1)S(1)}, u32[]{:S(2)}, u32[]{:S(2)}) collective-permute-start(bf16[64,1024]{1,0:T(8,128)(2,1)} %q_ref.1), channel_id=1, source_target_pairs={{0,1},{1,2},{2,3},{3,0},{4,5},{5,6},{6,7},{7,4},{8,9},{9,10},{10,1... | collective-permute-start | bytes 393224 | tf_op jit(solution)/shard_map/ppermute | solution.py:207
  2.2 24.9 %collective-permute-start.4 = (bf16[64,1024]{1,0:T(8,128)(2,1)}, bf16[64,1024]{1,0:T(8,128)(2,1)S(1)}, u32[]{:S(2)}, u32[]{:S(2)}) collective-permute-start(bf16[64,1024]{1,0:T(8,128)(2,1)} %q_ref.1), channel_id=1, source_target_pairs={{0,3},{1,0},{2,1},{3,2},{4,7},{5,4},{6,5},{7,6},{8,11},{9,8},{10,9... | collective-permute-start | bytes 393224 | tf_op jit(solution)/shard_map/ppermute | solution.py:207
  4.0 17.0 %collective-permute-start.2 = (bf16[64,1024]{1,0:T(8,128)(2,1)}, bf16[64,1024]{1,0:T(8,128)(2,1)S(1)}, u32[]{:S(2)}, u32[]{:S(2)}) collective-permute-start(bf16[64,1024]{1,0:T(8,128)(2,1)} %q_ref.1), channel_id=1, source_target_pairs={{0,2},{1,3},{2,0},{3,1},{4,6},{5,7},{6,4},{7,5},{8,10},{9,11},{10,... | collective-permute-start | bytes 393224 | tf_op jit(solution)/shard_map/ppermute | solution.py:207
  15.2 0.7 copy-start.6
  15.8 16.4 %copy-start.7 = (s32[64,8]{0,1:T(8,128)S(1)}, s32[64,8]{0,1:T(8,128)}, u32[]{:S(2)}) copy-start(s32[64,8]{0,1:T(8,128)} %param.24) | copy-start | bytes 6148
  19.8 17.2 %collective-permute-start.1 = (f32[64,1152]{1,0:T(8,128)}, f32[64,1152]{1,0:T(8,128)S(1)}, u32[]{:S(2)}, u32[]{:S(2)}) collective-permute-start(f32[64,1152]{1,0:T(8,128)} %shard_map.144), channel_id=1, source_target_pairs={{0,3},{1,0},{2,1},{3,2},{4,7},{5,4},{6,5},{7,6},{8,11},{9,8},{10,9... | collective-permute-start | bytes 884744 | tf_op jit(solution)/shard_map/ppermute | solution.py:216
  21.0 0.7 copy-start.5
  25.6 11.4 %collective-permute-start.3 = (f32[64,1152]{1,0:T(8,128)}, f32[64,1152]{1,0:T(8,128)S(1)}, u32[]{:S(2)}, u32[]{:S(2)}) collective-permute-start(f32[64,1152]{1,0:T(8,128)} %shard_map.145), channel_id=1, source_target_pairs={{0,2},{1,3},{2,0},{3,1},{4,6},{5,7},{6,4},{7,5},{8,10},{9,11},{10,... | collective-permute-start | bytes 884744 | tf_op jit(solution)/shard_map/ppermute | solution.py:216
  27.1 0.7 copy-start.4
  31.7 9.5 %collective-permute-start.5 = (f32[64,1152]{1,0:T(8,128)}, f32[64,1152]{1,0:T(8,128)S(1)}, u32[]{:S(2)}, u32[]{:S(2)}) collective-permute-start(f32[64,1152]{1,0:T(8,128)} %shard_map.146), channel_id=1, source_target_pairs={{0,1},{1,2},{2,3},{3,0},{4,5},{5,6},{6,7},{7,4},{8,9},{9,10},{10,1... | collective-permute-start | bytes 884744 | tf_op jit(solution)/shard_map/ppermute | solution.py:216
  36.3 7.6 %copy-start.1 = (f32[64,1152]{1,0:T(8,128)S(1)}, f32[64,1152]{1,0:T(8,128)}, u32[]{:S(2)}) copy-start(f32[64,1152]{1,0:T(8,128)} %shard_map.143) | copy-start | bytes 884740
  42.9 1.4 copy-start.3
  43.9 1.0 copy-start.8
  44.3 2.7 %copy-start.2 = (bf16[64,1024]{1,0:T(8,128)(2,1)}, bf16[64,1024]{1,0:T(8,128)(2,1)S(1)}, u32[]{:S(2)}) copy-start(bf16[64,1024]{1,0:T(8,128)(2,1)S(1)} %fusion.22) | copy-start | bytes 393220
  47.0 12.4 %copy-start.10 = (bf16[1,1024,512]{2,1,0:T(8,128)(2,1)S(1)}, bf16[1,1024,512]{2,1,0:T(8,128)(2,1)}, u32[]{:S(2)}) copy-start(bf16[1,1024,512]{2,1,0:T(8,128)(2,1)} %param.22) | copy-start | bytes 3145732
  47.0 63.6 %all-to-all-start = ((bf16[64,16,1024]{2,1,0:T(8,128)(2,1)}), bf16[64,16,1024]{2,1,0:T(8,128)(2,1)}, u32[]{:S(2)}, u32[]{:S(2)}) async-start(bf16[64,16,1024]{2,1,0:T(8,128)(2,1)} %bitcast.108), calls=%async_computation | async-start | bytes 4194304 | tf_op jit(solution)/shard_map/all_to_all | solution.py:119
  59.4 54.8 %collective-permute-start.6 = (bf16[1,1024,512]{2,1,0:T(8,128)(2,1)S(1)}, bf16[1,1024,512]{2,1,0:T(8,128)(2,1)}, u32[]{:S(2)}, u32[]{:S(2)}) collective-permute-start(bf16[1,1024,512]{2,1,0:T(8,128)(2,1)S(1)} %copy-done.10), channel_id=1, source_target_pairs={{0,4},{4,0},{8,12},{12,8},{16,20},{20,16},{24,28},{28,24},{32,36},... | collective-permute-start | bytes 3145736 | tf_op jit(solution)/shard_map/ppermute | solution.py:149
  59.6 57.7 %collective-permute-start.7 = (bf16[1,256,1024]{2,1,0:T(8,128)(2,1)}, bf16[1,256,1024]{2,1,0:T(8,128)(2,1)}, u32[]{:S(2)}, u32[]{:S(2)}) collective-permute-start(bf16[1,256,1024]{2,1,0:T(8,128)(2,1)} %param.23), channel_id=1, source_target_pairs={{0,4},{4,0},{8,12},{12,8},{16,20},{20,16},{24,28},{28,24},{32,36},... | collective-permute-start | bytes 1572872 | tf_op jit(solution)/shard_map/ppermute | solution.py:150
  110.5 2.9 %copy-start.11 = (bf16[1,256,1024]{2,1,0:T(8,128)(2,1)S(1)}, bf16[1,256,1024]{2,1,0:T(8,128)(2,1)}, u32[]{:S(2)}) copy-start(bf16[1,256,1024]{2,1,0:T(8,128)(2,1)} %param.23) | copy-start | bytes 1572868
  120.6 5.8 %copy-start.9 = (f32[64,8]{0,1:T(8,128)S(1)}, f32[64,8]{0,1:T(8,128)}, u32[]{:S(2)}) copy-start(f32[64,8]{0,1:T(8,128)} %param.25) | copy-start | bytes 6148
  120.6 56.9 %all-to-all-start.1 = ((bf16[64,16,1024]{2,1,0:T(8,128)(2,1)}), bf16[64,16,1024]{2,1,0:T(8,128)(2,1)}, u32[]{:S(2)}, u32[]{:S(2)}) async-start(bf16[64,16,1024]{2,1,0:T(8,128)(2,1)} %bitcast.121), calls=%async_computation.1 | async-start | bytes 4194304 | tf_op jit(solution)/shard_map/all_to_all | solution.py:121

commit v11 on v10

--- a/solution.py
+++ b/solution.py
@@ -20,7 +20,15 @@
 
 
 def _attend_kernel(
-    source_ref, q_ref, kv_ref, query_len_ref, query_seg_ref, key_pos_ref, key_seg_ref, out_ref
+    source_ref,
+    q_ref,
+    cache_ref,
+    fresh_ref,
+    query_len_ref,
+    query_seg_ref,
+    key_pos_ref,
+    key_seg_ref,
+    out_ref,
 ):
     rows = q_ref.shape[0]
     first = pl.multiple_of(source_ref[0] * rows, rows)
@@ -46,9 +54,9 @@
     heads_per_tile = 128 // HEAD_SIZE
     visible = jnp.concatenate([shown] * (2 * heads_per_tile), axis=0)
     for t in range(KEY_VALUE_HEADS // heads_per_tile):
-        k_tile = kv_ref[:, t * 128:(t + 1) * 128]
         v_start = KEY_VALUE_HEADS * HEAD_SIZE + t * 128
-        v_tile = kv_ref[:, v_start:v_start + 128]
+        key_tiles = [ref[:, t * 128:(t + 1) * 128] for ref in (cache_ref, fresh_ref)]
+        value_tiles = [ref[:, v_start:v_start + 128] for ref in (cache_ref, fresh_ref)]
         pieces = []
         for h in range(t * heads_per_tile, (t + 1) * heads_per_tile):
             q_tile = q_ref[:, h * 128:(h + 1) * 128].astype(jnp.float32)
@@ -58,14 +66,24 @@
                     q_half = pltpu.roll(q_half, HEAD_SIZE, 1)
                 pieces.append(q_half)
         q_stack = jnp.concatenate(pieces, axis=0).astype(jnp.bfloat16)
-        scores = lax.dot_general(
-            q_stack, k_tile, (((1,), (1,)), ((), ())), preferred_element_type=jnp.float32
+        scores = jnp.concatenate(
+            [
+                lax.dot_general(
+                    q_stack, k_tile, (((1,), (1,)), ((), ())), preferred_element_type=jnp.float32
+                )
+                for k_tile in key_tiles
+            ],
+            axis=1,
         ) * score_scale
         scores = jnp.where(visible, scores, masked_filler)
         highest = jnp.max(scores, axis=1, keepdims=True)
         weights = jnp.where(visible, jnp.exp(scores - highest), 0.0)
         total = jnp.sum(weights, axis=1, keepdims=True)
-        acc = jnp.dot(weights.astype(jnp.bfloat16), v_tile, preferred_element_type=jnp.float32)
+        rounded = weights.astype(jnp.bfloat16)
+        cached = cache_ref.shape[0]
+        acc = jnp.dot(
+            rounded[:, :cached], value_tiles[0], preferred_element_type=jnp.float32
+        ) + jnp.dot(rounded[:, cached:], value_tiles[1], preferred_element_type=jnp.float32)
         for local, h in enumerate(range(t * heads_per_tile, (t + 1) * heads_per_tile)):
             out_tile = jnp.zeros((rows, 128), jnp.float32)
             for g in range(2):
@@ -81,10 +99,10 @@
     out_ref[:, QUERY_HEADS * HEAD_SIZE:QUERY_HEADS * HEAD_SIZE + 128] = stats
 
 
-def attend_partial(source, q_block, kv, query_len, query_seg, key_pos, key_seg):
+def attend_partial(source, q_block, cached, fresh, query_len, query_seg, key_pos, key_seg):
     rows = q_block.shape[0]
     whole = lambda shape: pl.BlockSpec(shape, lambda i, s: (0,) * len(shape))
-    operands = (q_block, kv, query_len, query_seg, key_pos, key_seg)
+    operands = (q_block, cached, fresh, query_len, query_seg, key_pos, key_seg)
     return pl.pallas_call(
         _attend_kernel,
         out_shape=jax.ShapeDtypeStruct((rows, QUERY_HEADS * HEAD_SIZE + 128), jnp.float32),
@@ -179,9 +197,7 @@
     shifts = range(pool_size)
     fresh_order = pool_idx * tokens_per_device + jnp.arange(tokens_per_device, dtype=jnp.int32)
     fresh_seg = lax.dynamic_slice_in_dim(segments, pool_idx * tokens_per_device, tokens_per_device)
-    key_value_pairs = jnp.concatenate(
-        [cache_block_pool.reshape(pool_blocks * block_len, 2 * kv_width), fresh_kv], axis=0
-    )
+    cached_rows = cache_block_pool.reshape(pool_blocks * block_len, 2 * kv_width)
 
     unlisted = jnp.int32(1 << 30)
     key_pos = jnp.concatenate(
@@ -200,7 +216,14 @@
 
     def attend_block(query_block, source):
         return attend_partial(
-            source, query_block, key_value_pairs, query_len_all, query_seg_all, key_pos, key_seg
+            source,
+            query_block,
+            cached_rows,
+            fresh_kv,
+            query_len_all,
+            query_seg_all,
+            key_pos,
+            key_seg,
         )
 
     query_blocks = [queries] + [
@@ -266,7 +289,7 @@
     experts_sum = jnp.dot(
         mixing,
         expert_rows.astype(jnp.float32),
-        precision=lax.Precision.HIGHEST,
+        precision=lax.Precision.HIGH,
         preferred_element_type=jnp.float32,
     )
     layer_out = (residual + experts_sum).astype(jnp.bfloat16)

time: 182 us -> 179 us (0.984)
  other arithmetic: 9.1 us -> 6.68 us
    concatenate x1 -> x0, other arithmetic: 2.39 us -> none  [body(): jnp.concatenate([cache_block_pool.reshape(pool_blocks * block_len, 2 * kv...]
  transfers between devices with their start and end apart: 10 -> 10, of which waited for: 3 -> 3; matrix products, arithmetic and copies ran while one was open for 10% -> 9% of each run, Pallas kernels for 9% -> 9%
where the time goes in v11:
time: 179 us; the launch traced here: 178 us
  waiting for transfers between devices  104 us (58%)
  starting transfers between devices  27.7 us (15%)
  matrix products  17 us (9%)
  Pallas kernels  15.7 us (9%)
  other arithmetic  6.68 us (4%)
  local copies, waits for them, and re-layouts  5.48 us (3%)
    all_to_all x1, waiting for transfers between devices, direct_dispatch(): lax.all_to_all(unit_rows, 'tok', split_axis=0, concat_axis=0, tiled=True)  50.5 us
    all_to_all x1, waiting for transfers between devices, direct_dispatch(): lax.all_to_all(produced.reshape(EXPERTS * split, CAP // split, width), 't...  50.3 us
    pallas_call x4, Pallas kernels, attend_partial(): pl.pallas_call(_attend_kernel, out_shape=jax.ShapeDtypeStruct((rows, QUER...  15.7 us
    all_to_all x1, starting transfers between devices, direct_dispatch(): lax.all_to_all(unit_rows, 'tok', split_axis=0, concat_axis=0, tiled=True)  12.4 us
    dot_general x2, matrix products, pair_ffn(): jnp.dot(rows_in, gate_up_pair[part], preferred_element_type=jnp.float32)  5.99 us
    all_to_all x1, starting transfers between devices, direct_dispatch(): lax.all_to_all(produced.reshape(EXPERTS * split, CAP // split, width), 't...  5.77 us
    ppermute x3, starting transfers between devices, body(): lax.ppermute(queries, 'pool', [(i, (i + shift) % pool_size) for i in rang...  5.13 us
    dot_general x2, matrix products, pair_ffn(): jnp.dot(inner, down_pair[part], preferred_element_type=jnp.float32)  3.99 us
  transfers between devices with their start and end apart: 10, of which 3 were waited for; matrix products, arithmetic and copies ran while one was open for 9% of the time, Pallas kernels for 9%

profile of v11, /device:TPU:8, one launch (start us, length us, event | category | flops | bytes accessed | tf_op | source)
XLA Modules:
  0.0 177.8 jit_solution(11843944869345565638)
XLA Ops:
  0.6 1.6 collective-permute-start
  2.2 1.7 collective-permute-start.4
  4.0 1.8 %collective-permute-start.2 = (bf16[64,1024]{1,0:T(8,128)(2,1)}, bf16[64,1024]{1,0:T(8,128)(2,1)S(1)}, u32[]{:S(2)}, u32[]{:S(2)}) collective-permute-start(bf16[64,1024]{1,0:T(8,128)(2,1)} %q_ref.1), channel_id=1, source_target_pairs={{0,2},{1,3},{2,0},{3,1},{4,6},{5,7},{6,4},{7,5},{8,10},{9,11},{10,... | collective-permute-start | bytes 393224 | tf_op jit(solution)/shard_map/ppermute | solution.py:230
  5.8 0.8 select_reduce_fusion.1
  6.6 0.8 copy.29
  7.8 1.2 reduce-window.6
  9.3 0.7 dynamic-slice_bitcast_fusion
  11.4 1.4 fusion.43
  12.7 0.7 copy-done.6
  13.4 3.9 %shard_map.144 = f32[64,1152]{1,0:T(8,128)} custom-call(s32[1]{0:T(128)} %bitcast.9.source_ref, bf16[64,1024]{1,0:T(8,128)(2,1)} %copy-done.6, bf16[512,1024]{1,0:T(8,128)(2,1)} %bitcast.108, bf16[64,1024]{1,0:T(8,128)(2,1)} %fresh_ref.7, s32[1,256]{1,0:T(1,128)} %bitcast.127, s32[1,256]{1,0:T(1,128)} %query_seg_ref.7, s32[1,576]{1,0:T(1,128)} %reshape.204.key_pos_ref, ...), custom_call_target="tpu_custom_call" | custom-call | tf_op jit(solution)/shard_map/pallas_call | solution.py:106
  17.3 1.1 collective-permute-start.1
  19.1 3.9 %shard_map.146 = f32[64,1152]{1,0:T(8,128)} custom-call(s32[1]{0:T(128)} %bitcast.13.source_ref, bf16[64,1024]{1,0:T(8,128)(2,1)} %copy-done.5, bf16[512,1024]{1,0:T(8,128)(2,1)} %bitcast.109, bf16[64,1024]{1,0:T(8,128)(2,1)} %fresh_ref.7, s32[1,256]{1,0:T(1,128)} %bitcast.128, s32[1,256]{1,0:T(1,128)} %query_seg_ref.7, s32[1,576]{1,0:T(1,128)} %reshape.204.key_pos_ref, ...), custom_call_target="tpu_custom_call" | custom-call | tf_op jit(solution)/shard_map/pallas_call | solution.py:106
  23.0 0.9 collective-permute-start.5
  23.9 0.7 copy-done.4
  24.6 3.9 %shard_map.145 = f32[64,1152]{1,0:T(8,128)} custom-call(s32[1]{0:T(128)} %bitcast.11.source_ref, bf16[64,1024]{1,0:T(8,128)(2,1)} %copy-done.4, bf16[512,1024]{1,0:T(8,128)(2,1)} %bitcast.110, bf16[64,1024]{1,0:T(8,128)(2,1)} %fresh_ref.7, s32[1,256]{1,0:T(1,128)} %bitcast.129, s32[1,256]{1,0:T(1,128)} %query_seg_ref.7, s32[1,576]{1,0:T(1,128)} %reshape.204.key_pos_ref, ...), custom_call_target="tpu_custom_call" | custom-call | tf_op jit(solution)/shard_map/pallas_call | solution.py:106
  28.5 1.7 collective-permute-start.3
  30.3 3.9 %shard_map.143 = f32[64,1152]{1,0:T(8,128)} custom-call(s32[1]{0:T(128)} %bitcast.source_ref, bf16[64,1024]{1,0:T(8,128)(2,1)} %q_ref.1, bf16[512,1024]{1,0:T(8,128)(2,1)} %bitcast.111, bf16[64,1024]{1,0:T(8,128)(2,1)} %fresh_ref.7, s32[1,256]{1,0:T(1,128)} %bitcast.130, s32[1,256]{1,0:T(1,128)} %query_seg_ref.7, s32[1,576]{1,0:T(1,128)} %reshape.204.key_pos_ref, ...), custom_call_target="tpu_custom_call" | custom-call | tf_op jit(solution)/shard_map/pallas_call | solution.py:106
  34.3 0.7 fusion
  35.0 3.4 %collective-permute-done.5 = f32[64,1152]{1,0:T(8,128)S(1)} collective-permute-done((f32[64,1152]{1,0:T(8,128)}, f32[64,1152]{1,0:T(8,128)S(1)}, u32[]{:S(2)}, u32[]{:S(2)}) %collective-permute-start.5) | collective-permute-done | bytes 294944 | tf_op jit(solution)/shard_map/ppermute | solution.py:239
  38.4 0.8 fusion.46
  39.2 0.9 subtract_exponential_fusion
  42.1 2.1 %convolution_convert_fusion = bf16[1024,1024]{1,0:T(8,128)(2,1)} fusion(pred[1024,64]{0,1:T(8,128)(4,1)S(1)} %fusion, f32[64,1024]{1,0:T(8,128)S(1)} %get-tuple-element.7, f32[1024]{0:T(1024)S(1)} %copy-done.8, f32[64]{0:T(128)S(1)} %add_rsqrt_fusion), kind=kOutput, calls=%fused_computation.4 | convolution fusion | flops 135462912 | bytes 2429184 | tf_op jit(solution)/shard_map/dot_general | solution.py:278
  44.1 12.4 %all-to-all-start = ((bf16[64,16,1024]{2,1,0:T(8,128)(2,1)}), bf16[64,16,1024]{2,1,0:T(8,128)(2,1)}, u32[]{:S(2)}, u32[]{:S(2)}) async-start(bf16[64,16,1024]{2,1,0:T(8,128)(2,1)} %bitcast.112), calls=%async_computation | async-start | bytes 4194304 | tf_op jit(solution)/shard_map/all_to_all | solution.py:137
  57.2 50.5 %all-to-all-done = bf16[64,16,1024]{2,1,0:T(8,128)(2,1)} async-done(((bf16[64,16,1024]{2,1,0:T(8,128)(2,1)}), bf16[64,16,1024]{2,1,0:T(8,128)(2,1)}, u32[]{:S(2)}, u32[]{:S(2)}) %all-to-all-start) | async-done | bytes 2097184 | tf_op jit(solution)/shard_map/all_to_all | solution.py:137
  107.7 2.9 %fusion.6 = f32[1024,512]{1,0:T(8,128)S(1)} fusion(bf16[1024,1024]{1,0:T(8,128)(2,1)} %bitcast.24, bf16[1,1024,512]{2,1,0:T(8,128)(2,1)S(1)} %copy-done.10), kind=kOutput, calls=%fused_computation.15 | convolution fusion | flops 1073741824 | bytes 5242880 | tf_op jit(solution)/shard_map/dot_general | solution.py:122
  110.6 0.7 fusion.8
  111.4 3.1 %fusion.4 = f32[1024,512]{1,0:T(8,128)S(1)} fusion(bf16[1024,1024]{1,0:T(8,128)(2,1)} %bitcast.24, bf16[1,1024,512]{2,1,0:T(8,128)(2,1)} %collective-permute-done.6), kind=kOutput, calls=%fused_computation.13 | convolution fusion | flops 1073741824 | bytes 5242880 | tf_op jit(solution)/shard_map/dot_general | solution.py:122
  114.5 3.2 %add_convert_fusion = bf16[1024,1024]{1,0:T(8,128)(2,1)} fusion(bf16[1024,1024]{1,0:T(8,128)(2,1)S(1)} %fusion.8, f32[1024,512]{1,0:T(8,128)S(1)} %fusion.4, bf16[1,256,1024]{2,1,0:T(8,128)(2,1)} %collective-permute-done.7), kind=kOutput, calls=%fused_computation | convolution fusion | flops 543686656 | bytes 6815744 | tf_op jit(solution)/shard_map/dot_general | solution.py:126
  117.8 5.8 %all-to-all-start.1 = ((bf16[64,16,1024]{2,1,0:T(8,128)(2,1)}), bf16[64,16,1024]{2,1,0:T(8,128)(2,1)}, u32[]{:S(2)}, u32[]{:S(2)}) async-start(bf16[64,16,1024]{2,1,0:T(8,128)(2,1)} %bitcast.125), calls=%async_computation.1 | async-start | bytes 4194304 | tf_op jit(solution)/shard_map/all_to_all | solution.py:139
  123.6 0.7 select_reduce_fusion
  124.4 50.3 %all-to-all-done.1 = bf16[64,16,1024]{2,1,0:T(8,128)(2,1)} async-done(((bf16[64,16,1024]{2,1,0:T(8,128)(2,1)}), bf16[64,16,1024]{2,1,0:T(8,128)(2,1)}, u32[]{:S(2)}, u32[]{:S(2)}) %all-to-all-start.1) | async-done | bytes 2097184 | tf_op jit(solution)/shard_map/all_to_all | solution.py:139
  174.7 3.1 %fusion.1 = bf16[64,1024]{1,0:T(8,128)(2,1)} fusion(f32[64,1024]{1,0:T(8,128)S(1)} %get-tuple-element.7, f32[1024,64]{0,1:T(8,128)S(1)} %select_reduce_fusion, bf16[1024,1024]{1,0:T(8,128)(2,1)} %bitcast.30), kind=kOutput, calls=%fused_computation.8 | convolution fusion | flops 402784256 | bytes 2752512 | tf_op jit(solution)/shard_map/dot_general | solution.py:289
  (62 shorter events, 5.4 us)
Async XLA Ops:
  0.6 40.8 %copy-start = (bf16[1024,1024]{1,0:T(8,128)(2,1)S(1)}, bf16[1024,1024]{1,0:T(8,128)(2,1)}, u32[]{:S(2)}) copy-start(bf16[1024,1024]{1,0:T(8,128)(2,1)} %param.20) | copy-start | bytes 6291460
  0.6 12.1 %collective-permute-start = (bf16[64,1024]{1,0:T(8,128)(2,1)}, bf16[64,1024]{1,0:T(8,128)(2,1)S(1)}, u32[]{:S(2)}, u32[]{:S(2)}) collective-permute-start(bf16[64,1024]{1,0:T(8,128)(2,1)} %q_ref.1), channel_id=1, source_target_pairs={{0,1},{1,2},{2,3},{3,0},{4,5},{5,6},{6,7},{7,4},{8,9},{9,10},{10,1... | collective-permute-start | bytes 393224 | tf_op jit(solution)/shard_map/ppermute | solution.py:230
  2.2 16.2 %collective-permute-start.4 = (bf16[64,1024]{1,0:T(8,128)(2,1)}, bf16[64,1024]{1,0:T(8,128)(2,1)S(1)}, u32[]{:S(2)}, u32[]{:S(2)}) collective-permute-start(bf16[64,1024]{1,0:T(8,128)(2,1)} %q_ref.1), channel_id=1, source_target_pairs={{0,3},{1,0},{2,1},{3,2},{4,7},{5,4},{6,5},{7,6},{8,11},{9,8},{10,9... | collective-permute-start | bytes 393224 | tf_op jit(solution)/shard_map/ppermute | solution.py:230
  4.0 20.0 %collective-permute-start.2 = (bf16[64,1024]{1,0:T(8,128)(2,1)}, bf16[64,1024]{1,0:T(8,128)(2,1)S(1)}, u32[]{:S(2)}, u32[]{:S(2)}) collective-permute-start(bf16[64,1024]{1,0:T(8,128)(2,1)} %q_ref.1), channel_id=1, source_target_pairs={{0,2},{1,3},{2,0},{3,1},{4,6},{5,7},{6,4},{7,5},{8,10},{9,11},{10,... | collective-permute-start | bytes 393224 | tf_op jit(solution)/shard_map/ppermute | solution.py:230
  12.7 0.7 copy-start.6
  13.4 16.9 %copy-start.7 = (s32[64,8]{0,1:T(8,128)S(1)}, s32[64,8]{0,1:T(8,128)}, u32[]{:S(2)}) copy-start(s32[64,8]{0,1:T(8,128)} %param.24) | copy-start | bytes 6148
  17.3 17.7 %collective-permute-start.1 = (f32[64,1152]{1,0:T(8,128)}, f32[64,1152]{1,0:T(8,128)S(1)}, u32[]{:S(2)}, u32[]{:S(2)}) collective-permute-start(f32[64,1152]{1,0:T(8,128)} %shard_map.144), channel_id=1, source_target_pairs={{0,3},{1,0},{2,1},{3,2},{4,7},{5,4},{6,5},{7,6},{8,11},{9,8},{10,9... | collective-permute-start | bytes 884744 | tf_op jit(solution)/shard_map/ppermute | solution.py:239
  18.5 0.7 copy-start.5
  23.0 15.4 %collective-permute-start.5 = (f32[64,1152]{1,0:T(8,128)}, f32[64,1152]{1,0:T(8,128)S(1)}, u32[]{:S(2)}, u32[]{:S(2)}) collective-permute-start(f32[64,1152]{1,0:T(8,128)} %shard_map.146), channel_id=1, source_target_pairs={{0,1},{1,2},{2,3},{3,0},{4,5},{5,6},{6,7},{7,4},{8,9},{9,10},{10,1... | collective-permute-start | bytes 884744 | tf_op jit(solution)/shard_map/ppermute | solution.py:239
  23.9 0.7 copy-start.4
  28.5 9.9 %collective-permute-start.3 = (f32[64,1152]{1,0:T(8,128)}, f32[64,1152]{1,0:T(8,128)S(1)}, u32[]{:S(2)}, u32[]{:S(2)}) collective-permute-start(f32[64,1152]{1,0:T(8,128)} %shard_map.145), channel_id=1, source_target_pairs={{0,2},{1,3},{2,0},{3,1},{4,6},{5,7},{6,4},{7,5},{8,10},{9,11},{10,... | collective-permute-start | bytes 884744 | tf_op jit(solution)/shard_map/ppermute | solution.py:239
  34.3 6.8 %copy-start.1 = (f32[64,1152]{1,0:T(8,128)S(1)}, f32[64,1152]{1,0:T(8,128)}, u32[]{:S(2)}) copy-start(f32[64,1152]{1,0:T(8,128)} %shard_map.143) | copy-start | bytes 884740
  40.1 1.4 copy-start.3
  41.1 1.0 copy-start.8
  41.4 2.7 %copy-start.2 = (bf16[64,1024]{1,0:T(8,128)(2,1)}, bf16[64,1024]{1,0:T(8,128)(2,1)S(1)}, u32[]{:S(2)}) copy-start(bf16[64,1024]{1,0:T(8,128)(2,1)S(1)} %fusion.22) | copy-start | bytes 393220
  44.1 12.4 %copy-start.10 = (bf16[1,1024,512]{2,1,0:T(8,128)(2,1)S(1)}, bf16[1,1024,512]{2,1,0:T(8,128)(2,1)}, u32[]{:S(2)}) copy-start(bf16[1,1024,512]{2,1,0:T(8,128)(2,1)} %param.22) | copy-start | bytes 3145732
  44.1 63.6 %all-to-all-start = ((bf16[64,16,1024]{2,1,0:T(8,128)(2,1)}), bf16[64,16,1024]{2,1,0:T(8,128)(2,1)}, u32[]{:S(2)}, u32[]{:S(2)}) async-start(bf16[64,16,1024]{2,1,0:T(8,128)(2,1)} %bitcast.112), calls=%async_computation | async-start | bytes 4194304 | tf_op jit(solution)/shard_map/all_to_all | solution.py:137
  56.6 54.8 %collective-permute-start.6 = (bf16[1,1024,512]{2,1,0:T(8,128)(2,1)S(1)}, bf16[1,1024,512]{2,1,0:T(8,128)(2,1)}, u32[]{:S(2)}, u32[]{:S(2)}) collective-permute-start(bf16[1,1024,512]{2,1,0:T(8,128)(2,1)S(1)} %copy-done.10), channel_id=1, source_target_pairs={{0,4},{4,0},{8,12},{12,8},{16,20},{20,16},{24,28},{28,24},{32,36},... | collective-permute-start | bytes 3145736 | tf_op jit(solution)/shard_map/ppermute | solution.py:167
  56.8 57.7 %collective-permute-start.7 = (bf16[1,256,1024]{2,1,0:T(8,128)(2,1)}, bf16[1,256,1024]{2,1,0:T(8,128)(2,1)}, u32[]{:S(2)}, u32[]{:S(2)}) collective-permute-start(bf16[1,256,1024]{2,1,0:T(8,128)(2,1)} %param.23), channel_id=1, source_target_pairs={{0,4},{4,0},{8,12},{12,8},{16,20},{20,16},{24,28},{28,24},{32,36},... | collective-permute-start | bytes 1572872 | tf_op jit(solution)/shard_map/ppermute | solution.py:168
  107.7 2.9 %copy-start.11 = (bf16[1,256,1024]{2,1,0:T(8,128)(2,1)S(1)}, bf16[1,256,1024]{2,1,0:T(8,128)(2,1)}, u32[]{:S(2)}) copy-start(bf16[1,256,1024]{2,1,0:T(8,128)(2,1)} %param.23) | copy-start | bytes 1572868
  117.8 5.8 %copy-start.9 = (f32[64,8]{0,1:T(8,128)S(1)}, f32[64,8]{0,1:T(8,128)}, u32[]{:S(2)}) copy-start(f32[64,8]{0,1:T(8,128)} %param.25) | copy-start | bytes 6148
  117.8 56.9 %all-to-all-start.1 = ((bf16[64,16,1024]{2,1,0:T(8,128)(2,1)}), bf16[64,16,1024]{2,1,0:T(8,128)(2,1)}, u32[]{:S(2)}, u32[]{:S(2)}) async-start(bf16[64,16,1024]{2,1,0:T(8,128)(2,1)} %bitcast.125), calls=%async_computation.1 | async-start | bytes 4194304 | tf_op jit(solution)/shard_map/all_to_all | solution.py:139

commit v12 on v11

--- a/solution.py
+++ b/solution.py
@@ -116,10 +116,13 @@
 
 
 def pair_ffn(rows_in, gate_up_pair, down_pair):
+    parts = gate_up_pair.shape[0]
     hidden_units = gate_up_pair.shape[2] // 2
+    joined = jnp.concatenate([gate_up_pair[part] for part in range(parts)], axis=1)
+    gate_up_all = jnp.dot(rows_in, joined, preferred_element_type=jnp.float32)
     total = None
-    for part in range(gate_up_pair.shape[0]):
-        gate_up = jnp.dot(rows_in, gate_up_pair[part], preferred_element_type=jnp.float32)
+    for part in range(parts):
+        gate_up = gate_up_all[:, part * 2 * hidden_units:(part + 1) * 2 * hidden_units]
         inner = (jax.nn.silu(gate_up[:, :hidden_units]) * gate_up[:, hidden_units:]).astype(
             jnp.bfloat16
         )
@@ -289,7 +292,7 @@
     experts_sum = jnp.dot(
         mixing,
         expert_rows.astype(jnp.float32),
-        precision=lax.Precision.HIGH,
+        precision=lax.Precision.HIGHEST,
         preferred_element_type=jnp.float32,
     )
     layer_out = (residual + experts_sum).astype(jnp.bfloat16)

time: 179 us -> 177 us (0.989)
    all_to_all x1, waiting for transfers between devices: 50.5 us -> 48.3 us  [direct_dispatch(): lax.all_to_all(unit_rows, 'tok', split_axis=0, concat_axis=0, tiled=True)]
    ppermute x1, waiting for transfers between devices: 0.01 us -> 2.28 us  [body(): sibling_gate_up = lax.ppermute(expert_gate_up, 'tok', sibling)]
    dot_general x2 -> x1, matrix products: 5.99 us -> 4.23 us  [pair_ffn(): gate_up_all = jnp.dot(rows_in, joined, preferred_element_type=jnp.float32)]
  transfers between devices with their start and end apart: 10 -> 10, of which waited for: 3 -> 4; matrix products, arithmetic and copies ran while one was open for 9% -> 8% of each run, Pallas kernels for 9% -> 9%
where the time goes in v12:
time: 177 us
  waiting for transfers between devices  105 us (59%)
  starting transfers between devices  27.2 us (15%)
  Pallas kernels  15.7 us (9%)
  matrix products  15.7 us (9%)
  other arithmetic  6.68 us (4%)
  local copies, waits for them, and re-layouts  5.47 us (3%)
    all_to_all x1, waiting for transfers between devices, direct_dispatch(): lax.all_to_all(produced.reshape(EXPERTS * split, CAP // split, width), 't...  50.3 us
    all_to_all x1, waiting for transfers between devices, direct_dispatch(): lax.all_to_all(unit_rows, 'tok', split_axis=0, concat_axis=0, tiled=True)  48.3 us
    pallas_call x4, Pallas kernels, attend_partial(): pl.pallas_call(_attend_kernel, out_shape=jax.ShapeDtypeStruct((rows, QUER...  15.7 us
    all_to_all x1, starting transfers between devices, direct_dispatch(): lax.all_to_all(unit_rows, 'tok', split_axis=0, concat_axis=0, tiled=True)  12.4 us
    all_to_all x1, starting transfers between devices, direct_dispatch(): lax.all_to_all(produced.reshape(EXPERTS * split, CAP // split, width), 't...  5.76 us
    ppermute x3, starting transfers between devices, body(): lax.ppermute(queries, 'pool', [(i, (i + shift) % pool_size) for i in rang...  5.73 us
    dot_general x1, matrix products, pair_ffn(): gate_up_all = jnp.dot(rows_in, joined, preferred_element_type=jnp.float32)  4.23 us
    ppermute x3, waiting for transfers between devices, body(): lax.ppermute(partial, 'pool', [(i, (i - shift) % pool_size) for i in rang...  4 us
  transfers between devices with their start and end apart: 10, of which 4 were waited for; matrix products, arithmetic and copies ran while one was open for 8% of the time, Pallas kernels for 9%

profile of v12, /device:TPU:8, one launch (start us, length us, event | category | flops | bytes accessed | tf_op | source)
XLA Modules:
  0.0 176.5 jit_solution(13376817546874593018)
XLA Ops:
  0.6 1.6 collective-permute-start
  2.2 2.7 %collective-permute-start.2 = (bf16[64,1024]{1,0:T(8,128)(2,1)}, bf16[64,1024]{1,0:T(8,128)(2,1)S(1)}, u32[]{:S(2)}, u32[]{:S(2)}) collective-permute-start(bf16[64,1024]{1,0:T(8,128)(2,1)} %q_ref.1), channel_id=1, source_target_pairs={{0,2},{1,3},{2,0},{3,1},{4,6},{5,7},{6,4},{7,5},{8,10},{9,11},{10,... | collective-permute-start | bytes 393224 | tf_op jit(solution)/shard_map/ppermute | solution.py:233
  4.9 1.4 collective-permute-start.4
  6.4 0.8 select_reduce_fusion.1
  7.2 0.8 copy.29
  8.4 1.2 reduce-window.6
  9.9 0.7 dynamic-slice_bitcast_fusion
  12.0 1.4 fusion.43
  13.3 0.7 copy-done.6
  14.0 3.9 %shard_map.144 = f32[64,1152]{1,0:T(8,128)} custom-call(s32[1]{0:T(128)} %bitcast.9.source_ref, bf16[64,1024]{1,0:T(8,128)(2,1)} %copy-done.6, bf16[512,1024]{1,0:T(8,128)(2,1)} %bitcast.103, bf16[64,1024]{1,0:T(8,128)(2,1)} %fresh_ref.7, s32[1,256]{1,0:T(1,128)} %bitcast.122, s32[1,256]{1,0:T(1,128)} %query_seg_ref.7, s32[1,576]{1,0:T(1,128)} %reshape.204.key_pos_ref, ...), custom_call_target="tpu_custom_call" | custom-call | tf_op jit(solution)/shard_map/pallas_call | solution.py:106
  17.9 0.6 copy-done.5
  18.6 3.9 %shard_map.145 = f32[64,1152]{1,0:T(8,128)} custom-call(s32[1]{0:T(128)} %bitcast.11.source_ref, bf16[64,1024]{1,0:T(8,128)(2,1)} %copy-done.5, bf16[512,1024]{1,0:T(8,128)(2,1)} %bitcast.104, bf16[64,1024]{1,0:T(8,128)(2,1)} %fresh_ref.7, s32[1,256]{1,0:T(1,128)} %bitcast.123, s32[1,256]{1,0:T(1,128)} %query_seg_ref.7, s32[1,576]{1,0:T(1,128)} %reshape.204.key_pos_ref, ...), custom_call_target="tpu_custom_call" | custom-call | tf_op jit(solution)/shard_map/pallas_call | solution.py:106
  22.5 2.6 %collective-permute-start.3 = (f32[64,1152]{1,0:T(8,128)}, f32[64,1152]{1,0:T(8,128)S(1)}, u32[]{:S(2)}, u32[]{:S(2)}) collective-permute-start(f32[64,1152]{1,0:T(8,128)} %shard_map.145), channel_id=1, source_target_pairs={{0,2},{1,3},{2,0},{3,1},{4,6},{5,7},{6,4},{7,5},{8,10},{9,11},{10,... | collective-permute-start | bytes 884744 | tf_op jit(solution)/shard_map/ppermute | solution.py:242
  25.2 0.7 copy-done.4
  25.8 3.9 %shard_map.146 = f32[64,1152]{1,0:T(8,128)} custom-call(s32[1]{0:T(128)} %bitcast.13.source_ref, bf16[64,1024]{1,0:T(8,128)(2,1)} %copy-done.4, bf16[512,1024]{1,0:T(8,128)(2,1)} %bitcast.105, bf16[64,1024]{1,0:T(8,128)(2,1)} %fresh_ref.7, s32[1,256]{1,0:T(1,128)} %bitcast.124, s32[1,256]{1,0:T(1,128)} %query_seg_ref.7, s32[1,576]{1,0:T(1,128)} %reshape.204.key_pos_ref, ...), custom_call_target="tpu_custom_call" | custom-call | tf_op jit(solution)/shard_map/pallas_call | solution.py:106
  29.8 3.9 %shard_map.143 = f32[64,1152]{1,0:T(8,128)} custom-call(s32[1]{0:T(128)} %bitcast.source_ref, bf16[64,1024]{1,0:T(8,128)(2,1)} %q_ref.1, bf16[512,1024]{1,0:T(8,128)(2,1)} %bitcast.106, bf16[64,1024]{1,0:T(8,128)(2,1)} %fresh_ref.7, s32[1,256]{1,0:T(1,128)} %bitcast.125, s32[1,256]{1,0:T(1,128)} %query_seg_ref.7, s32[1,576]{1,0:T(1,128)} %reshape.204.key_pos_ref, ...), custom_call_target="tpu_custom_call" | custom-call | tf_op jit(solution)/shard_map/pallas_call | solution.py:106
  33.8 0.7 fusion.4
  34.5 4.0 %collective-permute-done.5 = f32[64,1152]{1,0:T(8,128)S(1)} collective-permute-done((f32[64,1152]{1,0:T(8,128)}, f32[64,1152]{1,0:T(8,128)S(1)}, u32[]{:S(2)}, u32[]{:S(2)}) %collective-permute-start.5) | collective-permute-done | bytes 294944 | tf_op jit(solution)/shard_map/ppermute | solution.py:242
  38.5 0.8 fusion.47
  39.3 0.9 subtract_exponential_fusion
  41.6 0.6 multiply_reduce_fusion
  42.2 2.1 %convolution_convert_fusion = bf16[1024,1024]{1,0:T(8,128)(2,1)} fusion(pred[1024,64]{0,1:T(8,128)(4,1)S(1)} %fusion.4, f32[64,1024]{1,0:T(8,128)S(1)} %get-tuple-element.7, f32[1024]{0:T(1024)S(1)} %copy-done.8, f32[64]{0:T(128)S(1)} %add_rsqrt_fusion), kind=kOutput, calls=%fused_computation.8 | convolution fusion | flops 135462912 | bytes 2429184 | tf_op jit(solution)/shard_map/dot_general | solution.py:281
  44.3 12.4 %all-to-all-start = ((bf16[64,16,1024]{2,1,0:T(8,128)(2,1)}), bf16[64,16,1024]{2,1,0:T(8,128)(2,1)}, u32[]{:S(2)}, u32[]{:S(2)}) async-start(bf16[64,16,1024]{2,1,0:T(8,128)(2,1)} %bitcast.107), calls=%async_computation | async-start | bytes 4194304 | tf_op jit(solution)/shard_map/all_to_all | solution.py:140
  57.3 2.3 %collective-permute-done.6 = bf16[1,1024,512]{2,1,0:T(8,128)(2,1)} collective-permute-done((bf16[1,1024,512]{2,1,0:T(8,128)(2,1)S(1)}, bf16[1,1024,512]{2,1,0:T(8,128)(2,1)}, u32[]{:S(2)}, u32[]{:S(2)}) %collective-permute-start.6) | collective-permute-done | bytes 1048608 | tf_op jit(solution)/shard_map/ppermute | solution.py:170
  59.6 48.3 %all-to-all-done = bf16[64,16,1024]{2,1,0:T(8,128)(2,1)} async-done(((bf16[64,16,1024]{2,1,0:T(8,128)(2,1)}), bf16[64,16,1024]{2,1,0:T(8,128)(2,1)}, u32[]{:S(2)}, u32[]{:S(2)}) %all-to-all-start) | async-done | bytes 2097184 | tf_op jit(solution)/shard_map/all_to_all | solution.py:140
  107.9 4.2 %fusion = f32[1024,1024]{1,0:T(8,128)S(1)} fusion(bf16[1024,1024]{1,0:T(8,128)(2,1)} %bitcast.24, bf16[1024,512]{1,0:T(8,128)(2,1)} %bitcast.26, bf16[1024,512]{1,0:T(8,128)(2,1)S(1)} %bitcast.128), kind=kOutput, calls=%fused_computation.1 | convolution fusion | flops 2151677952 | bytes 8388608 | tf_op jit(solution)/shard_map/dot_general | solution.py:122
  112.1 0.7 fusion.8
  112.9 3.2 %add_convert_fusion = bf16[1024,1024]{1,0:T(8,128)(2,1)} fusion(bf16[1024,1024]{1,0:T(8,128)(2,1)S(1)} %fusion.8, f32[1024,1024]{1,0:T(8,128)S(1)} %fusion, bf16[1,256,1024]{2,1,0:T(8,128)(2,1)} %collective-permute-done.7), kind=kOutput, calls=%fused_computation | convolution fusion | flops 543686656 | bytes 6815744 | tf_op jit(solution)/shard_map/dot_general | solution.py:129
  116.1 5.8 %all-to-all-start.1 = ((bf16[64,16,1024]{2,1,0:T(8,128)(2,1)}), bf16[64,16,1024]{2,1,0:T(8,128)(2,1)}, u32[]{:S(2)}, u32[]{:S(2)}) async-start(bf16[64,16,1024]{2,1,0:T(8,128)(2,1)} %bitcast.120), calls=%async_computation.1 | async-start | bytes 4194304 | tf_op jit(solution)/shard_map/all_to_all | solution.py:142
  122.0 0.7 select_reduce_fusion
  122.7 50.3 %all-to-all-done.1 = bf16[64,16,1024]{2,1,0:T(8,128)(2,1)} async-done(((bf16[64,16,1024]{2,1,0:T(8,128)(2,1)}), bf16[64,16,1024]{2,1,0:T(8,128)(2,1)}, u32[]{:S(2)}, u32[]{:S(2)}) %all-to-all-start.1) | async-done | bytes 2097184 | tf_op jit(solution)/shard_map/all_to_all | solution.py:142
  173.0 3.5 %fusion.5 = bf16[64,1024]{1,0:T(8,128)(2,1)} fusion(f32[64,1024]{1,0:T(8,128)S(1)} %get-tuple-element.7, f32[1024,64]{0,1:T(8,128)S(1)} %select_reduce_fusion, bf16[1024,1024]{1,0:T(8,128)(2,1)} %bitcast.30), kind=kOutput, calls=%fused_computation.12 | convolution fusion | flops 805437440 | bytes 2752512 | tf_op jit(solution)/shard_map/dot_general | solution.py:292
  (61 shorter events, 4.2 us)
Async XLA Ops:
  0.6 40.9 %copy-start = (bf16[1024,1024]{1,0:T(8,128)(2,1)S(1)}, bf16[1024,1024]{1,0:T(8,128)(2,1)}, u32[]{:S(2)}) copy-start(bf16[1024,1024]{1,0:T(8,128)(2,1)} %param.20) | copy-start | bytes 6291460
  0.6 12.7 %collective-permute-start = (bf16[64,1024]{1,0:T(8,128)(2,1)}, bf16[64,1024]{1,0:T(8,128)(2,1)S(1)}, u32[]{:S(2)}, u32[]{:S(2)}) collective-permute-start(bf16[64,1024]{1,0:T(8,128)(2,1)} %q_ref.1), channel_id=1, source_target_pairs={{0,1},{1,2},{2,3},{3,0},{4,5},{5,6},{6,7},{7,4},{8,9},{9,10},{10,1... | collective-permute-start | bytes 393224 | tf_op jit(solution)/shard_map/ppermute | solution.py:233
  2.2 15.7 %collective-permute-start.2 = (bf16[64,1024]{1,0:T(8,128)(2,1)}, bf16[64,1024]{1,0:T(8,128)(2,1)S(1)}, u32[]{:S(2)}, u32[]{:S(2)}) collective-permute-start(bf16[64,1024]{1,0:T(8,128)(2,1)} %q_ref.1), channel_id=1, source_target_pairs={{0,2},{1,3},{2,0},{3,1},{4,6},{5,7},{6,4},{7,5},{8,10},{9,11},{10,... | collective-permute-start | bytes 393224 | tf_op jit(solution)/shard_map/ppermute | solution.py:233
  4.9 20.2 %collective-permute-start.4 = (bf16[64,1024]{1,0:T(8,128)(2,1)}, bf16[64,1024]{1,0:T(8,128)(2,1)S(1)}, u32[]{:S(2)}, u32[]{:S(2)}) collective-permute-start(bf16[64,1024]{1,0:T(8,128)(2,1)} %q_ref.1), channel_id=1, source_target_pairs={{0,3},{1,0},{2,1},{3,2},{4,7},{5,4},{6,5},{7,6},{8,11},{9,8},{10,9... | collective-permute-start | bytes 393224 | tf_op jit(solution)/shard_map/ppermute | solution.py:233
  13.3 0.7 copy-start.6
  14.0 15.8 %copy-start.7 = (s32[64,8]{0,1:T(8,128)S(1)}, s32[64,8]{0,1:T(8,128)}, u32[]{:S(2)}) copy-start(s32[64,8]{0,1:T(8,128)} %param.24) | copy-start | bytes 6148
  17.9 16.6 %collective-permute-start.1 = (f32[64,1152]{1,0:T(8,128)}, f32[64,1152]{1,0:T(8,128)S(1)}, u32[]{:S(2)}, u32[]{:S(2)}) collective-permute-start(f32[64,1152]{1,0:T(8,128)} %shard_map.144), channel_id=1, source_target_pairs={{0,3},{1,0},{2,1},{3,2},{4,7},{5,4},{6,5},{7,6},{8,11},{9,8},{10,9... | collective-permute-start | bytes 884744 | tf_op jit(solution)/shard_map/ppermute | solution.py:242
  17.9 0.7 copy-start.5
  22.5 12.0 %collective-permute-start.3 = (f32[64,1152]{1,0:T(8,128)}, f32[64,1152]{1,0:T(8,128)S(1)}, u32[]{:S(2)}, u32[]{:S(2)}) collective-permute-start(f32[64,1152]{1,0:T(8,128)} %shard_map.145), channel_id=1, source_target_pairs={{0,2},{1,3},{2,0},{3,1},{4,6},{5,7},{6,4},{7,5},{8,10},{9,11},{10,... | collective-permute-start | bytes 884744 | tf_op jit(solution)/shard_map/ppermute | solution.py:242
  25.2 0.7 copy-start.4
  29.8 8.8 %collective-permute-start.5 = (f32[64,1152]{1,0:T(8,128)}, f32[64,1152]{1,0:T(8,128)S(1)}, u32[]{:S(2)}, u32[]{:S(2)}) collective-permute-start(f32[64,1152]{1,0:T(8,128)} %shard_map.146), channel_id=1, source_target_pairs={{0,1},{1,2},{2,3},{3,0},{4,5},{5,6},{6,7},{7,4},{8,9},{9,10},{10,1... | collective-permute-start | bytes 884744 | tf_op jit(solution)/shard_map/ppermute | solution.py:242
  33.7 7.5 %copy-start.1 = (f32[64,1152]{1,0:T(8,128)S(1)}, f32[64,1152]{1,0:T(8,128)}, u32[]{:S(2)}) copy-start(f32[64,1152]{1,0:T(8,128)} %shard_map.143) | copy-start | bytes 884740
  40.2 1.4 copy-start.3
  41.2 1.0 copy-start.8
  41.6 2.7 %copy-start.2 = (bf16[64,1024]{1,0:T(8,128)(2,1)}, bf16[64,1024]{1,0:T(8,128)(2,1)S(1)}, u32[]{:S(2)}) copy-start(bf16[64,1024]{1,0:T(8,128)(2,1)S(1)} %fusion.22) | copy-start | bytes 393220
  44.3 12.4 %copy-start.10 = (bf16[1,1024,512]{2,1,0:T(8,128)(2,1)S(1)}, bf16[1,1024,512]{2,1,0:T(8,128)(2,1)}, u32[]{:S(2)}) copy-start(bf16[1,1024,512]{2,1,0:T(8,128)(2,1)} %param.22) | copy-start | bytes 3145732
  44.3 63.6 %all-to-all-start = ((bf16[64,16,1024]{2,1,0:T(8,128)(2,1)}), bf16[64,16,1024]{2,1,0:T(8,128)(2,1)}, u32[]{:S(2)}, u32[]{:S(2)}) async-start(bf16[64,16,1024]{2,1,0:T(8,128)(2,1)} %bitcast.107), calls=%async_computation | async-start | bytes 4194304 | tf_op jit(solution)/shard_map/all_to_all | solution.py:140
  56.7 2.9 %collective-permute-start.6 = (bf16[1,1024,512]{2,1,0:T(8,128)(2,1)S(1)}, bf16[1,1024,512]{2,1,0:T(8,128)(2,1)}, u32[]{:S(2)}, u32[]{:S(2)}) collective-permute-start(bf16[1,1024,512]{2,1,0:T(8,128)(2,1)S(1)} %copy-done.10), channel_id=1, source_target_pairs={{0,4},{4,0},{8,12},{12,8},{16,20},{20,16},{24,28},{28,24},{32,36},... | collective-permute-start | bytes 3145736 | tf_op jit(solution)/shard_map/ppermute | solution.py:170
  56.9 55.9 %collective-permute-start.7 = (bf16[1,256,1024]{2,1,0:T(8,128)(2,1)}, bf16[1,256,1024]{2,1,0:T(8,128)(2,1)}, u32[]{:S(2)}, u32[]{:S(2)}) collective-permute-start(bf16[1,256,1024]{2,1,0:T(8,128)(2,1)} %param.23), channel_id=1, source_target_pairs={{0,4},{4,0},{8,12},{12,8},{16,20},{20,16},{24,28},{28,24},{32,36},... | collective-permute-start | bytes 1572872 | tf_op jit(solution)/shard_map/ppermute | solution.py:171
  107.9 4.2 %copy-start.11 = (bf16[1,256,1024]{2,1,0:T(8,128)(2,1)S(1)}, bf16[1,256,1024]{2,1,0:T(8,128)(2,1)}, u32[]{:S(2)}) copy-start(bf16[1,256,1024]{2,1,0:T(8,128)(2,1)} %param.23) | copy-start | bytes 1572868
  116.1 5.8 %copy-start.9 = (f32[64,8]{0,1:T(8,128)S(1)}, f32[64,8]{0,1:T(8,128)}, u32[]{:S(2)}) copy-start(f32[64,8]{0,1:T(8,128)} %param.25) | copy-start | bytes 6148
  116.1 56.9 %all-to-all-start.1 = ((bf16[64,16,1024]{2,1,0:T(8,128)(2,1)}), bf16[64,16,1024]{2,1,0:T(8,128)(2,1)}, u32[]{:S(2)}, u32[]{:S(2)}) async-start(bf16[64,16,1024]{2,1,0:T(8,128)(2,1)} %bitcast.120), calls=%async_computation.1 | async-start | bytes 4194304 | tf_op jit(solution)/shard_map/all_to_all | solution.py:142

commit v13 on v11

--- a/solution.py
+++ b/solution.py
@@ -26,8 +26,7 @@
     fresh_ref,
     query_len_ref,
     query_seg_ref,
-    key_pos_ref,
-    key_seg_ref,
+    key_info_ref,
     out_ref,
 ):
     rows = q_ref.shape[0]
@@ -44,9 +43,9 @@
     query_len = column(query_len_ref)
     query_seg = column(query_seg_ref)
     query_order = first + lax.broadcasted_iota(jnp.int32, (rows, 1), 0)
-    key_pos = key_pos_ref[...]
+    key_pos = key_info_ref[0:1, :]
     shown = (key_pos < query_len) | (
-        (key_seg_ref[...] == query_seg) & (key_pos - FRESH_BASE <= query_order)
+        (key_info_ref[1:2, :] == query_seg) & (key_pos - FRESH_BASE <= query_order)
     )
     lane = lax.broadcasted_iota(jnp.int32, (rows, 128), 1)
     low_half = lane < HEAD_SIZE
@@ -99,10 +98,10 @@
     out_ref[:, QUERY_HEADS * HEAD_SIZE:QUERY_HEADS * HEAD_SIZE + 128] = stats
 
 
-def attend_partial(source, q_block, cached, fresh, query_len, query_seg, key_pos, key_seg):
+def attend_partial(source, q_block, cached, fresh, query_len, query_seg, key_info):
     rows = q_block.shape[0]
     whole = lambda shape: pl.BlockSpec(shape, lambda i, s: (0,) * len(shape))
-    operands = (q_block, cached, fresh, query_len, query_seg, key_pos, key_seg)
+    operands = (q_block, cached, fresh, query_len, query_seg, key_info)
     return pl.pallas_call(
         _attend_kernel,
         out_shape=jax.ShapeDtypeStruct((rows, QUERY_HEADS * HEAD_SIZE + 128), jnp.float32),
@@ -200,12 +199,14 @@
     cached_rows = cache_block_pool.reshape(pool_blocks * block_len, 2 * kv_width)
 
     unlisted = jnp.int32(1 << 30)
-    key_pos = jnp.concatenate(
-        [jnp.where(cache_listed, cache_pos, unlisted), FRESH_BASE + fresh_order]
-    ).reshape(1, -1)
-    key_seg = jnp.concatenate(
-        [jnp.full((pool_blocks * block_len,), -1, jnp.int32), fresh_seg]
-    ).reshape(1, -1)
+    key_info = jnp.stack(
+        [
+            jnp.concatenate(
+                [jnp.where(cache_listed, cache_pos, unlisted), FRESH_BASE + fresh_order]
+            ),
+            jnp.concatenate([jnp.full((pool_blocks * block_len,), -1, jnp.int32), fresh_seg]),
+        ]
+    )
     query_len_all = jnp.sum(
         jnp.where(
             request_ids[:, :, None] == request_range[None, None, :], lengths[None, None, :], 0
@@ -222,8 +223,7 @@
             fresh_kv,
             query_len_all,
             query_seg_all,
-            key_pos,
-            key_seg,
+            key_info,
         )
 
     query_blocks = [queries] + [
@@ -289,7 +289,7 @@
     experts_sum = jnp.dot(
         mixing,
         expert_rows.astype(jnp.float32),
-        precision=lax.Precision.HIGH,
+        precision=lax.Precision.HIGHEST,
         preferred_element_type=jnp.float32,
     )
     layer_out = (residual + experts_sum).astype(jnp.bfloat16)

time: 179 us -> 178 us (level)
  transfers between devices with their start and end apart: 10 -> 10, of which waited for: 3 -> 3; matrix products, arithmetic and copies ran while one was open for 9% -> 8% of each run, Pallas kernels for 9% -> 9%
where the time goes in v13:
time: 178 us
  waiting for transfers between devices  104 us (58%)
  starting transfers between devices  27.6 us (16%)
  matrix products  17.4 us (10%)
  Pallas kernels  15.7 us (9%)
  other arithmetic  7.3 us (4%)
  local copies, waits for them, and re-layouts  4.34 us (2%)
    all_to_all x1, waiting for transfers between devices, direct_dispatch(): lax.all_to_all(unit_rows, 'tok', split_axis=0, concat_axis=0, tiled=True)  50.5 us
    all_to_all x1, waiting for transfers between devices, direct_dispatch(): lax.all_to_all(produced.reshape(EXPERTS * split, CAP // split, width), 't...  50.3 us
    pallas_call x4, Pallas kernels, attend_partial(): pl.pallas_call(_attend_kernel, out_shape=jax.ShapeDtypeStruct((rows, QUER...  15.7 us
    all_to_all x1, starting transfers between devices, direct_dispatch(): lax.all_to_all(unit_rows, 'tok', split_axis=0, concat_axis=0, tiled=True)  12.4 us
    dot_general x2, matrix products, pair_ffn(): jnp.dot(rows_in, gate_up_pair[part], preferred_element_type=jnp.float32)  5.99 us
    all_to_all x1, starting transfers between devices, direct_dispatch(): lax.all_to_all(produced.reshape(EXPERTS * split, CAP // split, width), 't...  5.77 us
    ppermute x3, starting transfers between devices, body(): lax.ppermute(queries, 'pool', [(i, (i + shift) % pool_size) for i in rang...  5.13 us
    dot_general x2, matrix products, pair_ffn(): jnp.dot(inner, down_pair[part], preferred_element_type=jnp.float32)  3.99 us
  transfers between devices with their start and end apart: 10, of which 3 were waited for; matrix products, arithmetic and copies ran while one was open for 8% of the time, Pallas kernels for 9%

profile of v13, /device:TPU:8, one launch (start us, length us, event | category | flops | bytes accessed | tf_op | source)
XLA Modules:
  0.0 177.6 jit_solution(17961858976180367112)
XLA Ops:
  0.6 1.6 collective-permute-start
  2.2 1.7 collective-permute-start.4
  4.0 1.8 %collective-permute-start.2 = (bf16[64,1024]{1,0:T(8,128)(2,1)}, bf16[64,1024]{1,0:T(8,128)(2,1)S(1)}, u32[]{:S(2)}, u32[]{:S(2)}) collective-permute-start(bf16[64,1024]{1,0:T(8,128)(2,1)} %q_ref.1), channel_id=1, source_target_pairs={{0,2},{1,3},{2,0},{3,1},{4,6},{5,7},{6,4},{7,5},{8,10},{9,11},{10,... | collective-permute-start | bytes 393224 | tf_op jit(solution)/shard_map/ppermute | solution.py:230
  5.8 0.8 select_reduce_fusion.1
  6.6 0.8 copy.29
  7.8 0.7 dynamic-slice_bitcast_fusion
  8.5 1.2 reduce-window.6
  10.8 1.4 fusion.43
  12.2 0.7 copy-done.6
  12.9 3.9 %shard_map.144 = f32[64,1152]{1,0:T(8,128)} custom-call(s32[1]{0:T(128)} %bitcast.9.source_ref, bf16[64,1024]{1,0:T(8,128)(2,1)} %copy-done.6, bf16[512,1024]{1,0:T(8,128)(2,1)} %bitcast.108, bf16[64,1024]{1,0:T(8,128)(2,1)} %fresh_ref.7, s32[1,256]{1,0:T(1,128)} %bitcast.127, s32[1,256]{1,0:T(1,128)} %query_seg_ref.7, s32[2,576]{1,0:T(2,128)} %pad_add_fusion.key_info_ref), custom_call_target="tpu_custom_call" | custom-call | tf_op jit(solution)/shard_map/pallas_call | solution.py:105
  16.8 1.1 collective-permute-start.1
  17.9 0.7 copy-done.5
  18.6 3.9 %shard_map.146 = f32[64,1152]{1,0:T(8,128)} custom-call(s32[1]{0:T(128)} %bitcast.13.source_ref, bf16[64,1024]{1,0:T(8,128)(2,1)} %copy-done.5, bf16[512,1024]{1,0:T(8,128)(2,1)} %bitcast.109, bf16[64,1024]{1,0:T(8,128)(2,1)} %fresh_ref.7, s32[1,256]{1,0:T(1,128)} %bitcast.128, s32[1,256]{1,0:T(1,128)} %query_seg_ref.7, s32[2,576]{1,0:T(2,128)} %pad_add_fusion.key_info_ref), custom_call_target="tpu_custom_call" | custom-call | tf_op jit(solution)/shard_map/pallas_call | solution.py:105
  22.5 0.9 collective-permute-start.5
  24.0 3.9 %shard_map.145 = f32[64,1152]{1,0:T(8,128)} custom-call(s32[1]{0:T(128)} %bitcast.11.source_ref, bf16[64,1024]{1,0:T(8,128)(2,1)} %copy-done.4, bf16[512,1024]{1,0:T(8,128)(2,1)} %bitcast.110, bf16[64,1024]{1,0:T(8,128)(2,1)} %fresh_ref.7, s32[1,256]{1,0:T(1,128)} %bitcast.129, s32[1,256]{1,0:T(1,128)} %query_seg_ref.7, s32[2,576]{1,0:T(2,128)} %pad_add_fusion.key_info_ref), custom_call_target="tpu_custom_call" | custom-call | tf_op jit(solution)/shard_map/pallas_call | solution.py:105
  28.0 1.7 collective-permute-start.3
  29.8 3.9 %shard_map.143 = f32[64,1152]{1,0:T(8,128)} custom-call(s32[1]{0:T(128)} %bitcast.source_ref, bf16[64,1024]{1,0:T(8,128)(2,1)} %q_ref.1, bf16[512,1024]{1,0:T(8,128)(2,1)} %bitcast.111, bf16[64,1024]{1,0:T(8,128)(2,1)} %fresh_ref.7, s32[1,256]{1,0:T(1,128)} %bitcast.130, s32[1,256]{1,0:T(1,128)} %query_seg_ref.7, s32[2,576]{1,0:T(2,128)} %pad_add_fusion.key_info_ref), custom_call_target="tpu_custom_call" | custom-call | tf_op jit(solution)/shard_map/pallas_call | solution.py:105
  33.7 0.7 fusion
  34.4 3.5 %collective-permute-done.5 = f32[64,1152]{1,0:T(8,128)S(1)} collective-permute-done((f32[64,1152]{1,0:T(8,128)}, f32[64,1152]{1,0:T(8,128)S(1)}, u32[]{:S(2)}, u32[]{:S(2)}) %collective-permute-start.5) | collective-permute-done | bytes 294944 | tf_op jit(solution)/shard_map/ppermute | solution.py:239
  37.9 0.8 fusion.46
  38.6 0.9 subtract_exponential_fusion
  41.5 2.1 %convolution_convert_fusion = bf16[1024,1024]{1,0:T(8,128)(2,1)} fusion(pred[1024,64]{0,1:T(8,128)(4,1)S(1)} %fusion, f32[64,1024]{1,0:T(8,128)S(1)} %get-tuple-element.7, f32[1024]{0:T(1024)S(1)} %copy-done.8, f32[64]{0:T(128)S(1)} %add_rsqrt_fusion), kind=kOutput, calls=%fused_computation.4 | convolution fusion | flops 135462912 | bytes 2429184 | tf_op jit(solution)/shard_map/dot_general | solution.py:278
  43.6 12.4 %all-to-all-start = ((bf16[64,16,1024]{2,1,0:T(8,128)(2,1)}), bf16[64,16,1024]{2,1,0:T(8,128)(2,1)}, u32[]{:S(2)}, u32[]{:S(2)}) async-start(bf16[64,16,1024]{2,1,0:T(8,128)(2,1)} %bitcast.112), calls=%async_computation | async-start | bytes 4194304 | tf_op jit(solution)/shard_map/all_to_all | solution.py:136
  56.6 50.5 %all-to-all-done = bf16[64,16,1024]{2,1,0:T(8,128)(2,1)} async-done(((bf16[64,16,1024]{2,1,0:T(8,128)(2,1)}), bf16[64,16,1024]{2,1,0:T(8,128)(2,1)}, u32[]{:S(2)}, u32[]{:S(2)}) %all-to-all-start) | async-done | bytes 2097184 | tf_op jit(solution)/shard_map/all_to_all | solution.py:136
  107.2 2.9 %fusion.6 = f32[1024,512]{1,0:T(8,128)S(1)} fusion(bf16[1024,1024]{1,0:T(8,128)(2,1)} %bitcast.24, bf16[1,1024,512]{2,1,0:T(8,128)(2,1)S(1)} %copy-done.10), kind=kOutput, calls=%fused_computation.15 | convolution fusion | flops 1073741824 | bytes 5242880 | tf_op jit(solution)/shard_map/dot_general | solution.py:121
  110.1 0.7 fusion.8
  110.8 3.1 %fusion.4 = f32[1024,512]{1,0:T(8,128)S(1)} fusion(bf16[1024,1024]{1,0:T(8,128)(2,1)} %bitcast.24, bf16[1,1024,512]{2,1,0:T(8,128)(2,1)} %collective-permute-done.6), kind=kOutput, calls=%fused_computation.13 | convolution fusion | flops 1073741824 | bytes 5242880 | tf_op jit(solution)/shard_map/dot_general | solution.py:121
  114.0 3.2 %add_convert_fusion = bf16[1024,1024]{1,0:T(8,128)(2,1)} fusion(bf16[1024,1024]{1,0:T(8,128)(2,1)S(1)} %fusion.8, f32[1024,512]{1,0:T(8,128)S(1)} %fusion.4, bf16[1,256,1024]{2,1,0:T(8,128)(2,1)} %collective-permute-done.7), kind=kOutput, calls=%fused_computation | convolution fusion | flops 543686656 | bytes 6815744 | tf_op jit(solution)/shard_map/dot_general | solution.py:125
  117.2 5.8 %all-to-all-start.1 = ((bf16[64,16,1024]{2,1,0:T(8,128)(2,1)}), bf16[64,16,1024]{2,1,0:T(8,128)(2,1)}, u32[]{:S(2)}, u32[]{:S(2)}) async-start(bf16[64,16,1024]{2,1,0:T(8,128)(2,1)} %bitcast.125), calls=%async_computation.1 | async-start | bytes 4194304 | tf_op jit(solution)/shard_map/all_to_all | solution.py:138
  123.1 0.7 select_reduce_fusion
  123.8 50.3 %all-to-all-done.1 = bf16[64,16,1024]{2,1,0:T(8,128)(2,1)} async-done(((bf16[64,16,1024]{2,1,0:T(8,128)(2,1)}), bf16[64,16,1024]{2,1,0:T(8,128)(2,1)}, u32[]{:S(2)}, u32[]{:S(2)}) %all-to-all-start.1) | async-done | bytes 2097184 | tf_op jit(solution)/shard_map/all_to_all | solution.py:138
  174.1 3.5 %fusion.1 = bf16[64,1024]{1,0:T(8,128)(2,1)} fusion(f32[64,1024]{1,0:T(8,128)S(1)} %get-tuple-element.7, f32[1024,64]{0,1:T(8,128)S(1)} %select_reduce_fusion, bf16[1024,1024]{1,0:T(8,128)(2,1)} %bitcast.30), kind=kOutput, calls=%fused_computation.8 | convolution fusion | flops 805437440 | bytes 2752512 | tf_op jit(solution)/shard_map/dot_general | solution.py:289
  (63 shorter events, 4.9 us)
Async XLA Ops:
  0.6 40.2 %copy-start = (bf16[1024,1024]{1,0:T(8,128)(2,1)S(1)}, bf16[1024,1024]{1,0:T(8,128)(2,1)}, u32[]{:S(2)}) copy-start(bf16[1024,1024]{1,0:T(8,128)(2,1)} %param.20) | copy-start | bytes 6291460
  0.6 11.6 %collective-permute-start = (bf16[64,1024]{1,0:T(8,128)(2,1)}, bf16[64,1024]{1,0:T(8,128)(2,1)S(1)}, u32[]{:S(2)}, u32[]{:S(2)}) collective-permute-start(bf16[64,1024]{1,0:T(8,128)(2,1)} %q_ref.1), channel_id=1, source_target_pairs={{0,1},{1,2},{2,3},{3,0},{4,5},{5,6},{6,7},{7,4},{8,9},{9,10},{10,1... | collective-permute-start | bytes 393224 | tf_op jit(solution)/shard_map/ppermute | solution.py:230
  2.2 15.7 %collective-permute-start.4 = (bf16[64,1024]{1,0:T(8,128)(2,1)}, bf16[64,1024]{1,0:T(8,128)(2,1)S(1)}, u32[]{:S(2)}, u32[]{:S(2)}) collective-permute-start(bf16[64,1024]{1,0:T(8,128)(2,1)} %q_ref.1), channel_id=1, source_target_pairs={{0,3},{1,0},{2,1},{3,2},{4,7},{5,4},{6,5},{7,6},{8,11},{9,8},{10,9... | collective-permute-start | bytes 393224 | tf_op jit(solution)/shard_map/ppermute | solution.py:230
  4.0 19.4 %collective-permute-start.2 = (bf16[64,1024]{1,0:T(8,128)(2,1)}, bf16[64,1024]{1,0:T(8,128)(2,1)S(1)}, u32[]{:S(2)}, u32[]{:S(2)}) collective-permute-start(bf16[64,1024]{1,0:T(8,128)(2,1)} %q_ref.1), channel_id=1, source_target_pairs={{0,2},{1,3},{2,0},{3,1},{4,6},{5,7},{6,4},{7,5},{8,10},{9,11},{10,... | collective-permute-start | bytes 393224 | tf_op jit(solution)/shard_map/ppermute | solution.py:230
  12.2 0.7 copy-start.6
  12.9 16.8 %copy-start.7 = (s32[64,8]{0,1:T(8,128)S(1)}, s32[64,8]{0,1:T(8,128)}, u32[]{:S(2)}) copy-start(s32[64,8]{0,1:T(8,128)} %param.24) | copy-start | bytes 6148
  16.8 17.6 %collective-permute-start.1 = (f32[64,1152]{1,0:T(8,128)}, f32[64,1152]{1,0:T(8,128)S(1)}, u32[]{:S(2)}, u32[]{:S(2)}) collective-permute-start(f32[64,1152]{1,0:T(8,128)} %shard_map.144), channel_id=1, source_target_pairs={{0,3},{1,0},{2,1},{3,2},{4,7},{5,4},{6,5},{7,6},{8,11},{9,8},{10,9... | collective-permute-start | bytes 884744 | tf_op jit(solution)/shard_map/ppermute | solution.py:239
  17.9 0.7 copy-start.5
  22.5 15.4 %collective-permute-start.5 = (f32[64,1152]{1,0:T(8,128)}, f32[64,1152]{1,0:T(8,128)S(1)}, u32[]{:S(2)}, u32[]{:S(2)}) collective-permute-start(f32[64,1152]{1,0:T(8,128)} %shard_map.146), channel_id=1, source_target_pairs={{0,1},{1,2},{2,3},{3,0},{4,5},{5,6},{6,7},{7,4},{8,9},{9,10},{10,1... | collective-permute-start | bytes 884744 | tf_op jit(solution)/shard_map/ppermute | solution.py:239
  23.4 0.7 copy-start.4
  28.0 9.9 %collective-permute-start.3 = (f32[64,1152]{1,0:T(8,128)}, f32[64,1152]{1,0:T(8,128)S(1)}, u32[]{:S(2)}, u32[]{:S(2)}) collective-permute-start(f32[64,1152]{1,0:T(8,128)} %shard_map.145), channel_id=1, source_target_pairs={{0,2},{1,3},{2,0},{3,1},{4,6},{5,7},{6,4},{7,5},{8,10},{9,11},{10,... | collective-permute-start | bytes 884744 | tf_op jit(solution)/shard_map/ppermute | solution.py:239
  33.7 6.9 %copy-start.1 = (f32[64,1152]{1,0:T(8,128)S(1)}, f32[64,1152]{1,0:T(8,128)}, u32[]{:S(2)}) copy-start(f32[64,1152]{1,0:T(8,128)} %shard_map.143) | copy-start | bytes 884740
  39.5 1.4 copy-start.3
  40.6 1.0 copy-start.8
  40.9 2.7 %copy-start.2 = (bf16[64,1024]{1,0:T(8,128)(2,1)}, bf16[64,1024]{1,0:T(8,128)(2,1)S(1)}, u32[]{:S(2)}) copy-start(bf16[64,1024]{1,0:T(8,128)(2,1)S(1)} %fusion.22) | copy-start | bytes 393220
  43.6 12.4 %copy-start.10 = (bf16[1,1024,512]{2,1,0:T(8,128)(2,1)S(1)}, bf16[1,1024,512]{2,1,0:T(8,128)(2,1)}, u32[]{:S(2)}) copy-start(bf16[1,1024,512]{2,1,0:T(8,128)(2,1)} %param.22) | copy-start | bytes 3145732
  43.6 63.6 %all-to-all-start = ((bf16[64,16,1024]{2,1,0:T(8,128)(2,1)}), bf16[64,16,1024]{2,1,0:T(8,128)(2,1)}, u32[]{:S(2)}, u32[]{:S(2)}) async-start(bf16[64,16,1024]{2,1,0:T(8,128)(2,1)} %bitcast.112), calls=%async_computation | async-start | bytes 4194304 | tf_op jit(solution)/shard_map/all_to_all | solution.py:136
  56.0 54.8 %collective-permute-start.6 = (bf16[1,1024,512]{2,1,0:T(8,128)(2,1)S(1)}, bf16[1,1024,512]{2,1,0:T(8,128)(2,1)}, u32[]{:S(2)}, u32[]{:S(2)}) collective-permute-start(bf16[1,1024,512]{2,1,0:T(8,128)(2,1)S(1)} %copy-done.10), channel_id=1, source_target_pairs={{0,4},{4,0},{8,12},{12,8},{16,20},{20,16},{24,28},{28,24},{32,36},... | collective-permute-start | bytes 3145736 | tf_op jit(solution)/shard_map/ppermute | solution.py:166
  56.2 57.7 %collective-permute-start.7 = (bf16[1,256,1024]{2,1,0:T(8,128)(2,1)}, bf16[1,256,1024]{2,1,0:T(8,128)(2,1)}, u32[]{:S(2)}, u32[]{:S(2)}) collective-permute-start(bf16[1,256,1024]{2,1,0:T(8,128)(2,1)} %param.23), channel_id=1, source_target_pairs={{0,4},{4,0},{8,12},{12,8},{16,20},{20,16},{24,28},{28,24},{32,36},... | collective-permute-start | bytes 1572872 | tf_op jit(solution)/shard_map/ppermute | solution.py:167
  107.2 2.9 %copy-start.11 = (bf16[1,256,1024]{2,1,0:T(8,128)(2,1)S(1)}, bf16[1,256,1024]{2,1,0:T(8,128)(2,1)}, u32[]{:S(2)}) copy-start(bf16[1,256,1024]{2,1,0:T(8,128)(2,1)} %param.23) | copy-start | bytes 1572868
  117.2 5.8 %copy-start.9 = (f32[64,8]{0,1:T(8,128)S(1)}, f32[64,8]{0,1:T(8,128)}, u32[]{:S(2)}) copy-start(f32[64,8]{0,1:T(8,128)} %param.25) | copy-start | bytes 6148
  117.2 56.9 %all-to-all-start.1 = ((bf16[64,16,1024]{2,1,0:T(8,128)(2,1)}), bf16[64,16,1024]{2,1,0:T(8,128)(2,1)}, u32[]{:S(2)}, u32[]{:S(2)}) async-start(bf16[64,16,1024]{2,1,0:T(8,128)(2,1)} %bitcast.125), calls=%async_computation.1 | async-start | bytes 4194304 | tf_op jit(solution)/shard_map/all_to_all | solution.py:138
